TPU v7x, 512 devices: a whole 4x8x8 slice. The times are simulated.
512 devices in a mesh: ctx: 32 (over x, y), head: 16 (over z, core).
Axes of the slice: x: 4, y: 8, z: 8, core: 2. Of those that a mesh axis runs over, the one named last changes fastest.
Arguments:
- q_soft: bfloat16 [16384, 4096], P(('ctx', 'head')), may hold values from -5 to 5
- k_soft: bfloat16 [16384, 4096], P(('ctx', 'head')), may hold values from -5 to 5
- v_soft: bfloat16 [16384, 4096], P(('ctx', 'head')), may hold values from -6 to 6
- q_light: bfloat16 [16384, 4096], P(('ctx', 'head')), may hold values from -6 to 6
- k_light: bfloat16 [16384, 4096], P(('ctx', 'head')), may hold values from -6 to 6
- v_light: bfloat16 [16384, 4096], P(('ctx', 'head')), may hold values from -100 to 100
- decay_log: float32 [32, 16384], P('head', 'ctx'), may hold values from -1 to 0
- norm_gain: float32 [4096], P('head'), may hold values from 0.5 to 1.5
- doc_lengths: int32 [32], replicated, may hold values from 1 to 4096, 16384 in all
Outputs:
- attn_soft: bfloat16 [16384, 4096], P(('ctx', 'head'))
- attn_light: bfloat16 [16384, 4096], P(('ctx', 'head'))
Inputs may be any that keep to these rules, and one draw needn't show every extreme that they name: `doc_lengths`: the lengths sum to 16384; the largest is exactly 4096.
All inputs are finite; a program needn't handle non-finite values.
Results may differ from a plain program's by a relative error of at most 0.013.
Values may be sent and summed in bfloat16 or wider, within the bound.
No kernel may reach another device: no remote copies, remote signals or barrier semaphores. Data moves between devices by JAX's collectives and lax.ppermute only.
A program may use at most 64 MiB of HBM per device.

v0:
```python
from functools import partial

import jax
import jax.numpy as jnp
from jax import lax
from jax.sharding import PartitionSpec as P

DOC_REACH = 8


def shifted(block, axis, distance):
    size = lax.axis_size(axis)
    route = [(i, (i + distance) % size) for i in range(size)]
    return lax.ppermute(block, axis, route)


def doc_index(positions, starts):
    return jnp.sum((positions[:, None] >= starts[None, :]).astype(jnp.int32), axis=1) - 1


def block_partial(
    kv_pair,
    source,
    queries,
    query_pos,
    query_doc,
    starts,
    row_count,
    heads_dev,
    head_width,
):
    key_block = kv_pair[0].reshape(row_count, heads_dev, head_width)
    val_block = kv_pair[1].reshape(row_count, heads_dev, head_width)
    key_pos = source * row_count + jnp.arange(row_count, dtype=jnp.int32)
    key_doc = doc_index(key_pos, starts)
    allowed = (query_doc[:, None] == key_doc[None, :]) & (key_pos[None, :] <= query_pos[:, None])
    scores = (
        jnp.einsum("thd,shd->hts", queries, key_block, preferred_element_type=jnp.float32)
        / head_width**0.5
    )
    scores = jnp.where(allowed[None], scores, -1e30)
    block_max = jnp.max(scores, axis=2)
    probs = jnp.where(allowed[None], jnp.exp(scores - block_max[:, :, None]), 0.0)
    block_total = jnp.sum(probs, axis=2)
    product = jnp.einsum(
        "hts,shd->thd", probs.astype(jnp.bfloat16), val_block, preferred_element_type=jnp.float32
    )
    return (block_max, block_total, product)


def empty_partial(row_count, heads_dev, head_width):
    return (
        jnp.full((heads_dev, row_count), -1e30, jnp.float32),
        jnp.zeros((heads_dev, row_count), jnp.float32),
        jnp.zeros((row_count, heads_dev, head_width), jnp.float32),
    )


def soft_attention(q_rows, kv_pair, doc_lengths, row_count, heads_dev, head_width):
    size = lax.axis_size("ctx")
    own_index = lax.axis_index("ctx")
    reach = min(DOC_REACH, size - 1)
    forward_steps = (reach + 1) // 2
    starts = jnp.cumsum(doc_lengths) - doc_lengths
    query_pos = own_index * row_count + jnp.arange(row_count, dtype=jnp.int32)
    query_doc = doc_index(query_pos, starts)
    queries = q_rows.reshape(row_count, heads_dev, head_width)
    absorb = partial(
        block_partial,
        queries=queries,
        query_pos=query_pos,
        query_doc=query_doc,
        starts=starts,
        row_count=row_count,
        heads_dev=heads_dev,
        head_width=head_width,
    )
    arrivals = []
    ahead = kv_pair
    for offset in range(1, forward_steps + 1):
        ahead = shifted(ahead, "ctx", 1)
        arrivals.append((ahead, offset))
    if reach > forward_steps:
        behind = shifted(kv_pair, "ctx", reach)
        arrivals.append((behind, reach))
        for offset in range(reach - 1, forward_steps, -1):
            behind = shifted(behind, "ctx", -1)
            arrivals.append((behind, offset))
    order = []
    fwd = [a for a in arrivals if a[1] <= forward_steps]
    bwd = [a for a in arrivals if a[1] > forward_steps]
    for i in range(max(len(fwd), len(bwd))):
        if i < len(fwd):
            order.append(fwd[i])
        if i < len(bwd):
            order.append(bwd[i])
    partials = [absorb(kv_pair, source=own_index)]
    skip = partial(empty_partial, row_count, heads_dev, head_width)
    for block, offset in order:
        source = own_index - offset
        last_doc = doc_index(jnp.full((1,), source * row_count + row_count - 1, jnp.int32), starts)[
            0
        ]
        needed = (source >= 0) & (last_doc == query_doc[0])
        partials.append(lax.cond(needed, partial(absorb, block, source=source), skip))
    row_max = partials[0][0]
    for part in partials[1:]:
        row_max = jnp.maximum(row_max, part[0])
    run_total = jnp.zeros_like(row_max)
    run_acc = jnp.zeros_like(partials[0][2])
    for part in partials:
        scale = jnp.exp(part[0] - row_max)
        run_total = run_total + part[1] * scale
        run_acc = run_acc + part[2] * scale.T[:, :, None]
    mixed = run_acc / run_total.T[:, :, None]
    return mixed.astype(jnp.bfloat16).reshape(row_count, heads_dev * head_width)


def lightning(q_rows, k_rows, v_rows, decay_log, norm_gain, row_count, heads_dev, head_width):
    size = lax.axis_size("ctx")
    own_index = lax.axis_index("ctx")
    cumul = jnp.cumsum(decay_log, axis=1)
    block_end = cumul[:, -1:]
    queries = q_rows.reshape(row_count, heads_dev, head_width)
    keys_here = k_rows.reshape(row_count, heads_dev, head_width)
    vals_here = v_rows.reshape(row_count, heads_dev, head_width)
    weighted = (keys_here * jnp.exp(block_end - cumul).T[:, :, None]).astype(jnp.bfloat16)
    update = jnp.einsum("thd,the->hde", weighted, vals_here, preferred_element_type=jnp.float32)
    end_hi = block_end.astype(jnp.bfloat16)
    end_lo = (block_end - end_hi.astype(jnp.float32)).astype(jnp.bfloat16)
    extra = jnp.zeros((heads_dev, 16, head_width), jnp.bfloat16)
    extra = extra.at[:, 0, :].set(jnp.broadcast_to(end_hi, (heads_dev, head_width)))
    extra = extra.at[:, 1, :].set(jnp.broadcast_to(end_lo, (heads_dev, head_width)))
    packed = jnp.concatenate([update.astype(jnp.bfloat16), extra], axis=1)
    gathered = lax.all_gather(packed, "ctx")
    ends = gathered[:, :, head_width, 0].astype(jnp.float32) + gathered[
        :, :, head_width + 1, 0
    ].astype(jnp.float32)
    blocks = jnp.arange(size, dtype=jnp.int32)
    between = (blocks[:, None] < blocks[None, :]) & (blocks[None, :] < own_index)
    exponent = jnp.einsum(
        "cb,bh->ch", between.astype(jnp.float32), ends, precision=lax.Precision.HIGHEST
    )
    weight = jnp.where((blocks < own_index)[:, None], jnp.exp(exponent), 0.0)
    entering = jnp.einsum(
        "ch,chde->hde",
        weight,
        gathered[:, :, :head_width, :].astype(jnp.float32),
        precision=lax.Precision.HIGHEST,
    )
    state_low = entering.astype(jnp.bfloat16)
    token_ids = jnp.arange(row_count, dtype=jnp.int32)
    causal = token_ids[None, :] <= token_ids[:, None]
    log_gap = jnp.where(causal[None], cumul[:, :, None] - cumul[:, None, :], -jnp.inf)
    raw_scores = jnp.einsum("thd,shd->hts", queries, keys_here, preferred_element_type=jnp.float32)
    gated = (raw_scores * jnp.exp(log_gap)).astype(jnp.bfloat16)
    inner = jnp.einsum("hts,shd->thd", gated, vals_here, preferred_element_type=jnp.float32)
    outer = (
        jnp.einsum("thd,hde->the", queries, state_low, preferred_element_type=jnp.float32)
        * jnp.exp(cumul).T[:, :, None]
    )
    raw_out = inner + outer
    mean_sq = jnp.mean(raw_out * raw_out, axis=2, keepdims=True)
    normed = raw_out * lax.rsqrt(mean_sq + 1e-06) * norm_gain.reshape(heads_dev, head_width)[None]
    return normed.astype(jnp.bfloat16).reshape(row_count, heads_dev * head_width)


def to_heads(arrays, parts):
    rows, width = arrays[0].shape
    chunk = width // parts
    send = jnp.stack([a.reshape(rows, parts, chunk) for a in arrays], axis=1)
    send = send.transpose(2, 1, 0, 3)
    got = lax.all_to_all(send, "head", split_axis=0, concat_axis=0, tiled=True)
    return got.transpose(1, 0, 2, 3).reshape(len(arrays), parts * rows, chunk)


def to_tokens(arrays, parts):
    rows, chunk = arrays[0].shape
    send = jnp.stack([a.reshape(parts, rows // parts, chunk) for a in arrays], axis=1)
    got = lax.all_to_all(send, "head", split_axis=0, concat_axis=0, tiled=True)
    return got.transpose(1, 2, 0, 3).reshape(len(arrays), rows // parts, parts * chunk)


def per_device(
    q_soft, k_soft, v_soft, q_light, k_light, v_light, decay_log, norm_gain, doc_lengths
):
    parts = lax.axis_size("head")
    kv_soft = to_heads([k_soft, v_soft], parts)
    kv_soft, q_soft = lax.optimization_barrier((kv_soft, q_soft))
    rest = to_heads([q_soft, q_light, k_light, v_light], parts)
    heads_dev = decay_log.shape[0]
    row_count = kv_soft.shape[1]
    head_width = kv_soft.shape[2] // heads_dev
    light_out = lightning(
        rest[1], rest[2], rest[3], decay_log, norm_gain, row_count, heads_dev, head_width
    )
    soft_out = soft_attention(rest[0], kv_soft, doc_lengths, row_count, heads_dev, head_width)
    returned = to_tokens([soft_out, light_out], parts)
    return (returned[0], returned[1])


def solution(mesh):
    in_specs = (
        P(("ctx", "head"), None),
        P(("ctx", "head"), None),
        P(("ctx", "head"), None),
        P(("ctx", "head"), None),
        P(("ctx", "head"), None),
        P(("ctx", "head"), None),
        P("head", "ctx"),
        P("head"),
        P(),
    )
    out_specs = (P(("ctx", "head"), None), P(("ctx", "head"), None))
    return jax.shard_map(
        per_device, mesh=mesh, in_specs=in_specs, out_specs=out_specs, check_vma=False
    )
```

profile of v0, /device:TPU:27, one launch (start us, length us, event | category | flops | bytes accessed | tf_op | source)
XLA Modules:
  0.0 246.1 jit_solution(15667668606870071201)
XLA Ops:
  10.3 11.1 %all-to-all-start = ((bf16[16,2,32,256]{3,2,1,0:T(8,128)(2,1)}), bf16[16,2,32,256]{3,2,1,0:T(8,128)(2,1)S(1)}, u32[]{:S(2)}, u32[]{:S(2)}) async-start(bf16[16,2,32,256]{3,2,1,0:T(8,128)(2,1)} %copy.414), calls=%async_computation | async-start | bytes 1048576 | tf_op jit(solution)/shard_map/all_to_all | solution.py:173
  21.6 17.1 %all-to-all-done = bf16[16,2,32,256]{3,2,1,0:T(8,128)(2,1)S(1)} async-done(((bf16[16,2,32,256]{3,2,1,0:T(8,128)(2,1)}), bf16[16,2,32,256]{3,2,1,0:T(8,128)(2,1)S(1)}, u32[]{:S(2)}, u32[]{:S(2)}) %all-to-all-start) | async-done | bytes 524320 | tf_op jit(solution)/shard_map/all_to_all | solution.py:173
  40.3 3.5 %all-to-all-start.1 = ((bf16[16,4,32,256]{3,2,1,0:T(8,128)(2,1)}), bf16[16,4,32,256]{3,2,1,0:T(8,128)(2,1)S(1)}, u32[]{:S(2)}, u32[]{:S(2)}) async-start(bf16[16,4,32,256]{3,2,1,0:T(8,128)(2,1)} %copy.418), calls=%async_computation.1 | async-start | bytes 2097152 | tf_op jit(solution)/shard_map/all_to_all | solution.py:173
  45.6 25.6 %all-to-all-done.1 = bf16[16,4,32,256]{3,2,1,0:T(8,128)(2,1)S(1)} async-done(((bf16[16,4,32,256]{3,2,1,0:T(8,128)(2,1)}), bf16[16,4,32,256]{3,2,1,0:T(8,128)(2,1)S(1)}, u32[]{:S(2)}, u32[]{:S(2)}) %all-to-all-start.1) | async-done | bytes 1048608 | tf_op jit(solution)/shard_map/all_to_all | solution.py:173
  73.1 4.4 %collective-permute-start = (bf16[2,512,256]{2,1,0:T(8,128)(2,1)S(1)}, bf16[2,512,256]{2,1,0:T(8,128)(2,1)S(1)}, u32[]{:S(2)}, u32[]{:S(2)}) collective-permute-start(bf16[2,512,256]{2,1,0:T(8,128)(2,1)S(1)} %bitcast.190), channel_id=1, source_target_pairs={{0,16},{16,32},{32,48},{48,64},{64,80},{80,96},{96,112},{112,128},... | collective-permute-start | bytes 1572872 | tf_op jit(solution)/shard_map/ppermute | solution.py:14
  77.5 3.1 %collective-permute-start.1 = (bf16[2,512,256]{2,1,0:T(8,128)(2,1)S(1)}, bf16[2,512,256]{2,1,0:T(8,128)(2,1)S(1)}, u32[]{:S(2)}, u32[]{:S(2)}) collective-permute-start(bf16[2,512,256]{2,1,0:T(8,128)(2,1)S(1)} %bitcast.191), channel_id=1, source_target_pairs={{0,128},{16,144},{32,160},{48,176},{64,192},{80,208},{96,224},{112... | collective-permute-start | bytes 1572872 | tf_op jit(solution)/shard_map/ppermute | solution.py:14
  81.7 7.2 %collective-permute-done = bf16[2,512,256]{2,1,0:T(8,128)(2,1)S(1)} collective-permute-done((bf16[2,512,256]{2,1,0:T(8,128)(2,1)S(1)}, bf16[2,512,256]{2,1,0:T(8,128)(2,1)S(1)}, u32[]{:S(2)}, u32[]{:S(2)}) %collective-permute-start) | collective-permute-done | bytes 524320 | tf_op jit(solution)/shard_map/ppermute | solution.py:14
  88.9 5.0 %collective-permute-start.2 = (bf16[2,512,256]{2,1,0:T(8,128)(2,1)S(1)}, bf16[2,512,256]{2,1,0:T(8,128)(2,1)}, u32[]{:S(2)}, u32[]{:S(2)}) collective-permute-start(bf16[2,512,256]{2,1,0:T(8,128)(2,1)S(1)} %collective-permute-done), channel_id=1, source_target_pairs={{0,16},{16,32},{32,48},{48,64},{64,80},{80,96},{96,112},{112,128},... | collective-permute-start | bytes 1572872 | tf_op jit(solution)/shard_map/ppermute | solution.py:14
  94.0 1.9 collective-permute-start.3
  96.8 10.1 %collective-permute-done.2 = bf16[2,512,256]{2,1,0:T(8,128)(2,1)} collective-permute-done((bf16[2,512,256]{2,1,0:T(8,128)(2,1)S(1)}, bf16[2,512,256]{2,1,0:T(8,128)(2,1)}, u32[]{:S(2)}, u32[]{:S(2)}) %collective-permute-start.2) | collective-permute-done | bytes 524320 | tf_op jit(solution)/shard_map/ppermute | solution.py:14
  106.9 5.4 %collective-permute-start.4 = (bf16[2,512,256]{2,1,0:T(8,128)(2,1)}, bf16[2,512,256]{2,1,0:T(8,128)(2,1)}, u32[]{:S(2)}, u32[]{:S(2)}) collective-permute-start(bf16[2,512,256]{2,1,0:T(8,128)(2,1)} %collective-permute-done.2), channel_id=1, source_target_pairs={{0,16},{16,32},{32,48},{48,64},{64,80},{80,96},{96,112},{112,128},... | collective-permute-start | bytes 1572872 | tf_op jit(solution)/shard_map/ppermute | solution.py:14
  112.3 1.9 collective-permute-start.5
  127.1 4.6 %collective-permute-start.6 = (bf16[2,512,256]{2,1,0:T(8,128)(2,1)}, bf16[2,512,256]{2,1,0:T(8,128)(2,1)}, u32[]{:S(2)}, u32[]{:S(2)}) collective-permute-start(bf16[2,512,256]{2,1,0:T(8,128)(2,1)} %collective-permute-done.4), channel_id=1, source_target_pairs={{0,16},{16,32},{32,48},{48,64},{64,80},{80,96},{96,112},{112,128},... | collective-permute-start | bytes 1572872 | tf_op jit(solution)/shard_map/ppermute | solution.py:14
  131.7 15.3 %collective-permute-start.7 = (bf16[2,512,256]{2,1,0:T(8,128)(2,1)}, bf16[2,512,256]{2,1,0:T(8,128)(2,1)}, u32[]{:S(2)}, u32[]{:S(2)}) collective-permute-start(bf16[2,512,256]{2,1,0:T(8,128)(2,1)} %collective-permute-done.5), channel_id=1, source_target_pairs={{0,496},{16,0},{32,16},{48,32},{64,48},{80,64},{96,80},{112,96},{1... | collective-permute-start | bytes 1572872 | tf_op jit(solution)/shard_map/ppermute | solution.py:14
  147.8 5.9 %conditional.8 = (f32[2,512]{1,0:T(2,128)}, f32[2,512]{1,0:T(2,128)S(1)}, f32[512,2,128]{0,2,1:T(8,128)S(1)}) conditional(s32[]{:T(128)} %convert_element_type.154, () %tuple.82, (s32[512]{0:T(512)S(1)}, s32[]{:T(128)}, s32[32]{0:T(128)S(1)}, s32[512]{0:T(512)S(1)}, bf16[2,512,256]{2,1,0:T(8,128)(2,1)}, ...), branch_computations={%region_4.5_spmd, %region_5.9_spmd} | conditional | flops 276085248 | bytes 11831464 | solution.py:105
  152.0 1.5 convolution_bitcast_fusion
  153.7 5.9 %conditional.10 = (f32[2,512]{1,0:T(2,128)}, f32[2,512]{1,0:T(2,128)S(1)}, f32[512,2,128]{0,2,1:T(8,128)S(1)}) conditional(s32[]{:T(128)} %convert_element_type.158, () %tuple.86, (s32[512]{0:T(512)S(1)}, s32[]{:T(128)}, s32[32]{0:T(128)S(1)}, s32[512]{0:T(512)S(1)}, bf16[2,512,256]{2,1,0:T(8,128)(2,1)}, ...), branch_computations={%region_16.17_spmd, %region_17.21_spmd} | conditional | flops 276085248 | bytes 11831464 | solution.py:105
  160.5 5.9 %conditional.12 = (f32[2,512]{1,0:T(2,128)}, f32[2,512]{1,0:T(2,128)S(1)}, f32[512,2,128]{0,2,1:T(8,128)S(1)}) conditional(s32[]{:T(128)} %convert_element_type.162, () %tuple.90, (s32[512]{0:T(512)S(1)}, s32[]{:T(128)}, s32[32]{0:T(128)S(1)}, s32[512]{0:T(512)S(1)}, bf16[2,512,256]{2,1,0:T(8,128)(2,1)}, ...), branch_computations={%region_28.29_spmd, %region_29.33_spmd} | conditional | flops 276085248 | bytes 11831464 | solution.py:105
  164.6 1.5 convolution_bitcast_fusion.4
  170.1 6.1 %conditional.13 = (f32[2,512]{1,0:T(2,128)}, f32[2,512]{1,0:T(2,128)S(1)}, f32[512,2,128]{0,2,1:T(8,128)S(1)}) conditional(s32[]{:T(128)} %convert_element_type.164, () %tuple.92, (s32[512]{0:T(512)S(1)}, s32[]{:T(128)}, s32[32]{0:T(128)S(1)}, s32[512]{0:T(512)S(1)}, bf16[2,512,256]{2,1,0:T(8,128)(2,1)}, ...), branch_computations={%region_34.35_spmd, %region_35.39_spmd} | conditional | flops 276085248 | bytes 11831464 | solution.py:105
  174.3 1.5 convolution_bitcast_fusion.5
  177.1 1.6 fusion.106
  179.2 10.2 %conditional.14 = (f32[2,512]{1,0:T(2,128)}, f32[2,512]{1,0:T(2,128)S(1)}, f32[512,2,128]{0,2,1:T(8,128)S(1)}) conditional(s32[]{:T(128)} %convert_element_type.166, () %tuple.94, (s32[512]{0:T(512)S(1)}, s32[]{:T(128)}, s32[32]{0:T(128)S(1)}, s32[512]{0:T(512)S(1)}, bf16[2,512,256]{2,1,0:T(8,128)(2,1)}, ...), branch_computations={%region_40.41_spmd, %region_41.45_spmd} | conditional | flops 276085248 | bytes 13928672 | solution.py:105
  182.3 2.3 fusion.78
  185.8 2.4 convolution_bitcast_fusion.6
  190.2 8.5 %conditional.15 = (f32[2,512]{1,0:T(2,128)}, f32[2,512]{1,0:T(2,128)S(1)}, f32[512,2,128]{0,2,1:T(8,128)}) conditional(s32[]{:T(128)} %convert_element_type.168, () %tuple.96, (s32[512]{0:T(512)S(1)}, s32[]{:T(128)}, s32[32]{0:T(128)S(1)}, s32[512]{0:T(512)S(1)}, bf16[2,512,256]{2,1,0:T(8,128)(2,1)}, ...), branch_computations={%region_46.47_spmd, %region_47.51_spmd} | conditional | flops 276085248 | bytes 12880068 | solution.py:105
  192.6 2.3 fusion.91
  200.3 2.0 fusion.112
  202.3 1.7 divide_convert_fusion
  205.4 1.7 slice.184
  207.5 1.8 fusion.104
  211.4 26.4 %all_to_all.15 = bf16[16,2,32,256]{3,2,1,0:T(8,128)(2,1)S(1)} all-to-all(bf16[16,2,32,256]{3,2,1,0:T(8,128)(2,1)S(1)} %copy.459), channel_id=1, replica_groups=mesh['ctx'=32,'head'=16] {'head'}, dimensions={0} | all-to-all | bytes 1048576 | tf_op jit(solution)/shard_map/all_to_all | solution.py:180
  (204 shorter events, 58.8 us)
Async XLA Ops:
  7.2 14.3 %copy-start.20 = (bf16[32,4096]{1,0:T(8,128)(2,1)S(1)}, bf16[32,4096]{1,0:T(8,128)(2,1)}, u32[]{:S(2)}) copy-start(bf16[32,4096]{1,0:T(8,128)(2,1)} %param.32) | copy-start | bytes 786436
  8.2 13.3 %copy-start.21 = (bf16[32,4096]{1,0:T(8,128)(2,1)S(1)}, bf16[32,4096]{1,0:T(8,128)(2,1)}, u32[]{:S(2)}) copy-start(bf16[32,4096]{1,0:T(8,128)(2,1)} %param.33) | copy-start | bytes 786436
  9.3 12.3 %copy-start.22 = (bf16[32,4096]{1,0:T(8,128)(2,1)S(1)}, bf16[32,4096]{1,0:T(8,128)(2,1)}, u32[]{:S(2)}) copy-start(bf16[32,4096]{1,0:T(8,128)(2,1)} %param.34) | copy-start | bytes 786436
  10.3 28.5 %copy-start.23 = (bf16[32,4096]{1,0:T(8,128)(2,1)S(1)}, bf16[32,4096]{1,0:T(8,128)(2,1)}, u32[]{:S(2)}) copy-start(bf16[32,4096]{1,0:T(8,128)(2,1)} %param.29) | copy-start | bytes 786436
  10.3 28.5 %all-to-all-start = ((bf16[16,2,32,256]{3,2,1,0:T(8,128)(2,1)}), bf16[16,2,32,256]{3,2,1,0:T(8,128)(2,1)S(1)}, u32[]{:S(2)}, u32[]{:S(2)}) async-start(bf16[16,2,32,256]{3,2,1,0:T(8,128)(2,1)} %copy.414), calls=%async_computation | async-start | bytes 1048576 | tf_op jit(solution)/shard_map/all_to_all | solution.py:173
  39.0 5.0 %copy-start.29 = (f32[2,512]{1,0:T(2,128)S(1)}, f32[2,512]{1,0:T(2,128)}, u32[]{:S(2)}) copy-start(f32[2,512]{1,0:T(2,128)} %param.35) | copy-start | bytes 12292
  40.3 30.8 %all-to-all-start.1 = ((bf16[16,4,32,256]{3,2,1,0:T(8,128)(2,1)}), bf16[16,4,32,256]{3,2,1,0:T(8,128)(2,1)S(1)}, u32[]{:S(2)}, u32[]{:S(2)}) async-start(bf16[16,4,32,256]{3,2,1,0:T(8,128)(2,1)} %copy.418), calls=%async_computation.1 | async-start | bytes 2097152 | tf_op jit(solution)/shard_map/all_to_all | solution.py:173
  43.9 160.5 %all-gather.3.cloned.1.call-start = ((), (), s32[]{:S(2)}) async-start(), calls=%async_computation.3 | async-start | bytes 2433024 | tf_op jit(solution)/shard_map/all_gather | solution.py:135
  71.2 9.5 %copy-start.30 = (s32[32]{0:T(128)S(1)}, s32[32]{0:T(128)}, u32[]{:S(2)}) copy-start(s32[32]{0:T(128)} %param.37) | copy-start | bytes 388
  73.1 15.8 %collective-permute-start = (bf16[2,512,256]{2,1,0:T(8,128)(2,1)S(1)}, bf16[2,512,256]{2,1,0:T(8,128)(2,1)S(1)}, u32[]{:S(2)}, u32[]{:S(2)}) collective-permute-start(bf16[2,512,256]{2,1,0:T(8,128)(2,1)S(1)} %bitcast.190), channel_id=1, source_target_pairs={{0,16},{16,32},{32,48},{48,64},{64,80},{80,96},{96,112},{112,128},... | collective-permute-start | bytes 1572872 | tf_op jit(solution)/shard_map/ppermute | solution.py:14
  77.5 16.4 %collective-permute-start.1 = (bf16[2,512,256]{2,1,0:T(8,128)(2,1)S(1)}, bf16[2,512,256]{2,1,0:T(8,128)(2,1)S(1)}, u32[]{:S(2)}, u32[]{:S(2)}) collective-permute-start(bf16[2,512,256]{2,1,0:T(8,128)(2,1)S(1)} %bitcast.191), channel_id=1, source_target_pairs={{0,128},{16,144},{32,160},{48,176},{64,192},{80,208},{96,224},{112... | collective-permute-start | bytes 1572872 | tf_op jit(solution)/shard_map/ppermute | solution.py:14
  88.9 36.1 %copy-start.19 = (bf16[2,512,256]{2,1,0:T(8,128)(2,1)}, bf16[2,512,256]{2,1,0:T(8,128)(2,1)S(1)}, u32[]{:S(2)}) copy-start(bf16[2,512,256]{2,1,0:T(8,128)(2,1)S(1)} %collective-permute-done) | copy-start | bytes 1572868
  88.9 18.0 %collective-permute-start.2 = (bf16[2,512,256]{2,1,0:T(8,128)(2,1)S(1)}, bf16[2,512,256]{2,1,0:T(8,128)(2,1)}, u32[]{:S(2)}, u32[]{:S(2)}) collective-permute-start(bf16[2,512,256]{2,1,0:T(8,128)(2,1)S(1)} %collective-permute-done), channel_id=1, source_target_pairs={{0,16},{16,32},{32,48},{48,64},{64,80},{80,96},{96,112},{112,128},... | collective-permute-start | bytes 1572872 | tf_op jit(solution)/shard_map/ppermute | solution.py:14
  93.9 31.1 %copy-start.16 = (bf16[2,512,256]{2,1,0:T(8,128)(2,1)}, bf16[2,512,256]{2,1,0:T(8,128)(2,1)S(1)}, u32[]{:S(2)}) copy-start(bf16[2,512,256]{2,1,0:T(8,128)(2,1)S(1)} %collective-permute-done.1) | copy-start | bytes 1572868
  94.0 18.4 %collective-permute-start.3 = (bf16[2,512,256]{2,1,0:T(8,128)(2,1)S(1)}, bf16[2,512,256]{2,1,0:T(8,128)(2,1)S(1)}, u32[]{:S(2)}, u32[]{:S(2)}) collective-permute-start(bf16[2,512,256]{2,1,0:T(8,128)(2,1)S(1)} %collective-permute-done.1), channel_id=1, source_target_pairs={{0,496},{16,0},{32,16},{48,32},{64,48},{80,64},{96,80},{112,96},{1... | collective-permute-start | bytes 1572872 | tf_op jit(solution)/shard_map/ppermute | solution.py:14
  106.9 20.2 %collective-permute-start.4 = (bf16[2,512,256]{2,1,0:T(8,128)(2,1)}, bf16[2,512,256]{2,1,0:T(8,128)(2,1)}, u32[]{:S(2)}, u32[]{:S(2)}) collective-permute-start(bf16[2,512,256]{2,1,0:T(8,128)(2,1)} %collective-permute-done.2), channel_id=1, source_target_pairs={{0,16},{16,32},{32,48},{48,64},{64,80},{80,96},{96,112},{112,128},... | collective-permute-start | bytes 1572872 | tf_op jit(solution)/shard_map/ppermute | solution.py:14
  112.3 35.5 %copy-start.18 = (bf16[2,512,256]{2,1,0:T(8,128)(2,1)}, bf16[2,512,256]{2,1,0:T(8,128)(2,1)S(1)}, u32[]{:S(2)}) copy-start(bf16[2,512,256]{2,1,0:T(8,128)(2,1)S(1)} %collective-permute-done.3) | copy-start | bytes 1572868
  112.3 19.3 %collective-permute-start.5 = (bf16[2,512,256]{2,1,0:T(8,128)(2,1)S(1)}, bf16[2,512,256]{2,1,0:T(8,128)(2,1)}, u32[]{:S(2)}, u32[]{:S(2)}) collective-permute-start(bf16[2,512,256]{2,1,0:T(8,128)(2,1)S(1)} %collective-permute-done.3), channel_id=1, source_target_pairs={{0,496},{16,0},{32,16},{48,32},{64,48},{80,64},{96,80},{112,96},{1... | collective-permute-start | bytes 1572872 | tf_op jit(solution)/shard_map/ppermute | solution.py:14
  125.3 53.3 %copy-start.12 = (pred[512,512]{0,1:T(8,128)(4,1)}, pred[512,512]{0,1:T(8,128)(4,1)S(1)}, u32[]{:S(2)}) copy-start(pred[512,512]{0,1:T(8,128)(4,1)S(1)} %compare_and_fusion.8) | copy-start | bytes 786436
  127.1 52.1 %collective-permute-start.6 = (bf16[2,512,256]{2,1,0:T(8,128)(2,1)}, bf16[2,512,256]{2,1,0:T(8,128)(2,1)}, u32[]{:S(2)}, u32[]{:S(2)}) collective-permute-start(bf16[2,512,256]{2,1,0:T(8,128)(2,1)} %collective-permute-done.4), channel_id=1, source_target_pairs={{0,16},{16,32},{32,48},{48,64},{64,80},{80,96},{96,112},{112,128},... | collective-permute-start | bytes 1572872 | tf_op jit(solution)/shard_map/ppermute | solution.py:14
  131.7 57.8 %collective-permute-start.7 = (bf16[2,512,256]{2,1,0:T(8,128)(2,1)}, bf16[2,512,256]{2,1,0:T(8,128)(2,1)}, u32[]{:S(2)}, u32[]{:S(2)}) collective-permute-start(bf16[2,512,256]{2,1,0:T(8,128)(2,1)} %collective-permute-done.5), channel_id=1, source_target_pairs={{0,496},{16,0},{32,16},{48,32},{64,48},{80,64},{96,80},{112,96},{1... | collective-permute-start | bytes 1572872 | tf_op jit(solution)/shard_map/ppermute | solution.py:14
  147.0 32.2 %copy-start.27 = (bf16[512,2,128]{2,1,0:T(2,128)(2,1)}, bf16[512,2,128]{2,1,0:T(2,128)(2,1)S(1)}, u32[]{:S(2)}) copy-start(bf16[512,2,128]{2,1,0:T(2,128)(2,1)S(1)} %reshape_squeeze.19) | copy-start | bytes 786436
  159.7 6.7 %copy-start.17 = (bf16[2,512,256]{2,1,0:T(8,128)(2,1)S(1)}, bf16[2,512,256]{2,1,0:T(8,128)(2,1)}, u32[]{:S(2)}) copy-start(bf16[2,512,256]{2,1,0:T(8,128)(2,1)} %copy-done.16) | copy-start | bytes 1572868
  182.2 2.4 copy-start.13
  192.6 2.3 copy-start.14
  200.2 2.0 copy-start.1
  200.2 2.0 copy-start.3
  200.3 2.0 copy-start.5
  200.3 2.0 copy-start.7
  207.1 2.3 copy-start.15
  207.2 2.6 %copy-start.25 = (bf16[512,2,128]{2,1,0:T(2,128)(2,1)S(1)}, bf16[512,2,128]{2,1,0:T(2,128)(2,1)}, u32[]{:S(2)}) copy-start(bf16[512,2,128]{2,1,0:T(2,128)(2,1)} %copy-done.24) | copy-start | bytes 786436
  207.2 2.6 %copy-start.26 = (pred[512,512]{1,0:T(8,128)(4,1)S(1)}, pred[512,512]{1,0:T(8,128)(4,1)}, u32[]{:S(2)}) copy-start(pred[512,512]{1,0:T(8,128)(4,1)} %iota_compare_fusion) | copy-start | bytes 786436
  (11 other events, 12.4 us)
Sparse Core Ops, SparseCore 0:
  73.2 81.1 all-gather.2
where the time goes:
time: 248 us; the launch traced here: 246 us
  waiting for transfers between devices  60 us (24%)
  starting transfers between devices  56.4 us (23%)
  local copies, waits for them, and re-layouts  31.5 us (13%)
  matrix products  26.6 us (11%)
  blocking collectives  26.4 us (11%)
  between operations  25.1 us (10%)
  other arithmetic  19.7 us (8%)
    all_to_all x2, waiting for transfers between devices, to_heads(): got = lax.all_to_all(send, 'head', split_axis=0, concat_axis=0, tiled=True)  42.7 us
    ppermute x8, starting transfers between devices, shifted(): return lax.ppermute(block, axis, route)  41.7 us
    all_to_all x1, blocking collectives, to_tokens(): got = lax.all_to_all(send, 'head', split_axis=0, concat_axis=0, tiled=True)  26.4 us
    ppermute x8, waiting for transfers between devices, shifted(): return lax.ppermute(block, axis, route)  17.3 us
    all_to_all x2, starting transfers between devices, to_heads(): got = lax.all_to_all(send, 'head', split_axis=0, concat_axis=0, tiled=True)  14.7 us
    dot_general x7, matrix products, block_partial(): jnp.einsum('hts,shd->thd', probs.astype(jnp.bfloat16), val_block, preferr...  12 us
    dot_general x7, matrix products, block_partial(): jnp.einsum('thd,shd->hts', queries, key_block, preferred_element_type=jnp...  11.1 us
    another operation x17, local copies, waits for them, and re-layouts  9.21 us
  transfers between devices with their start and end apart: 11, of which 4 were waited for; matrix products, arithmetic and copies ran while one was open for 23% of the time, Pallas kernels for 0%

commit v1 on v0

--- a/solution.py
+++ b/solution.py
@@ -75,34 +75,33 @@
         heads_dev=heads_dev,
         head_width=head_width,
     )
-    arrivals = []
-    ahead = kv_pair
-    for offset in range(1, forward_steps + 1):
-        ahead = shifted(ahead, "ctx", 1)
-        arrivals.append((ahead, offset))
-    if reach > forward_steps:
-        behind = shifted(kv_pair, "ctx", reach)
-        arrivals.append((behind, reach))
-        for offset in range(reach - 1, forward_steps, -1):
-            behind = shifted(behind, "ctx", -1)
-            arrivals.append((behind, offset))
-    order = []
-    fwd = [a for a in arrivals if a[1] <= forward_steps]
-    bwd = [a for a in arrivals if a[1] > forward_steps]
-    for i in range(max(len(fwd), len(bwd))):
-        if i < len(fwd):
-            order.append(fwd[i])
-        if i < len(bwd):
-            order.append(bwd[i])
-    partials = [absorb(kv_pair, source=own_index)]
     skip = partial(empty_partial, row_count, heads_dev, head_width)
-    for block, offset in order:
+
+    def partial_of(block, offset):
         source = own_index - offset
         last_doc = doc_index(jnp.full((1,), source * row_count + row_count - 1, jnp.int32), starts)[
             0
         ]
         needed = (source >= 0) & (last_doc == query_doc[0])
-        partials.append(lax.cond(needed, partial(absorb, block, source=source), skip))
+        return lax.cond(needed, partial(absorb, block, source=source), skip)
+
+    fwd_offsets = list(range(1, forward_steps + 1))
+    bwd_offsets = list(range(reach, forward_steps, -1))
+    partials = [absorb(kv_pair, source=own_index)]
+    ahead = shifted(kv_pair, "ctx", 1)
+    behind = shifted(kv_pair, "ctx", reach) if bwd_offsets else None
+    for i in range(max(len(fwd_offsets), len(bwd_offsets))):
+        now = []
+        if i < len(fwd_offsets):
+            now.append((ahead, fwd_offsets[i]))
+        if i < len(bwd_offsets):
+            now.append((behind, bwd_offsets[i]))
+        ahead_next = shifted(ahead, "ctx", 1) if i + 1 < len(fwd_offsets) else None
+        behind_next = shifted(behind, "ctx", -1) if i + 1 < len(bwd_offsets) else None
+        done = [partial_of(block, offset) for block, offset in now]
+        ahead_next, behind_next, done = lax.optimization_barrier((ahead_next, behind_next, done))
+        partials.extend(done)
+        ahead, behind = ahead_next, behind_next
     row_max = partials[0][0]
     for part in partials[1:]:
         row_max = jnp.maximum(row_max, part[0])
@@ -185,9 +184,9 @@
     q_soft, k_soft, v_soft, q_light, k_light, v_light, decay_log, norm_gain, doc_lengths
 ):
     parts = lax.axis_size("head")
-    kv_soft = to_heads([k_soft, v_soft], parts)
-    kv_soft, q_soft = lax.optimization_barrier((kv_soft, q_soft))
-    rest = to_heads([q_soft, q_light, k_light, v_light], parts)
+    moved = to_heads([k_soft, v_soft, q_soft, q_light, k_light, v_light], parts)
+    kv_soft = moved[:2]
+    rest = moved[2:]
     heads_dev = decay_log.shape[0]
     row_count = kv_soft.shape[1]
     head_width = kv_soft.shape[2] // heads_dev

time: 248 us -> 254 us (1.024)
  the two profiles are of different devices: /device:TPU:27 before, /device:TPU:3 now
where the time goes in v1:
time: 254 us; the launch traced here: 252 us
  waiting for transfers between devices  73.2 us (29%)
  local copies, waits for them, and re-layouts  40.6 us (16%)
  starting transfers between devices  36.2 us (14%)
  matrix products  32.2 us (13%)
  between operations  24.5 us (10%)
  blocking collectives  23.5 us (9%)
  other arithmetic  21.5 us (8%)
    ppermute x8, waiting for transfers between devices, shifted(): return lax.ppermute(block, axis, route)  37.2 us
    all_to_all x1, waiting for transfers between devices, to_heads(): got = lax.all_to_all(send, 'head', split_axis=0, concat_axis=0, tiled=True)  36 us
    ppermute x8, starting transfers between devices, shifted(): return lax.ppermute(block, axis, route)  25.1 us
    all_to_all x1, blocking collectives, to_tokens(): got = lax.all_to_all(send, 'head', split_axis=0, concat_axis=0, tiled=True)  23.5 us
    dot_general x8, matrix products, block_partial(): jnp.einsum('hts,shd->thd', probs.astype(jnp.bfloat16), val_block, preferr...  14.3 us
    dot_general x8, matrix products, block_partial(): jnp.einsum('thd,shd->hts', queries, key_block, preferred_element_type=jnp...  13.4 us
    another operation x15, local copies, waits for them, and re-layouts  11.4 us
    all_to_all x1, starting transfers between devices, to_heads(): got = lax.all_to_all(send, 'head', split_axis=0, concat_axis=0, tiled=True)  11.1 us
  transfers between devices with their start and end apart: 10, of which 4 were waited for; matrix products, arithmetic and copies ran while one was open for 30% of the time, Pallas kernels for 0%

profile of v1, /device:TPU:3, one launch (start us, length us, event | category | flops | bytes accessed | tf_op | source)
XLA Modules:
  0.0 252.1 jit_solution(10751723183230209685)
XLA Ops:
  12.4 11.1 %all-to-all-start = ((bf16[16,6,32,256]{3,2,1,0:T(8,128)(2,1)}), bf16[16,6,32,256]{3,2,1,0:T(8,128)(2,1)S(1)}, u32[]{:S(2)}, u32[]{:S(2)}) async-start(bf16[16,6,32,256]{3,2,1,0:T(8,128)(2,1)} %copy.339), calls=%async_computation | async-start | bytes 3145728 | tf_op jit(solution)/shard_map/all_to_all | solution.py:172
  25.9 36.0 %all-to-all-done = bf16[16,6,32,256]{3,2,1,0:T(8,128)(2,1)S(1)} async-done(((bf16[16,6,32,256]{3,2,1,0:T(8,128)(2,1)}), bf16[16,6,32,256]{3,2,1,0:T(8,128)(2,1)S(1)}, u32[]{:S(2)}, u32[]{:S(2)}) %all-to-all-start) | async-done | bytes 1572896 | tf_op jit(solution)/shard_map/all_to_all | solution.py:172
  64.9 3.2 %collective-permute-start = (bf16[2,512,256]{2,1,0:T(8,128)(2,1)S(1)}, bf16[2,512,256]{2,1,0:T(8,128)(2,1)}, u32[]{:S(2)}, u32[]{:S(2)}) collective-permute-start(bf16[2,512,256]{2,1,0:T(8,128)(2,1)S(1)} %bitcast.192), channel_id=1, source_target_pairs={{0,16},{16,32},{32,48},{48,64},{64,80},{80,96},{96,112},{112,128},... | collective-permute-start | bytes 1572872 | tf_op jit(solution)/shard_map/ppermute | solution.py:14
  68.1 3.1 %collective-permute-start.2 = (bf16[2,512,256]{2,1,0:T(8,128)(2,1)S(1)}, bf16[2,512,256]{2,1,0:T(8,128)(2,1)}, u32[]{:S(2)}, u32[]{:S(2)}) collective-permute-start(bf16[2,512,256]{2,1,0:T(8,128)(2,1)S(1)} %bitcast.193), channel_id=1, source_target_pairs={{0,128},{16,144},{32,160},{48,176},{64,192},{80,208},{96,224},{112... | collective-permute-start | bytes 1572872 | tf_op jit(solution)/shard_map/ppermute | solution.py:14
  71.5 11.7 %collective-permute-done = bf16[2,512,256]{2,1,0:T(8,128)(2,1)} collective-permute-done((bf16[2,512,256]{2,1,0:T(8,128)(2,1)S(1)}, bf16[2,512,256]{2,1,0:T(8,128)(2,1)}, u32[]{:S(2)}, u32[]{:S(2)}) %collective-permute-start) | collective-permute-done | bytes 524320 | tf_op jit(solution)/shard_map/ppermute | solution.py:14
  83.2 1.9 collective-permute-start.1
  85.2 21.4 %collective-permute-done.2 = bf16[2,512,256]{2,1,0:T(8,128)(2,1)} collective-permute-done((bf16[2,512,256]{2,1,0:T(8,128)(2,1)S(1)}, bf16[2,512,256]{2,1,0:T(8,128)(2,1)}, u32[]{:S(2)}, u32[]{:S(2)}) %collective-permute-start.2) | collective-permute-done | bytes 524320 | tf_op jit(solution)/shard_map/ppermute | solution.py:14
  112.4 5.7 %conditional.8 = (f32[2,512]{1,0:T(2,128)}, f32[2,512]{1,0:T(2,128)S(1)}, f32[512,2,128]{2,0,1:T(8,128)S(1)}) conditional(s32[]{:T(128)} %convert_element_type.154, () %tuple.84, (s32[512]{0:T(512)S(1)}, s32[]{:T(128)}, s32[32]{0:T(128)S(1)}, s32[512]{0:T(512)S(1)}, bf16[2,512,256]{2,1,0:T(8,128)(2,1)}, ...), branch_computations={%region_4.5_spmd, %region_5.9_spmd} | conditional | flops 276085248 | bytes 10782888 | solution.py:86
  118.8 4.1 %collective-permute-done.3 = bf16[2,512,256]{2,1,0:T(8,128)(2,1)} collective-permute-done((bf16[2,512,256]{2,1,0:T(8,128)(2,1)}, bf16[2,512,256]{2,1,0:T(8,128)(2,1)}, u32[]{:S(2)}, u32[]{:S(2)}) %collective-permute-start.3) | collective-permute-done | bytes 524320 | tf_op jit(solution)/shard_map/ppermute | solution.py:14
  122.9 4.4 %collective-permute-start.4 = (bf16[2,512,256]{2,1,0:T(8,128)(2,1)}, bf16[2,512,256]{2,1,0:T(8,128)(2,1)}, u32[]{:S(2)}, u32[]{:S(2)}) collective-permute-start(bf16[2,512,256]{2,1,0:T(8,128)(2,1)} %collective-permute-done.1), channel_id=1, source_target_pairs={{0,16},{16,32},{32,48},{48,64},{64,80},{80,96},{96,112},{112,128},... | collective-permute-start | bytes 1572872 | tf_op jit(solution)/shard_map/ppermute | solution.py:14
  127.2 3.0 %collective-permute-start.5 = (bf16[2,512,256]{2,1,0:T(8,128)(2,1)}, bf16[2,512,256]{2,1,0:T(8,128)(2,1)}, u32[]{:S(2)}, u32[]{:S(2)}) collective-permute-start(bf16[2,512,256]{2,1,0:T(8,128)(2,1)} %collective-permute-done.3), channel_id=1, source_target_pairs={{0,496},{16,0},{32,16},{48,32},{64,48},{80,64},{96,80},{112,96},{1... | collective-permute-start | bytes 1572872 | tf_op jit(solution)/shard_map/ppermute | solution.py:14
  141.6 5.7 %conditional.10 = (f32[2,512]{1,0:T(2,128)}, f32[2,512]{1,0:T(2,128)S(1)}, f32[512,2,128]{2,0,1:T(8,128)S(1)}) conditional(s32[]{:T(128)} %convert_element_type.158, () %tuple.89, (s32[512]{0:T(512)S(1)}, s32[]{:T(128)}, s32[32]{0:T(128)S(1)}, s32[512]{0:T(512)S(1)}, bf16[2,512,256]{2,1,0:T(8,128)(2,1)}, ...), branch_computations={%region_16.17_spmd, %region_17.21_spmd} | conditional | flops 276085248 | bytes 10782888 | solution.py:86
  148.1 5.7 %conditional.11 = (f32[2,512]{1,0:T(2,128)}, f32[2,512]{1,0:T(2,128)S(1)}, f32[512,2,128]{2,0,1:T(8,128)S(1)}) conditional(s32[]{:T(128)} %convert_element_type.160, () %tuple.91, (s32[512]{0:T(512)S(1)}, s32[]{:T(128)}, s32[32]{0:T(128)S(1)}, s32[512]{0:T(512)S(1)}, bf16[2,512,256]{2,1,0:T(8,128)(2,1)}, ...), branch_computations={%region_22.23_spmd, %region_23.27_spmd} | conditional | flops 276085248 | bytes 10782888 | solution.py:86
  153.8 2.4 collective-permute-start.6
  156.2 5.1 %collective-permute-start.7 = (bf16[2,512,256]{2,1,0:T(8,128)(2,1)}, bf16[2,512,256]{2,1,0:T(8,128)(2,1)}, u32[]{:S(2)}, u32[]{:S(2)}) collective-permute-start(bf16[2,512,256]{2,1,0:T(8,128)(2,1)} %collective-permute-done.5), channel_id=1, source_target_pairs={{0,496},{16,0},{32,16},{48,32},{64,48},{80,64},{96,80},{112,96},{1... | collective-permute-start | bytes 1572872 | tf_op jit(solution)/shard_map/ppermute | solution.py:14
  165.6 2.0 copy.365
  168.7 5.7 %conditional.12 = (f32[2,512]{1,0:T(2,128)}, f32[2,512]{1,0:T(2,128)S(1)}, f32[512,2,128]{2,0,1:T(8,128)S(1)}) conditional(s32[]{:T(128)} %convert_element_type.162, () %tuple.94, (s32[512]{0:T(512)S(1)}, s32[]{:T(128)}, s32[32]{0:T(128)S(1)}, s32[512]{0:T(512)S(1)}, bf16[2,512,256]{2,1,0:T(8,128)(2,1)}, ...), branch_computations={%region_28.29_spmd, %region_29.33_spmd} | conditional | flops 276085248 | bytes 11831492 | solution.py:86
  174.4 7.7 %conditional.13 = (f32[2,512]{1,0:T(2,128)}, f32[2,512]{1,0:T(2,128)S(1)}, f32[512,2,128]{2,0,1:T(8,128)S(1)}) conditional(s32[]{:T(128)} %convert_element_type.164, () %tuple.96, (s32[512]{0:T(512)S(1)}, s32[]{:T(128)}, s32[32]{0:T(128)S(1)}, s32[512]{0:T(512)S(1)}, bf16[2,512,256]{2,1,0:T(8,128)(2,1)}, ...), branch_computations={%region_34.35_spmd, %region_35.39_spmd} | conditional | flops 276085248 | bytes 11831492 | solution.py:86
  177.0 2.3 fusion.65
  182.1 10.1 %conditional.14 = (f32[2,512]{1,0:T(2,128)}, f32[2,512]{1,0:T(2,128)S(1)}, f32[512,2,128]{2,0,1:T(8,128)}) conditional(s32[]{:T(128)} %convert_element_type.166, () %tuple.99, (s32[512]{0:T(512)S(1)}, s32[]{:T(128)}, s32[32]{0:T(128)S(1)}, s32[512]{0:T(512)S(1)}, bf16[2,512,256]{2,1,0:T(8,128)(2,1)}, ...), branch_computations={%region_40.41_spmd, %region_41.45_spmd} | conditional | flops 276085248 | bytes 11831492 | solution.py:86
  183.2 2.0 copy.358
  186.4 2.3 fusion.78
  189.9 2.3 convolution_bitcast_fusion.6
  192.2 10.1 %conditional.15 = (f32[2,512]{1,0:T(2,128)}, f32[2,512]{1,0:T(2,128)S(1)}, f32[512,2,128]{2,0,1:T(8,128)}) conditional(s32[]{:T(128)} %convert_element_type.168, () %tuple.101, (s32[512]{0:T(512)S(1)}, s32[]{:T(128)}, s32[32]{0:T(128)S(1)}, s32[512]{0:T(512)S(1)}, bf16[2,512,256]{2,1,0:T(8,128)(2,1)}, ...), branch_computations={%region_46.47_spmd, %region_47.51_spmd} | conditional | flops 276085248 | bytes 11831492 | solution.py:86
  193.3 2.1 copy.360
  196.5 2.3 fusion.91
  200.0 2.3 convolution_bitcast_fusion.7
  202.3 2.0 copy.369
  204.3 2.0 copy.368
  209.2 2.0 fusion.112
  217.6 2.1 multiply_reduce_fusion
  220.3 23.5 %all_to_all.10 = bf16[16,2,32,256]{3,2,1,0:T(8,128)(2,1)S(1)} all-to-all(bf16[16,2,32,256]{3,2,1,0:T(8,128)(2,1)S(1)} %copy.382), channel_id=1, replica_groups=mesh['ctx'=32,'head'=16] {'head'}, dimensions={0} | all-to-all | bytes 1048576 | tf_op jit(solution)/shard_map/all_to_all | solution.py:179
  (201 shorter events, 71.2 us)
Async XLA Ops:
  7.2 3.1 %copy-start.17 = (bf16[32,4096]{1,0:T(8,128)(2,1)S(1)}, bf16[32,4096]{1,0:T(8,128)(2,1)}, u32[]{:S(2)}) copy-start(bf16[32,4096]{1,0:T(8,128)(2,1)} %param.32) | copy-start | bytes 786436
  7.2 3.2 %copy-start.18 = (bf16[32,4096]{1,0:T(8,128)(2,1)S(1)}, bf16[32,4096]{1,0:T(8,128)(2,1)}, u32[]{:S(2)}) copy-start(bf16[32,4096]{1,0:T(8,128)(2,1)} %param.33) | copy-start | bytes 786436
  7.2 3.3 %copy-start.19 = (bf16[32,4096]{1,0:T(8,128)(2,1)S(1)}, bf16[32,4096]{1,0:T(8,128)(2,1)}, u32[]{:S(2)}) copy-start(bf16[32,4096]{1,0:T(8,128)(2,1)} %param.34) | copy-start | bytes 786436
  12.4 11.2 %copy-start.23 = (f32[2,512]{1,0:T(2,128)S(1)}, f32[2,512]{1,0:T(2,128)}, u32[]{:S(2)}) copy-start(f32[2,512]{1,0:T(2,128)} %param.35) | copy-start | bytes 12292
  12.4 49.6 %all-to-all-start = ((bf16[16,6,32,256]{3,2,1,0:T(8,128)(2,1)}), bf16[16,6,32,256]{3,2,1,0:T(8,128)(2,1)S(1)}, u32[]{:S(2)}, u32[]{:S(2)}) async-start(bf16[16,6,32,256]{3,2,1,0:T(8,128)(2,1)} %copy.339), calls=%async_computation | async-start | bytes 3145728 | tf_op jit(solution)/shard_map/all_to_all | solution.py:172
  23.5 188.8 %all-gather.3.cloned.1.call-start = ((), (), s32[]{:S(2)}) async-start(), calls=%async_computation.2 | async-start | bytes 2433024 | tf_op jit(solution)/shard_map/all_gather | solution.py:134
  63.0 8.3 %copy-start.24 = (s32[32]{0:T(128)S(1)}, s32[32]{0:T(128)}, u32[]{:S(2)}) copy-start(s32[32]{0:T(128)} %param.37) | copy-start | bytes 388
  63.1 49.2 %copy-start.20 = (bf16[512,2,128]{2,1,0:T(2,128)(2,1)}, bf16[512,2,128]{2,1,0:T(2,128)(2,1)S(1)}, u32[]{:S(2)}) copy-start(bf16[512,2,128]{2,1,0:T(2,128)(2,1)S(1)} %reshape_squeeze.21) | copy-start | bytes 786436
  64.9 18.4 %collective-permute-start = (bf16[2,512,256]{2,1,0:T(8,128)(2,1)S(1)}, bf16[2,512,256]{2,1,0:T(8,128)(2,1)}, u32[]{:S(2)}, u32[]{:S(2)}) collective-permute-start(bf16[2,512,256]{2,1,0:T(8,128)(2,1)S(1)} %bitcast.192), channel_id=1, source_target_pairs={{0,16},{16,32},{32,48},{48,64},{64,80},{80,96},{96,112},{112,128},... | collective-permute-start | bytes 1572872 | tf_op jit(solution)/shard_map/ppermute | solution.py:14
  68.1 38.5 %collective-permute-start.2 = (bf16[2,512,256]{2,1,0:T(8,128)(2,1)S(1)}, bf16[2,512,256]{2,1,0:T(8,128)(2,1)}, u32[]{:S(2)}, u32[]{:S(2)}) collective-permute-start(bf16[2,512,256]{2,1,0:T(8,128)(2,1)S(1)} %bitcast.193), channel_id=1, source_target_pairs={{0,128},{16,144},{32,160},{48,176},{64,192},{80,208},{96,224},{112... | collective-permute-start | bytes 1572872 | tf_op jit(solution)/shard_map/ppermute | solution.py:14
  83.2 35.5 %collective-permute-start.1 = (bf16[2,512,256]{2,1,0:T(8,128)(2,1)}, bf16[2,512,256]{2,1,0:T(8,128)(2,1)}, u32[]{:S(2)}, u32[]{:S(2)}) collective-permute-start(bf16[2,512,256]{2,1,0:T(8,128)(2,1)} %collective-permute-done), channel_id=1, source_target_pairs={{0,16},{16,32},{32,48},{48,64},{64,80},{80,96},{96,112},{112,128},... | collective-permute-start | bytes 1572872 | tf_op jit(solution)/shard_map/ppermute | solution.py:14
  106.5 16.3 %collective-permute-start.3 = (bf16[2,512,256]{2,1,0:T(8,128)(2,1)}, bf16[2,512,256]{2,1,0:T(8,128)(2,1)}, u32[]{:S(2)}, u32[]{:S(2)}) collective-permute-start(bf16[2,512,256]{2,1,0:T(8,128)(2,1)} %collective-permute-done.2), channel_id=1, source_target_pairs={{0,496},{16,0},{32,16},{48,32},{64,48},{80,64},{96,80},{112,96},{1... | collective-permute-start | bytes 1572872 | tf_op jit(solution)/shard_map/ppermute | solution.py:14
  112.3 34.9 %copy-start.21 = (bf16[512,2,128]{2,1,0:T(2,128)(2,1)}, bf16[512,2,128]{2,1,0:T(2,128)(2,1)S(1)}, u32[]{:S(2)}) copy-start(bf16[512,2,128]{2,1,0:T(2,128)(2,1)S(1)} %reshape_squeeze.19) | copy-start | bytes 786436
  118.1 21.1 %copy-start.11 = (bf16[1,16,32,256]{3,2,1,0:T(8,128)(2,1)S(1)}, bf16[1,16,32,256]{3,2,1,0:T(8,128)(2,1)}, u32[]{:S(2)}) copy-start(bf16[1,16,32,256]{3,2,1,0:T(8,128)(2,1)} %get-tuple-element.565) | copy-start | bytes 786436
  122.9 30.9 %collective-permute-start.4 = (bf16[2,512,256]{2,1,0:T(8,128)(2,1)}, bf16[2,512,256]{2,1,0:T(8,128)(2,1)}, u32[]{:S(2)}, u32[]{:S(2)}) collective-permute-start(bf16[2,512,256]{2,1,0:T(8,128)(2,1)} %collective-permute-done.1), channel_id=1, source_target_pairs={{0,16},{16,32},{32,48},{48,64},{64,80},{80,96},{96,112},{112,128},... | collective-permute-start | bytes 1572872 | tf_op jit(solution)/shard_map/ppermute | solution.py:14
  127.2 26.6 %collective-permute-start.5 = (bf16[2,512,256]{2,1,0:T(8,128)(2,1)}, bf16[2,512,256]{2,1,0:T(8,128)(2,1)}, u32[]{:S(2)}, u32[]{:S(2)}) collective-permute-start(bf16[2,512,256]{2,1,0:T(8,128)(2,1)} %collective-permute-done.3), channel_id=1, source_target_pairs={{0,496},{16,0},{32,16},{48,32},{64,48},{80,64},{96,80},{112,96},{1... | collective-permute-start | bytes 1572872 | tf_op jit(solution)/shard_map/ppermute | solution.py:14
  153.8 2.5 copy-start.2
  153.8 9.3 %copy-start.10 = (pred[512,512]{0,1:T(8,128)(4,1)S(1)}, pred[512,512]{0,1:T(8,128)(4,1)}, u32[]{:S(2)}) copy-start(pred[512,512]{0,1:T(8,128)(4,1)} %compare_and_fusion.8) | copy-start | bytes 786436
  153.8 28.3 %collective-permute-start.6 = (bf16[2,512,256]{2,1,0:T(8,128)(2,1)}, bf16[2,512,256]{2,1,0:T(8,128)(2,1)}, u32[]{:S(2)}, u32[]{:S(2)}) collective-permute-start(bf16[2,512,256]{2,1,0:T(8,128)(2,1)} %collective-permute-done.4), channel_id=1, source_target_pairs={{0,16},{16,32},{32,48},{48,64},{64,80},{80,96},{96,112},{112,128},... | collective-permute-start | bytes 1572872 | tf_op jit(solution)/shard_map/ppermute | solution.py:14
  156.2 25.9 %collective-permute-start.7 = (bf16[2,512,256]{2,1,0:T(8,128)(2,1)}, bf16[2,512,256]{2,1,0:T(8,128)(2,1)}, u32[]{:S(2)}, u32[]{:S(2)}) collective-permute-start(bf16[2,512,256]{2,1,0:T(8,128)(2,1)} %collective-permute-done.5), channel_id=1, source_target_pairs={{0,496},{16,0},{32,16},{48,32},{64,48},{80,64},{96,80},{112,96},{1... | collective-permute-start | bytes 1572872 | tf_op jit(solution)/shard_map/ppermute | solution.py:14
  164.6 3.1 %copy-start.1 = (f32[512,2,128]{2,0,1:T(8,128)S(1)}, f32[512,2,128]{2,0,1:T(8,128)}, u32[]{:S(2)}) copy-start(f32[512,2,128]{2,0,1:T(8,128)} %copy-done) | copy-start | bytes 1572868
  177.0 2.3 copy-start.13
  185.3 3.4 %copy-start.14 = (pred[512,512]{0,1:T(8,128)(4,1)S(1)}, pred[512,512]{0,1:T(8,128)(4,1)}, u32[]{:S(2)}) copy-start(pred[512,512]{0,1:T(8,128)(4,1)} %compare_and_fusion.6) | copy-start | bytes 786436 | tf_op jit(solution)/shard_map/cond
  195.4 3.4 %copy-start.15 = (pred[512,512]{0,1:T(8,128)(4,1)S(1)}, pred[512,512]{0,1:T(8,128)(4,1)}, u32[]{:S(2)}) copy-start(pred[512,512]{0,1:T(8,128)(4,1)} %compare_and_fusion.7) | copy-start | bytes 786436 | tf_op jit(solution)/shard_map/cond
  209.1 2.0 copy-start.3
  209.1 2.0 copy-start.4
  209.1 2.0 copy-start.5
  209.1 2.0 copy-start.6
  209.2 2.0 copy-start.7
  209.2 2.1 copy-start.9
  215.0 2.3 copy-start.16
  217.6 2.1 copy-start.25
  (4 other events, 5.6 us)
Sparse Core Ops, SparseCore 0:
  64.9 81.0 all-gather.2

commit v2 on v1

--- a/solution.py
+++ b/solution.py
@@ -3,6 +3,7 @@
 import jax
 import jax.numpy as jnp
 from jax import lax
+from jax.experimental import pallas as pl
 from jax.sharding import PartitionSpec as P
 
 DOC_REACH = 8
@@ -18,41 +19,61 @@
     return jnp.sum((positions[:, None] >= starts[None, :]).astype(jnp.int32), axis=1) - 1
 
 
-def block_partial(
-    kv_pair,
-    source,
-    queries,
-    query_pos,
-    query_doc,
-    starts,
-    row_count,
-    heads_dev,
-    head_width,
+def online_block_kernel(
+    q_doc, k_doc, q_pos, k_pos, q_ref, k_ref, v_ref, m_in, l_in, acc_in, m_out, l_out, acc_out
 ):
-    key_block = kv_pair[0].reshape(row_count, heads_dev, head_width)
-    val_block = kv_pair[1].reshape(row_count, heads_dev, head_width)
-    key_pos = source * row_count + jnp.arange(row_count, dtype=jnp.int32)
-    key_doc = doc_index(key_pos, starts)
-    allowed = (query_doc[:, None] == key_doc[None, :]) & (key_pos[None, :] <= query_pos[:, None])
-    scores = (
-        jnp.einsum("thd,shd->hts", queries, key_block, preferred_element_type=jnp.float32)
-        / head_width**0.5
-    )
-    scores = jnp.where(allowed[None], scores, -1e30)
-    block_max = jnp.max(scores, axis=2)
-    probs = jnp.where(allowed[None], jnp.exp(scores - block_max[:, :, None]), 0.0)
-    block_total = jnp.sum(probs, axis=2)
-    product = jnp.einsum(
-        "hts,shd->thd", probs.astype(jnp.bfloat16), val_block, preferred_element_type=jnp.float32
-    )
-    return (block_max, block_total, product)
-
-
-def empty_partial(row_count, heads_dev, head_width):
-    return (
-        jnp.full((heads_dev, row_count), -1e30, jnp.float32),
-        jnp.zeros((heads_dev, row_count), jnp.float32),
-        jnp.zeros((row_count, heads_dev, head_width), jnp.float32),
+    heads_dev = m_in.shape[0]
+    head_width = q_ref.shape[1] // heads_dev
+    allowed = (q_doc[...] == k_doc[...]) & (k_pos[...] <= q_pos[...])
+    for h in range(heads_dev):
+        cols = slice(h * head_width, (h + 1) * head_width)
+        scores = lax.dot_general(
+            q_ref[:, cols],
+            k_ref[:, cols],
+            (((1,), (1,)), ((), ())),
+            preferred_element_type=jnp.float32,
+        )
+        scores = jnp.where(allowed, scores / head_width**0.5, -1e30)
+        run_max = m_in[h][:, :1]
+        new_max = jnp.maximum(run_max, jnp.max(scores, axis=1, keepdims=True))
+        correction = jnp.exp(run_max - new_max)
+        probs = jnp.where(allowed, jnp.exp(scores - new_max), 0.0)
+        new_total = l_in[h][:, :1] * correction + jnp.sum(probs, axis=1, keepdims=True)
+        product = jnp.dot(
+            probs.astype(jnp.bfloat16), v_ref[:, cols], preferred_element_type=jnp.float32
+        )
+        acc_out[:, cols] = acc_in[:, cols] * correction + product
+        m_out[h] = jnp.broadcast_to(new_max, m_out.shape[1:])
+        l_out[h] = jnp.broadcast_to(new_total, l_out.shape[1:])
+
+
+def online_block(running, kv_pair, queries, query_doc, query_pos, key_doc, key_pos):
+    run_max, run_total, run_acc = running
+    rows, width = queries.shape
+    heads_dev = run_max.shape[0]
+    flops = 4 * rows * rows * width
+    return pl.pallas_call(
+        online_block_kernel,
+        out_shape=(
+            jax.ShapeDtypeStruct(run_max.shape, jnp.float32),
+            jax.ShapeDtypeStruct(run_total.shape, jnp.float32),
+            jax.ShapeDtypeStruct(run_acc.shape, jnp.float32),
+        ),
+        input_output_aliases={7: 0, 8: 1, 9: 2},
+        cost_estimate=pl.CostEstimate(
+            flops=flops, transcendentals=heads_dev * rows * rows, bytes_accessed=6 * rows * width * 4
+        ),
+    )(
+        query_doc[:, None],
+        key_doc[None, :],
+        query_pos[:, None],
+        key_pos[None, :],
+        queries,
+        kv_pair[0],
+        kv_pair[1],
+        run_max,
+        run_total,
+        run_acc,
     )
 
 
@@ -64,54 +85,47 @@
     starts = jnp.cumsum(doc_lengths) - doc_lengths
     query_pos = own_index * row_count + jnp.arange(row_count, dtype=jnp.int32)
     query_doc = doc_index(query_pos, starts)
-    queries = q_rows.reshape(row_count, heads_dev, head_width)
-    absorb = partial(
-        block_partial,
-        queries=queries,
-        query_pos=query_pos,
-        query_doc=query_doc,
-        starts=starts,
-        row_count=row_count,
-        heads_dev=heads_dev,
-        head_width=head_width,
-    )
-    skip = partial(empty_partial, row_count, heads_dev, head_width)
-
-    def partial_of(block, offset):
+    lanes = 128
+    running = (
+        jnp.full((heads_dev, row_count, lanes), -1e30, jnp.float32),
+        jnp.zeros((heads_dev, row_count, lanes), jnp.float32),
+        jnp.zeros((row_count, heads_dev * head_width), jnp.float32),
+    )
+
+    def absorb(running, block, source):
+        key_pos = source * row_count + jnp.arange(row_count, dtype=jnp.int32)
+        key_doc = doc_index(key_pos, starts)
+        return online_block(running, block, q_rows, query_doc, query_pos, key_doc, key_pos)
+
+    def absorb_if_needed(running, block, offset):
         source = own_index - offset
         last_doc = doc_index(jnp.full((1,), source * row_count + row_count - 1, jnp.int32), starts)[
             0
         ]
         needed = (source >= 0) & (last_doc == query_doc[0])
-        return lax.cond(needed, partial(absorb, block, source=source), skip)
+        return lax.cond(
+            needed, lambda r: absorb(r, block, source), lambda r: r, running
+        )
 
     fwd_offsets = list(range(1, forward_steps + 1))
     bwd_offsets = list(range(reach, forward_steps, -1))
-    partials = [absorb(kv_pair, source=own_index)]
+    running = absorb(running, kv_pair, own_index)
     ahead = shifted(kv_pair, "ctx", 1)
     behind = shifted(kv_pair, "ctx", reach) if bwd_offsets else None
     for i in range(max(len(fwd_offsets), len(bwd_offsets))):
-        now = []
-        if i < len(fwd_offsets):
-            now.append((ahead, fwd_offsets[i]))
-        if i < len(bwd_offsets):
-            now.append((behind, bwd_offsets[i]))
         ahead_next = shifted(ahead, "ctx", 1) if i + 1 < len(fwd_offsets) else None
         behind_next = shifted(behind, "ctx", -1) if i + 1 < len(bwd_offsets) else None
-        done = [partial_of(block, offset) for block, offset in now]
-        ahead_next, behind_next, done = lax.optimization_barrier((ahead_next, behind_next, done))
-        partials.extend(done)
+        if i < len(fwd_offsets):
+            running = absorb_if_needed(running, ahead, fwd_offsets[i])
+        if i < len(bwd_offsets):
+            running = absorb_if_needed(running, behind, bwd_offsets[i])
+        ahead_next, behind_next, running = lax.optimization_barrier(
+            (ahead_next, behind_next, running)
+        )
         ahead, behind = ahead_next, behind_next
-    row_max = partials[0][0]
-    for part in partials[1:]:
-        row_max = jnp.maximum(row_max, part[0])
-    run_total = jnp.zeros_like(row_max)
-    run_acc = jnp.zeros_like(partials[0][2])
-    for part in partials:
-        scale = jnp.exp(part[0] - row_max)
-        run_total = run_total + part[1] * scale
-        run_acc = run_acc + part[2] * scale.T[:, :, None]
-    mixed = run_acc / run_total.T[:, :, None]
+    run_max, run_total, run_acc = running
+    totals = run_total[:, :, 0].T
+    mixed = run_acc.reshape(row_count, heads_dev, head_width) / totals[:, :, None]
     return mixed.astype(jnp.bfloat16).reshape(row_count, heads_dev * head_width)
 
 

time: 254 us -> 241 us (0.949)
  the two profiles are of different devices: /device:TPU:3 before, /device:TPU:23 now
where the time goes in v2:
time: 241 us; the launch traced here: 240 us
  starting transfers between devices  53.2 us (22%)
  waiting for transfers between devices  46.6 us (19%)
  local copies, waits for them, and re-layouts  38.3 us (16%)
  Pallas kernels  36.7 us (15%)
  between operations  24.7 us (10%)
  blocking collectives  22.5 us (9%)
  other arithmetic  13.8 us (6%)
  matrix products  3.55 us (1%)
    ppermute x8, starting transfers between devices, shifted(): return lax.ppermute(block, axis, route)  42 us
    all_to_all x1, waiting for transfers between devices, to_heads(): got = lax.all_to_all(send, 'head', split_axis=0, concat_axis=0, tiled=True)  36.7 us
    pallas_call x8, Pallas kernels, online_block(): pl.pallas_call(online_block_kernel, out_shape=(jax.ShapeDtypeStruct(run_m...  36.7 us
    all_to_all x1, blocking collectives, to_tokens(): got = lax.all_to_all(send, 'head', split_axis=0, concat_axis=0, tiled=True)  22.5 us
    squeeze x7, local copies, waits for them, and re-layouts, online_block(): kv_pair[1]  12.1 us
    all_to_all x1, starting transfers between devices, to_heads(): got = lax.all_to_all(send, 'head', split_axis=0, concat_axis=0, tiled=True)  11.1 us
    ppermute x8, waiting for transfers between devices, shifted(): return lax.ppermute(block, axis, route)  9.88 us
    broadcast_in_dim x7, local copies, waits for them, and re-layouts, online_block(): query_pos[:, None]  6.01 us
  transfers between devices with their start and end apart: 10, of which 2 were waited for; matrix products, arithmetic and copies ran while one was open for 17% of the time, Pallas kernels for 15%

profile of v2, /device:TPU:23, one launch (start us, length us, event | category | flops | bytes accessed | tf_op | source)
XLA Modules:
  0.0 240.1 jit_solution(11362130465755807045)
XLA Ops:
  11.4 11.1 %all-to-all-start = ((bf16[16,6,32,256]{3,2,1,0:T(8,128)(2,1)}), bf16[16,6,32,256]{3,2,1,0:T(8,128)(2,1)S(1)}, u32[]{:S(2)}, u32[]{:S(2)}) async-start(bf16[16,6,32,256]{3,2,1,0:T(8,128)(2,1)} %copy.211), calls=%async_computation | async-start | bytes 3145728 | tf_op jit(solution)/shard_map/all_to_all | solution.py:186
  24.3 36.7 %all-to-all-done = bf16[16,6,32,256]{3,2,1,0:T(8,128)(2,1)S(1)} async-done(((bf16[16,6,32,256]{3,2,1,0:T(8,128)(2,1)}), bf16[16,6,32,256]{3,2,1,0:T(8,128)(2,1)S(1)}, u32[]{:S(2)}, u32[]{:S(2)}) %all-to-all-start) | async-done | bytes 1572896 | tf_op jit(solution)/shard_map/all_to_all | solution.py:186
  64.0 3.2 %collective-permute-start = (bf16[2,512,256]{2,1,0:T(8,128)(2,1)S(1)}, bf16[2,512,256]{2,1,0:T(8,128)(2,1)}, u32[]{:S(2)}, u32[]{:S(2)}) collective-permute-start(bf16[2,512,256]{2,1,0:T(8,128)(2,1)S(1)} %bitcast.189), channel_id=1, source_target_pairs={{0,16},{16,32},{32,48},{48,64},{64,80},{80,96},{96,112},{112,128},... | collective-permute-start | bytes 1572872 | tf_op jit(solution)/shard_map/ppermute | solution.py:15
  67.2 2.1 collective-permute-start.2
  70.5 9.9 %collective-permute-done = bf16[2,512,256]{2,1,0:T(8,128)(2,1)} collective-permute-done((bf16[2,512,256]{2,1,0:T(8,128)(2,1)S(1)}, bf16[2,512,256]{2,1,0:T(8,128)(2,1)}, u32[]{:S(2)}, u32[]{:S(2)}) %collective-permute-start) | collective-permute-done | bytes 524320 | tf_op jit(solution)/shard_map/ppermute | solution.py:15
  80.3 3.4 %collective-permute-start.1 = (bf16[2,512,256]{2,1,0:T(8,128)(2,1)}, bf16[2,512,256]{2,1,0:T(8,128)(2,1)}, u32[]{:S(2)}, u32[]{:S(2)}) collective-permute-start(bf16[2,512,256]{2,1,0:T(8,128)(2,1)} %collective-permute-done), channel_id=1, source_target_pairs={{0,16},{16,32},{32,48},{48,64},{64,80},{80,96},{96,112},{112,128},... | collective-permute-start | bytes 1572872 | tf_op jit(solution)/shard_map/ppermute | solution.py:15
  83.8 1.9 collective-permute-start.3
  91.2 4.6 %shard_map.104 = (f32[2,512,128]{2,1,0:T(8,128)S(1)}, f32[2,512,128]{2,1,0:T(8,128)S(1)}, f32[512,256]{1,0:T(8,128)S(1)}) custom-call(s32[512,1]{1,0:T(8,128)} %copy.213.q_doc, s32[1,512]{1,0:T(1,128)S(1)} %bitcast.200, s32[512,1]{1,0:T(8,128)} %iota_add_fusion.16.q_pos, ...), custom_call_target="tpu_custom_call", output_to_operand_aliasing={{0}: (7, {}), {1}: (8, {}), {2}: (9, {})} | custom-call | flops 268435456 | bytes 3145728 | tf_op jit(solution)/shard_map/pallas_call | solution.py:55
  95.8 9.5 %conditional.8 = ((f32[2,512,128]{2,1,0:T(8,128)S(1)}, f32[2,512,128]{2,1,0:T(8,128)S(1)}, f32[512,256]{1,0:T(8,128)S(1)})) conditional(s32[]{:T(128)} %convert_element_type.140, (f32[2,512,128]{2,1,0:T(8,128)S(1)}, f32[2,512,128]{2,1,0:T(8,128)S(1)}, f32[512,256]{1,0:T(8,128)S(1)}) %shard_map.104, (s32[512]{0:T(512)S(1)}, s32[]{:T(128)}, ...), branch_computations={%region_6.7_spmd, %region_7.9_spmd} | conditional | flops 268485632 | bytes 4214940 | solution.py:106
  95.8 1.9 slice_bitcast_fusion
  100.6 4.6 %branch_1_fun.9 = (f32[2,512,128]{2,1,0:T(8,128)S(1)}, f32[2,512,128]{2,1,0:T(8,128)S(1)}, f32[512,256]{1,0:T(8,128)S(1)}) custom-call(s32[512,1]{1,0:T(8,128)} %copy.194.q_doc, s32[1,512]{1,0:T(1,128)} %bitcast.218, s32[512,1]{1,0:T(8,128)} %copy.195.q_pos, ...), custom_call_target="tpu_custom_call", output_to_operand_aliasing={{0}: (7, {}), {1}: (8, {}), {2}: (9, {})} | custom-call | flops 268435456 | bytes 3145728 | tf_op jit(solution)/shard_map/cond/branch_1_fun/pallas_call | solution.py:55
  105.4 14.9 %collective-permute-start.4 = (bf16[2,512,256]{2,1,0:T(8,128)(2,1)}, bf16[2,512,256]{2,1,0:T(8,128)(2,1)}, u32[]{:S(2)}, u32[]{:S(2)}) collective-permute-start(bf16[2,512,256]{2,1,0:T(8,128)(2,1)} %collective-permute-done.1), channel_id=1, source_target_pairs={{0,16},{16,32},{32,48},{48,64},{64,80},{80,96},{96,112},{112,128},... | collective-permute-start | bytes 1572872 | tf_op jit(solution)/shard_map/ppermute | solution.py:15
  120.3 11.2 %collective-permute-start.5 = (bf16[2,512,256]{2,1,0:T(8,128)(2,1)}, bf16[2,512,256]{2,1,0:T(8,128)(2,1)}, u32[]{:S(2)}, u32[]{:S(2)}) collective-permute-start(bf16[2,512,256]{2,1,0:T(8,128)(2,1)} %collective-permute-done.3), channel_id=1, source_target_pairs={{0,496},{16,0},{32,16},{48,32},{64,48},{80,64},{96,80},{112,96},{1... | collective-permute-start | bytes 1572872 | tf_op jit(solution)/shard_map/ppermute | solution.py:15
  134.1 9.5 %conditional.10 = ((f32[2,512,128]{2,1,0:T(8,128)S(1)}, f32[2,512,128]{2,1,0:T(8,128)S(1)}, f32[512,256]{1,0:T(8,128)S(1)})) conditional(s32[]{:T(128)} %convert_element_type.144, (f32[2,512,128]{2,1,0:T(8,128)S(1)}, f32[2,512,128]{2,1,0:T(8,128)S(1)}, f32[512,256]{1,0:T(8,128)S(1)}) %get-tuple-element.476, (s32[512]{0:T(512)S(1)}, s32[]{:T(128)}, ...), branch_computations={%region_14.15_spmd, %region_15.17_spmd} | conditional | flops 268485632 | bytes 4214940 | solution.py:106
  134.1 1.9 slice_bitcast_fusion.4
  139.0 4.6 %branch_1_fun.11 = (f32[2,512,128]{2,1,0:T(8,128)S(1)}, f32[2,512,128]{2,1,0:T(8,128)S(1)}, f32[512,256]{1,0:T(8,128)S(1)}) custom-call(s32[512,1]{1,0:T(8,128)} %copy.198.q_doc, s32[1,512]{1,0:T(1,128)} %bitcast.220, s32[512,1]{1,0:T(8,128)} %copy.199.q_pos, ...), custom_call_target="tpu_custom_call", output_to_operand_aliasing={{0}: (7, {}), {1}: (8, {}), {2}: (9, {})} | custom-call | flops 268435456 | bytes 3145728 | tf_op jit(solution)/shard_map/cond/branch_1_fun/pallas_call | solution.py:55
  143.6 9.5 %conditional.11 = ((f32[2,512,128]{2,1,0:T(8,128)S(1)}, f32[2,512,128]{2,1,0:T(8,128)S(1)}, f32[512,256]{1,0:T(8,128)S(1)})) conditional(s32[]{:T(128)} %convert_element_type.142, (f32[2,512,128]{2,1,0:T(8,128)S(1)}, f32[2,512,128]{2,1,0:T(8,128)S(1)}, f32[512,256]{1,0:T(8,128)S(1)}) %get-tuple-element.477, (s32[512]{0:T(512)S(1)}, s32[]{:T(128)}, ...), branch_computations={%region_17.18_spmd, %region_18.20_spmd} | conditional | flops 268485632 | bytes 4214940 | solution.py:106
  143.6 1.9 slice_bitcast_fusion.6
  148.5 4.6 %branch_1_fun.12 = (f32[2,512,128]{2,1,0:T(8,128)S(1)}, f32[2,512,128]{2,1,0:T(8,128)S(1)}, f32[512,256]{1,0:T(8,128)S(1)}) custom-call(s32[512,1]{1,0:T(8,128)} %copy.200.q_doc, s32[1,512]{1,0:T(1,128)} %bitcast.221, s32[512,1]{1,0:T(8,128)} %copy.201.q_pos, ...), custom_call_target="tpu_custom_call", output_to_operand_aliasing={{0}: (7, {}), {1}: (8, {}), {2}: (9, {})} | custom-call | flops 268435456 | bytes 3145728 | tf_op jit(solution)/shard_map/cond/branch_1_fun/pallas_call | solution.py:55
  153.1 1.9 collective-permute-start.6
  155.0 3.4 %collective-permute-start.7 = (bf16[2,512,256]{2,1,0:T(8,128)(2,1)}, bf16[2,512,256]{2,1,0:T(8,128)(2,1)S(1)}, u32[]{:S(2)}, u32[]{:S(2)}) collective-permute-start(bf16[2,512,256]{2,1,0:T(8,128)(2,1)} %collective-permute-done.5), channel_id=1, source_target_pairs={{0,496},{16,0},{32,16},{48,32},{64,48},{80,64},{96,80},{112,96},{1... | collective-permute-start | bytes 1572872 | tf_op jit(solution)/shard_map/ppermute | solution.py:15
  163.5 9.7 %conditional.12 = ((f32[2,512,128]{2,1,0:T(8,128)S(1)}, f32[2,512,128]{2,1,0:T(8,128)S(1)}, f32[512,256]{1,0:T(8,128)S(1)})) conditional(s32[]{:T(128)} %convert_element_type.148, (f32[2,512,128]{2,1,0:T(8,128)S(1)}, f32[2,512,128]{2,1,0:T(8,128)S(1)}, f32[512,256]{1,0:T(8,128)S(1)}) %get-tuple-element.478, (s32[512]{0:T(512)S(1)}, s32[]{:T(128)}, ...), branch_computations={%region_22.23_spmd, %region_23.25_spmd} | conditional | flops 268485632 | bytes 4214940 | solution.py:106
  168.6 4.6 %branch_1_fun.13 = (f32[2,512,128]{2,1,0:T(8,128)S(1)}, f32[2,512,128]{2,1,0:T(8,128)S(1)}, f32[512,256]{1,0:T(8,128)S(1)}) custom-call(s32[512,1]{1,0:T(8,128)} %copy.202.q_doc, s32[1,512]{1,0:T(1,128)} %bitcast.222, s32[512,1]{1,0:T(8,128)} %copy.203.q_pos, ...), custom_call_target="tpu_custom_call", output_to_operand_aliasing={{0}: (7, {}), {1}: (8, {}), {2}: (9, {})} | custom-call | flops 268435456 | bytes 3145728 | tf_op jit(solution)/shard_map/cond/branch_1_fun/pallas_call | solution.py:55
  173.2 9.4 %conditional.13 = ((f32[2,512,128]{2,1,0:T(8,128)S(1)}, f32[2,512,128]{2,1,0:T(8,128)S(1)}, f32[512,256]{1,0:T(8,128)S(1)})) conditional(s32[]{:T(128)} %convert_element_type.146, (f32[2,512,128]{2,1,0:T(8,128)S(1)}, f32[2,512,128]{2,1,0:T(8,128)S(1)}, f32[512,256]{1,0:T(8,128)S(1)}) %get-tuple-element.479, (s32[512]{0:T(512)S(1)}, s32[]{:T(128)}, ...), branch_computations={%region_25.26_spmd, %region_26.28_spmd} | conditional | flops 268485632 | bytes 4214940 | solution.py:106
  173.2 1.9 slice_bitcast_fusion.10
  178.1 4.6 %branch_1_fun.14 = (f32[2,512,128]{2,1,0:T(8,128)S(1)}, f32[2,512,128]{2,1,0:T(8,128)S(1)}, f32[512,256]{1,0:T(8,128)S(1)}) custom-call(s32[512,1]{1,0:T(8,128)} %copy.204.q_doc, s32[1,512]{1,0:T(1,128)} %bitcast.223, s32[512,1]{1,0:T(8,128)} %copy.205.q_pos, ...), custom_call_target="tpu_custom_call", output_to_operand_aliasing={{0}: (7, {}), {1}: (8, {}), {2}: (9, {})} | custom-call | flops 268435456 | bytes 3145728 | tf_op jit(solution)/shard_map/cond/branch_1_fun/pallas_call | solution.py:55
  182.7 9.4 %conditional.14 = ((f32[2,512,128]{2,1,0:T(8,128)S(1)}, f32[2,512,128]{2,1,0:T(8,128)S(1)}, f32[512,256]{1,0:T(8,128)S(1)})) conditional(s32[]{:T(128)} %convert_element_type.136, (f32[2,512,128]{2,1,0:T(8,128)S(1)}, f32[2,512,128]{2,1,0:T(8,128)S(1)}, f32[512,256]{1,0:T(8,128)S(1)}) %get-tuple-element.480, (s32[512]{0:T(512)S(1)}, s32[]{:T(128)}, ...), branch_computations={%region_28.29_spmd, %region_29.31_spmd} | conditional | flops 268485632 | bytes 4214940 | solution.py:106
  182.7 1.9 slice_bitcast_fusion.12
  187.5 4.6 %branch_1_fun.15 = (f32[2,512,128]{2,1,0:T(8,128)S(1)}, f32[2,512,128]{2,1,0:T(8,128)S(1)}, f32[512,256]{1,0:T(8,128)S(1)}) custom-call(s32[512,1]{1,0:T(8,128)} %copy.206.q_doc, s32[1,512]{1,0:T(1,128)} %bitcast.224, s32[512,1]{1,0:T(8,128)} %copy.207.q_pos, ...), custom_call_target="tpu_custom_call", output_to_operand_aliasing={{0}: (7, {}), {1}: (8, {}), {2}: (9, {})} | custom-call | flops 268435456 | bytes 3145728 | tf_op jit(solution)/shard_map/cond/branch_1_fun/pallas_call | solution.py:55
  192.1 8.6 %conditional.15 = ((f32[2,512,128]{2,1,0:T(8,128)S(1)}, f32[512,256]{1,0:T(8,128)S(1)})) conditional(s32[]{:T(128)} %convert_element_type.134, (f32[2,512,128]{2,1,0:T(8,128)S(1)}, f32[512,256]{1,0:T(8,128)S(1)}) %tuple.82, (s32[512]{0:T(512)S(1)}, s32[]{:T(128)}, s32[32]{0:T(128)S(1)}, s32[512]{0:T(512)S(1)}, bf16[2,512,256]{2,1,0:T(8,128)(2,1)S(1)}, ...), branch_computations={%region_31.32_spmd, %region_32.34_spmd} | conditional | flops 268485632 | bytes 4214956 | solution.py:106
  195.9 4.6 %branch_1_fun.16 = (f32[2,512,128]{2,1,0:T(8,128)S(1)}, f32[2,512,128]{2,1,0:T(8,128)S(1)}, f32[512,256]{1,0:T(8,128)S(1)}) custom-call(s32[512,1]{1,0:T(8,128)} %copy.208.q_doc, s32[1,512]{1,0:T(1,128)} %bitcast.225, s32[512,1]{1,0:T(8,128)} %copy.209.q_pos, ...), custom_call_target="tpu_custom_call", output_to_operand_aliasing={{0}: (7, {}), {1}: (8, {}), {2}: (9, {})} | custom-call | flops 268435456 | bytes 3145728 | tf_op jit(solution)/shard_map/cond/branch_1_fun/pallas_call | solution.py:55
  209.3 22.5 %all_to_all.10 = bf16[16,2,32,256]{3,2,1,0:T(8,128)(2,1)S(1)} all-to-all(bf16[16,2,32,256]{3,2,1,0:T(8,128)(2,1)S(1)} %copy.226), channel_id=1, replica_groups=mesh['ctx'=32,'head'=16] {'head'}, dimensions={0} | all-to-all | bytes 1048576 | tf_op jit(solution)/shard_map/all_to_all | solution.py:193
  (149 shorter events, 46.5 us)
Async XLA Ops:
  7.2 2.2 copy-start
  7.2 2.2 copy-start.1
  7.2 2.3 copy-start.2
  7.2 2.3 copy-start.3
  11.4 11.2 %copy-start.6 = (f32[2,512]{1,0:T(2,128)S(1)}, f32[2,512]{1,0:T(2,128)}, u32[]{:S(2)}) copy-start(f32[2,512]{1,0:T(2,128)} %param.35) | copy-start | bytes 12292
  11.4 49.6 %all-to-all-start = ((bf16[16,6,32,256]{3,2,1,0:T(8,128)(2,1)}), bf16[16,6,32,256]{3,2,1,0:T(8,128)(2,1)S(1)}, u32[]{:S(2)}, u32[]{:S(2)}) async-start(bf16[16,6,32,256]{3,2,1,0:T(8,128)(2,1)} %copy.211), calls=%async_computation | async-start | bytes 3145728 | tf_op jit(solution)/shard_map/all_to_all | solution.py:186
  22.6 179.7 %all-gather.3.cloned.1.call-start = ((), (), s32[]{:S(2)}) async-start(), calls=%async_computation.2 | async-start | bytes 2433024 | tf_op jit(solution)/shard_map/all_gather | solution.py:148
  62.2 7.2 %copy-start.7 = (s32[32]{0:T(128)S(1)}, s32[32]{0:T(128)}, u32[]{:S(2)}) copy-start(s32[32]{0:T(128)} %param.37) | copy-start | bytes 388
  62.3 1.7 copy-start.4
  64.0 16.3 %collective-permute-start = (bf16[2,512,256]{2,1,0:T(8,128)(2,1)S(1)}, bf16[2,512,256]{2,1,0:T(8,128)(2,1)}, u32[]{:S(2)}, u32[]{:S(2)}) collective-permute-start(bf16[2,512,256]{2,1,0:T(8,128)(2,1)S(1)} %bitcast.189), channel_id=1, source_target_pairs={{0,16},{16,32},{32,48},{48,64},{64,80},{80,96},{96,112},{112,128},... | collective-permute-start | bytes 1572872 | tf_op jit(solution)/shard_map/ppermute | solution.py:15
  67.2 16.5 %collective-permute-start.2 = (bf16[2,512,256]{2,1,0:T(8,128)(2,1)S(1)}, bf16[2,512,256]{2,1,0:T(8,128)(2,1)}, u32[]{:S(2)}, u32[]{:S(2)}) collective-permute-start(bf16[2,512,256]{2,1,0:T(8,128)(2,1)S(1)} %bitcast.190), channel_id=1, source_target_pairs={{0,128},{16,144},{32,160},{48,176},{64,192},{80,208},{96,224},{112... | collective-permute-start | bytes 1572872 | tf_op jit(solution)/shard_map/ppermute | solution.py:15
  80.3 25.1 %collective-permute-start.1 = (bf16[2,512,256]{2,1,0:T(8,128)(2,1)}, bf16[2,512,256]{2,1,0:T(8,128)(2,1)}, u32[]{:S(2)}, u32[]{:S(2)}) collective-permute-start(bf16[2,512,256]{2,1,0:T(8,128)(2,1)} %collective-permute-done), channel_id=1, source_target_pairs={{0,16},{16,32},{32,48},{48,64},{64,80},{80,96},{96,112},{112,128},... | collective-permute-start | bytes 1572872 | tf_op jit(solution)/shard_map/ppermute | solution.py:15
  83.8 21.7 %collective-permute-start.3 = (bf16[2,512,256]{2,1,0:T(8,128)(2,1)}, bf16[2,512,256]{2,1,0:T(8,128)(2,1)}, u32[]{:S(2)}, u32[]{:S(2)}) collective-permute-start(bf16[2,512,256]{2,1,0:T(8,128)(2,1)} %collective-permute-done.2), channel_id=1, source_target_pairs={{0,496},{16,0},{32,16},{48,32},{64,48},{80,64},{96,80},{112,96},{1... | collective-permute-start | bytes 1572872 | tf_op jit(solution)/shard_map/ppermute | solution.py:15
  105.4 47.6 %collective-permute-start.4 = (bf16[2,512,256]{2,1,0:T(8,128)(2,1)}, bf16[2,512,256]{2,1,0:T(8,128)(2,1)}, u32[]{:S(2)}, u32[]{:S(2)}) collective-permute-start(bf16[2,512,256]{2,1,0:T(8,128)(2,1)} %collective-permute-done.1), channel_id=1, source_target_pairs={{0,16},{16,32},{32,48},{48,64},{64,80},{80,96},{96,112},{112,128},... | collective-permute-start | bytes 1572872 | tf_op jit(solution)/shard_map/ppermute | solution.py:15
  120.3 32.7 %collective-permute-start.5 = (bf16[2,512,256]{2,1,0:T(8,128)(2,1)}, bf16[2,512,256]{2,1,0:T(8,128)(2,1)}, u32[]{:S(2)}, u32[]{:S(2)}) collective-permute-start(bf16[2,512,256]{2,1,0:T(8,128)(2,1)} %collective-permute-done.3), channel_id=1, source_target_pairs={{0,496},{16,0},{32,16},{48,32},{64,48},{80,64},{96,80},{112,96},{1... | collective-permute-start | bytes 1572872 | tf_op jit(solution)/shard_map/ppermute | solution.py:15
  153.1 29.6 %collective-permute-start.6 = (bf16[2,512,256]{2,1,0:T(8,128)(2,1)}, bf16[2,512,256]{2,1,0:T(8,128)(2,1)}, u32[]{:S(2)}, u32[]{:S(2)}) collective-permute-start(bf16[2,512,256]{2,1,0:T(8,128)(2,1)} %collective-permute-done.4), channel_id=1, source_target_pairs={{0,16},{16,32},{32,48},{48,64},{64,80},{80,96},{96,112},{112,128},... | collective-permute-start | bytes 1572872 | tf_op jit(solution)/shard_map/ppermute | solution.py:15
  155.0 27.6 %collective-permute-start.7 = (bf16[2,512,256]{2,1,0:T(8,128)(2,1)}, bf16[2,512,256]{2,1,0:T(8,128)(2,1)S(1)}, u32[]{:S(2)}, u32[]{:S(2)}) collective-permute-start(bf16[2,512,256]{2,1,0:T(8,128)(2,1)} %collective-permute-done.5), channel_id=1, source_target_pairs={{0,496},{16,0},{32,16},{48,32},{64,48},{80,64},{96,80},{112,96},{1... | collective-permute-start | bytes 1572872 | tf_op jit(solution)/shard_map/ppermute | solution.py:15
  205.4 2.2 copy-start.5
  207.6 1.1 copy-start.8
Sparse Core Ops, SparseCore 0:
  64.1 79.8 all-gather.2

commit v3 on v2

--- a/solution.py
+++ b/solution.py
@@ -20,11 +20,13 @@
 
 
 def online_block_kernel(
-    q_doc, k_doc, q_pos, k_pos, q_ref, k_ref, v_ref, m_in, l_in, acc_in, m_out, l_out, acc_out
+    q_doc, k_doc, q_pos, k_pos, q_ref, kv_ref, m_in, l_in, acc_in, m_out, l_out, acc_out
 ):
     heads_dev = m_in.shape[0]
     head_width = q_ref.shape[1] // heads_dev
-    allowed = (q_doc[...] == k_doc[...]) & (k_pos[...] <= q_pos[...])
+    k_ref = kv_ref.at[0]
+    v_ref = kv_ref.at[1]
+    allowed = (q_doc[:, :1] == k_doc[:1, :]) & (k_pos[:1, :] <= q_pos[:, :1])
     for h in range(heads_dev):
         cols = slice(h * head_width, (h + 1) * head_width)
         scores = lax.dot_general(
@@ -33,7 +35,7 @@
             (((1,), (1,)), ((), ())),
             preferred_element_type=jnp.float32,
         )
-        scores = jnp.where(allowed, scores / head_width**0.5, -1e30)
+        scores = jnp.where(allowed, scores * (1.0 / head_width**0.5), -1e30)
         run_max = m_in[h][:, :1]
         new_max = jnp.maximum(run_max, jnp.max(scores, axis=1, keepdims=True))
         correction = jnp.exp(run_max - new_max)
@@ -59,18 +61,17 @@
             jax.ShapeDtypeStruct(run_total.shape, jnp.float32),
             jax.ShapeDtypeStruct(run_acc.shape, jnp.float32),
         ),
-        input_output_aliases={7: 0, 8: 1, 9: 2},
+        input_output_aliases={6: 0, 7: 1, 8: 2},
         cost_estimate=pl.CostEstimate(
             flops=flops, transcendentals=heads_dev * rows * rows, bytes_accessed=6 * rows * width * 4
         ),
     )(
-        query_doc[:, None],
-        key_doc[None, :],
-        query_pos[:, None],
-        key_pos[None, :],
+        query_doc,
+        key_doc,
+        query_pos,
+        key_pos,
         queries,
-        kv_pair[0],
-        kv_pair[1],
+        kv_pair,
         run_max,
         run_total,
         run_acc,
@@ -86,6 +87,8 @@
     query_pos = own_index * row_count + jnp.arange(row_count, dtype=jnp.int32)
     query_doc = doc_index(query_pos, starts)
     lanes = 128
+    query_doc_wide = jnp.broadcast_to(query_doc[:, None], (row_count, lanes))
+    query_pos_wide = jnp.broadcast_to(query_pos[:, None], (row_count, lanes))
     running = (
         jnp.full((heads_dev, row_count, lanes), -1e30, jnp.float32),
         jnp.zeros((heads_dev, row_count, lanes), jnp.float32),
@@ -95,7 +98,15 @@
     def absorb(running, block, source):
         key_pos = source * row_count + jnp.arange(row_count, dtype=jnp.int32)
         key_doc = doc_index(key_pos, starts)
-        return online_block(running, block, q_rows, query_doc, query_pos, key_doc, key_pos)
+        return online_block(
+            running,
+            block,
+            q_rows,
+            query_doc_wide,
+            query_pos_wide,
+            jnp.broadcast_to(key_doc[None, :], (8, row_count)),
+            jnp.broadcast_to(key_pos[None, :], (8, row_count)),
+        )
 
     def absorb_if_needed(running, block, offset):
         source = own_index - offset

time: 241 us -> 223 us (0.925)
  the two profiles are of different devices: /device:TPU:23 before, /device:TPU:63 now
where the time goes in v3:
time: 223 us; the launch traced here: 222 us
  waiting for transfers between devices  68.9 us (31%)
  Pallas kernels  40.1 us (18%)
  starting transfers between devices  32.6 us (15%)
  between operations  24.7 us (11%)
  blocking collectives  23.8 us (11%)
  local copies, waits for them, and re-layouts  23.3 us (10%)
  other arithmetic  4.51 us (2%)
  matrix products  3.54 us (2%)
    pallas_call x9, Pallas kernels, online_block(): pl.pallas_call(online_block_kernel, out_shape=(jax.ShapeDtypeStruct(run_m...  40.1 us
    all_to_all x1, waiting for transfers between devices, to_heads(): got = lax.all_to_all(send, 'head', split_axis=0, concat_axis=0, tiled=True)  36.7 us
    ppermute x8, waiting for transfers between devices, shifted(): return lax.ppermute(block, axis, route)  32.1 us
    all_to_all x1, blocking collectives, to_tokens(): got = lax.all_to_all(send, 'head', split_axis=0, concat_axis=0, tiled=True)  23.8 us
    ppermute x8, starting transfers between devices, shifted(): return lax.ppermute(block, axis, route)  21.4 us
    all_to_all x1, starting transfers between devices, to_heads(): got = lax.all_to_all(send, 'head', split_axis=0, concat_axis=0, tiled=True)  11.1 us
    broadcast_in_dim x9, local copies, waits for them, and re-layouts, absorb(): jnp.broadcast_to(key_doc[None, :], (8, row_count))  5.43 us
    broadcast_in_dim x9, local copies, waits for them, and re-layouts, absorb(): jnp.broadcast_to(key_pos[None, :], (8, row_count))  5.38 us
  transfers between devices with their start and end apart: 10, of which 5 were waited for; matrix products, arithmetic and copies ran while one was open for 8% of the time, Pallas kernels for 18%

profile of v3, /device:TPU:63, one launch (start us, length us, event | category | flops | bytes accessed | tf_op | source)
XLA Modules:
  0.0 222.1 jit_solution(763426990785461703)
XLA Ops:
  11.4 11.1 %all-to-all-start = ((bf16[16,6,32,256]{3,2,1,0:T(8,128)(2,1)}), bf16[16,6,32,256]{3,2,1,0:T(8,128)(2,1)S(1)}, u32[]{:S(2)}, u32[]{:S(2)}) async-start(bf16[16,6,32,256]{3,2,1,0:T(8,128)(2,1)} %copy.128), calls=%async_computation | async-start | bytes 3145728 | tf_op jit(solution)/shard_map/all_to_all | solution.py:197
  24.3 36.7 %all-to-all-done = bf16[16,6,32,256]{3,2,1,0:T(8,128)(2,1)S(1)} async-done(((bf16[16,6,32,256]{3,2,1,0:T(8,128)(2,1)}), bf16[16,6,32,256]{3,2,1,0:T(8,128)(2,1)S(1)}, u32[]{:S(2)}, u32[]{:S(2)}) %all-to-all-start) | async-done | bytes 1572896 | tf_op jit(solution)/shard_map/all_to_all | solution.py:197
  63.0 1.9 collective-permute-start
  65.0 2.5 %collective-permute-start.2 = (bf16[2,512,256]{2,1,0:T(8,128)(2,1)S(1)}, bf16[2,512,256]{2,1,0:T(8,128)(2,1)}, u32[]{:S(2)}, u32[]{:S(2)}) collective-permute-start(bf16[2,512,256]{2,1,0:T(8,128)(2,1)S(1)} %bitcast.122), channel_id=1, source_target_pairs={{0,128},{16,144},{32,160},{48,176},{64,192},{80,208},{96,224},{112... | collective-permute-start | bytes 1572872 | tf_op jit(solution)/shard_map/ppermute | solution.py:15
  67.8 11.5 %collective-permute-done = bf16[2,512,256]{2,1,0:T(8,128)(2,1)} collective-permute-done((bf16[2,512,256]{2,1,0:T(8,128)(2,1)S(1)}, bf16[2,512,256]{2,1,0:T(8,128)(2,1)}, u32[]{:S(2)}, u32[]{:S(2)}) %collective-permute-start) | collective-permute-done | bytes 524320 | tf_op jit(solution)/shard_map/ppermute | solution.py:15
  79.3 4.4 %collective-permute-start.1 = (bf16[2,512,256]{2,1,0:T(8,128)(2,1)}, bf16[2,512,256]{2,1,0:T(8,128)(2,1)}, u32[]{:S(2)}, u32[]{:S(2)}) collective-permute-start(bf16[2,512,256]{2,1,0:T(8,128)(2,1)} %collective-permute-done), channel_id=1, source_target_pairs={{0,16},{16,32},{32,48},{48,64},{64,80},{80,96},{96,112},{112,128},... | collective-permute-start | bytes 1572872 | tf_op jit(solution)/shard_map/ppermute | solution.py:15
  83.7 1.9 collective-permute-start.3
  91.3 4.5 %shard_map.104 = (f32[2,512,128]{2,1,0:T(8,128)S(1)}, f32[2,512,128]{2,1,0:T(8,128)S(1)}, f32[512,256]{1,0:T(8,128)S(1)}) custom-call(s32[512,128]{1,0:T(8,128)S(1)} %broadcast_in_dim.84.q_doc, s32[8,512]{1,0:T(8,128)} %broadcast_in_dim.85.k_doc, s32[512,128]{1,0:T(8,128)S(1)} %broadcast_in_dim.86.q_pos, ...), custom_call_target="tpu_custom_call", output_to_operand_aliasing={{0}: (6, {}), {1}: (7, {}), {2}: (8, {})} | custom-call | flops 268435456 | bytes 3145728 | tf_op jit(solution)/shard_map/pallas_call | solution.py:57
  95.7 5.8 %conditional.8 = ((f32[2,512,128]{2,1,0:T(8,128)S(1)}, f32[2,512,128]{2,1,0:T(8,128)S(1)}, f32[512,256]{1,0:T(8,128)S(1)})) conditional(s32[]{:T(128)} %convert_element_type.140, (f32[2,512,128]{2,1,0:T(8,128)S(1)}, f32[2,512,128]{2,1,0:T(8,128)S(1)}, f32[512,256]{1,0:T(8,128)S(1)}) %shard_map.104, (s32[]{:T(128)}, s32[32]{0:T(128)S(1)}, ...), branch_computations={%region_6.7_spmd, %region_7.9_spmd} | conditional | flops 268485120 | bytes 3192984 | solution.py:117
  97.0 4.5 %branch_1_fun.9 = (f32[2,512,128]{2,1,0:T(8,128)S(1)}, f32[2,512,128]{2,1,0:T(8,128)S(1)}, f32[512,256]{1,0:T(8,128)S(1)}) custom-call(s32[512,128]{1,0:T(8,128)S(1)} %get-tuple-element.227.q_doc, s32[8,512]{1,0:T(8,128)} %broadcast_in_dim.24.k_doc, ...), custom_call_target="tpu_custom_call", output_to_operand_aliasing={{0}: (6, {}), {1}: (7, {}), {2}: (8, {})} | custom-call | flops 268435456 | bytes 3145728 | tf_op jit(solution)/shard_map/cond/branch_1_fun/pallas_call | solution.py:57
  101.5 5.8 %conditional.9 = ((f32[2,512,128]{2,1,0:T(8,128)S(1)}, f32[2,512,128]{2,1,0:T(8,128)S(1)}, f32[512,256]{1,0:T(8,128)S(1)})) conditional(s32[]{:T(128)} %convert_element_type.138, (f32[2,512,128]{2,1,0:T(8,128)S(1)}, f32[2,512,128]{2,1,0:T(8,128)S(1)}, f32[512,256]{1,0:T(8,128)S(1)}) %get-tuple-element.454, (s32[]{:T(128)}, s32[32]{0:T(128)S(1)}, ...), branch_computations={%region_9.10_spmd, %region_10.12_spmd} | conditional | flops 268485120 | bytes 3192984 | solution.py:117
  102.8 4.5 %branch_1_fun.10 = (f32[2,512,128]{2,1,0:T(8,128)S(1)}, f32[2,512,128]{2,1,0:T(8,128)S(1)}, f32[512,256]{1,0:T(8,128)S(1)}) custom-call(s32[512,128]{1,0:T(8,128)S(1)} %get-tuple-element.236.q_doc, s32[8,512]{1,0:T(8,128)} %broadcast_in_dim.28.k_doc, ...), custom_call_target="tpu_custom_call", output_to_operand_aliasing={{0}: (6, {}), {1}: (7, {}), {2}: (8, {})} | custom-call | flops 268435456 | bytes 3145728 | tf_op jit(solution)/shard_map/cond/branch_1_fun/pallas_call | solution.py:57
  107.3 14.3 %collective-permute-done.3 = bf16[2,512,256]{2,1,0:T(8,128)(2,1)} collective-permute-done((bf16[2,512,256]{2,1,0:T(8,128)(2,1)}, bf16[2,512,256]{2,1,0:T(8,128)(2,1)}, u32[]{:S(2)}, u32[]{:S(2)}) %collective-permute-start.3) | collective-permute-done | bytes 524320 | tf_op jit(solution)/shard_map/ppermute | solution.py:15
  121.5 3.5 %collective-permute-start.4 = (bf16[2,512,256]{2,1,0:T(8,128)(2,1)}, bf16[2,512,256]{2,1,0:T(8,128)(2,1)}, u32[]{:S(2)}, u32[]{:S(2)}) collective-permute-start(bf16[2,512,256]{2,1,0:T(8,128)(2,1)} %collective-permute-done.1), channel_id=1, source_target_pairs={{0,16},{16,32},{32,48},{48,64},{64,80},{80,96},{96,112},{112,128},... | collective-permute-start | bytes 1572872 | tf_op jit(solution)/shard_map/ppermute | solution.py:15
  125.0 1.9 collective-permute-start.5
  129.5 6.0 %conditional.10 = ((f32[2,512,128]{2,1,0:T(8,128)S(1)}, f32[2,512,128]{2,1,0:T(8,128)S(1)}, f32[512,256]{1,0:T(8,128)S(1)})) conditional(s32[]{:T(128)} %convert_element_type.144, (f32[2,512,128]{2,1,0:T(8,128)S(1)}, f32[2,512,128]{2,1,0:T(8,128)S(1)}, f32[512,256]{1,0:T(8,128)S(1)}) %get-tuple-element.455, (s32[]{:T(128)}, s32[32]{0:T(128)S(1)}, ...), branch_computations={%region_14.15_spmd, %region_15.17_spmd} | conditional | flops 268485120 | bytes 3192984 | solution.py:117
  131.0 4.5 %branch_1_fun.11 = (f32[2,512,128]{2,1,0:T(8,128)S(1)}, f32[2,512,128]{2,1,0:T(8,128)S(1)}, f32[512,256]{1,0:T(8,128)S(1)}) custom-call(s32[512,128]{1,0:T(8,128)S(1)} %get-tuple-element.245.q_doc, s32[8,512]{1,0:T(8,128)} %broadcast_in_dim.36.k_doc, ...), custom_call_target="tpu_custom_call", output_to_operand_aliasing={{0}: (6, {}), {1}: (7, {}), {2}: (8, {})} | custom-call | flops 268435456 | bytes 3145728 | tf_op jit(solution)/shard_map/cond/branch_1_fun/pallas_call | solution.py:57
  135.5 5.8 %conditional.11 = ((f32[2,512,128]{2,1,0:T(8,128)S(1)}, f32[2,512,128]{2,1,0:T(8,128)S(1)}, f32[512,256]{1,0:T(8,128)S(1)})) conditional(s32[]{:T(128)} %convert_element_type.142, (f32[2,512,128]{2,1,0:T(8,128)S(1)}, f32[2,512,128]{2,1,0:T(8,128)S(1)}, f32[512,256]{1,0:T(8,128)S(1)}) %get-tuple-element.456, (s32[]{:T(128)}, s32[32]{0:T(128)S(1)}, ...), branch_computations={%region_17.18_spmd, %region_18.20_spmd} | conditional | flops 268485120 | bytes 3192984 | solution.py:117
  136.8 4.5 %branch_1_fun.12 = (f32[2,512,128]{2,1,0:T(8,128)S(1)}, f32[2,512,128]{2,1,0:T(8,128)S(1)}, f32[512,256]{1,0:T(8,128)S(1)}) custom-call(s32[512,128]{1,0:T(8,128)S(1)} %get-tuple-element.254.q_doc, s32[8,512]{1,0:T(8,128)} %broadcast_in_dim.40.k_doc, ...), custom_call_target="tpu_custom_call", output_to_operand_aliasing={{0}: (6, {}), {1}: (7, {}), {2}: (8, {})} | custom-call | flops 268435456 | bytes 3145728 | tf_op jit(solution)/shard_map/cond/branch_1_fun/pallas_call | solution.py:57
  141.2 2.4 %collective-permute-done.4 = bf16[2,512,256]{2,1,0:T(8,128)(2,1)} collective-permute-done((bf16[2,512,256]{2,1,0:T(8,128)(2,1)}, bf16[2,512,256]{2,1,0:T(8,128)(2,1)}, u32[]{:S(2)}, u32[]{:S(2)}) %collective-permute-start.4) | collective-permute-done | bytes 524320 | tf_op jit(solution)/shard_map/ppermute | solution.py:15
  143.6 3.9 %collective-permute-done.5 = bf16[2,512,256]{2,1,0:T(8,128)(2,1)} collective-permute-done((bf16[2,512,256]{2,1,0:T(8,128)(2,1)}, bf16[2,512,256]{2,1,0:T(8,128)(2,1)}, u32[]{:S(2)}, u32[]{:S(2)}) %collective-permute-start.5) | collective-permute-done | bytes 524320 | tf_op jit(solution)/shard_map/ppermute | solution.py:15
  147.5 2.2 collective-permute-start.6
  149.7 3.1 %collective-permute-start.7 = (bf16[2,512,256]{2,1,0:T(8,128)(2,1)}, bf16[2,512,256]{2,1,0:T(8,128)(2,1)}, u32[]{:S(2)}, u32[]{:S(2)}) collective-permute-start(bf16[2,512,256]{2,1,0:T(8,128)(2,1)} %collective-permute-done.5), channel_id=1, source_target_pairs={{0,496},{16,0},{32,16},{48,32},{64,48},{80,64},{96,80},{112,96},{1... | collective-permute-start | bytes 1572872 | tf_op jit(solution)/shard_map/ppermute | solution.py:15
  158.0 5.8 %conditional.12 = ((f32[2,512,128]{2,1,0:T(8,128)S(1)}, f32[2,512,128]{2,1,0:T(8,128)S(1)}, f32[512,256]{1,0:T(8,128)S(1)})) conditional(s32[]{:T(128)} %convert_element_type.148, (f32[2,512,128]{2,1,0:T(8,128)S(1)}, f32[2,512,128]{2,1,0:T(8,128)S(1)}, f32[512,256]{1,0:T(8,128)S(1)}) %get-tuple-element.457, (s32[]{:T(128)}, s32[32]{0:T(128)S(1)}, ...), branch_computations={%region_22.23_spmd, %region_23.25_spmd} | conditional | flops 268485120 | bytes 3192984 | solution.py:117
  159.4 4.5 %branch_1_fun.13 = (f32[2,512,128]{2,1,0:T(8,128)S(1)}, f32[2,512,128]{2,1,0:T(8,128)S(1)}, f32[512,256]{1,0:T(8,128)S(1)}) custom-call(s32[512,128]{1,0:T(8,128)S(1)} %get-tuple-element.263.q_doc, s32[8,512]{1,0:T(8,128)} %broadcast_in_dim.42.k_doc, ...), custom_call_target="tpu_custom_call", output_to_operand_aliasing={{0}: (6, {}), {1}: (7, {}), {2}: (8, {})} | custom-call | flops 268435456 | bytes 3145728 | tf_op jit(solution)/shard_map/cond/branch_1_fun/pallas_call | solution.py:57
  163.8 5.8 %conditional.13 = ((f32[2,512,128]{2,1,0:T(8,128)S(1)}, f32[2,512,128]{2,1,0:T(8,128)S(1)}, f32[512,256]{1,0:T(8,128)S(1)})) conditional(s32[]{:T(128)} %convert_element_type.146, (f32[2,512,128]{2,1,0:T(8,128)S(1)}, f32[2,512,128]{2,1,0:T(8,128)S(1)}, f32[512,256]{1,0:T(8,128)S(1)}) %get-tuple-element.458, (s32[]{:T(128)}, s32[32]{0:T(128)S(1)}, ...), branch_computations={%region_25.26_spmd, %region_26.28_spmd} | conditional | flops 268485120 | bytes 3192984 | solution.py:117
  165.1 4.5 %branch_1_fun.14 = (f32[2,512,128]{2,1,0:T(8,128)S(1)}, f32[2,512,128]{2,1,0:T(8,128)S(1)}, f32[512,256]{1,0:T(8,128)S(1)}) custom-call(s32[512,128]{1,0:T(8,128)S(1)} %get-tuple-element.272.q_doc, s32[8,512]{1,0:T(8,128)} %broadcast_in_dim.56.k_doc, ...), custom_call_target="tpu_custom_call", output_to_operand_aliasing={{0}: (6, {}), {1}: (7, {}), {2}: (8, {})} | custom-call | flops 268435456 | bytes 3145728 | tf_op jit(solution)/shard_map/cond/branch_1_fun/pallas_call | solution.py:57
  169.6 6.0 %conditional.14 = ((f32[2,512,128]{2,1,0:T(8,128)S(1)}, f32[2,512,128]{2,1,0:T(8,128)S(1)}, f32[512,256]{1,0:T(8,128)S(1)})) conditional(s32[]{:T(128)} %convert_element_type.136, (f32[2,512,128]{2,1,0:T(8,128)S(1)}, f32[2,512,128]{2,1,0:T(8,128)S(1)}, f32[512,256]{1,0:T(8,128)S(1)}) %get-tuple-element.459, (s32[]{:T(128)}, s32[32]{0:T(128)S(1)}, ...), branch_computations={%region_28.29_spmd, %region_29.31_spmd} | conditional | flops 268485120 | bytes 3192984 | solution.py:117
  171.1 4.5 %branch_1_fun.15 = (f32[2,512,128]{2,1,0:T(8,128)S(1)}, f32[2,512,128]{2,1,0:T(8,128)S(1)}, f32[512,256]{1,0:T(8,128)S(1)}) custom-call(s32[512,128]{1,0:T(8,128)S(1)} %get-tuple-element.281.q_doc, s32[8,512]{1,0:T(8,128)} %broadcast_in_dim.58.k_doc, ...), custom_call_target="tpu_custom_call", output_to_operand_aliasing={{0}: (6, {}), {1}: (7, {}), {2}: (8, {})} | custom-call | flops 268435456 | bytes 3145728 | tf_op jit(solution)/shard_map/cond/branch_1_fun/pallas_call | solution.py:57
  175.6 5.8 %conditional.15 = ((f32[2,512,128]{2,1,0:T(8,128)S(1)}, f32[512,256]{1,0:T(8,128)S(1)})) conditional(s32[]{:T(128)} %convert_element_type.134, (f32[2,512,128]{2,1,0:T(8,128)S(1)}, f32[512,256]{1,0:T(8,128)S(1)}) %tuple.82, (s32[]{:T(128)}, s32[32]{0:T(128)S(1)}, s32[512,128]{1,0:T(8,128)S(1)}, s32[512,128]{1,0:T(8,128)S(1)}, ...), branch_computations={%region_31.32_spmd, %region_32.34_spmd} | conditional | flops 268485120 | bytes 3193000 | solution.py:117
  176.9 4.5 %branch_1_fun.16 = (f32[2,512,128]{2,1,0:T(8,128)S(1)}, f32[2,512,128]{2,1,0:T(8,128)S(1)}, f32[512,256]{1,0:T(8,128)S(1)}) custom-call(s32[512,128]{1,0:T(8,128)S(1)} %get-tuple-element.290.q_doc, s32[8,512]{1,0:T(8,128)} %broadcast_in_dim.60.k_doc, ...), custom_call_target="tpu_custom_call", output_to_operand_aliasing={{0}: (6, {}), {1}: (7, {}), {2}: (8, {})} | custom-call | flops 268435456 | bytes 3145728 | tf_op jit(solution)/shard_map/cond/branch_1_fun/pallas_call | solution.py:57
  189.9 23.8 %all_to_all.10 = bf16[16,2,32,256]{3,2,1,0:T(8,128)(2,1)S(1)} all-to-all(bf16[16,2,32,256]{3,2,1,0:T(8,128)(2,1)S(1)} %copy.142), channel_id=1, replica_groups=mesh['ctx'=32,'head'=16] {'head'}, dimensions={0} | all-to-all | bytes 1048576 | tf_op jit(solution)/shard_map/all_to_all | solution.py:204
  (144 shorter events, 31.5 us)
Async XLA Ops:
  7.2 2.2 copy-start.1
  7.2 2.2 copy-start.2
  7.2 2.3 %copy-start.3 = (bf16[32,4096]{1,0:T(8,128)(2,1)S(1)}, bf16[32,4096]{1,0:T(8,128)(2,1)}, u32[]{:S(2)}) copy-start(bf16[32,4096]{1,0:T(8,128)(2,1)} %param.33) | copy-start | bytes 786436
  7.2 2.3 %copy-start.4 = (bf16[32,4096]{1,0:T(8,128)(2,1)S(1)}, bf16[32,4096]{1,0:T(8,128)(2,1)}, u32[]{:S(2)}) copy-start(bf16[32,4096]{1,0:T(8,128)(2,1)} %param.34) | copy-start | bytes 786436
  11.4 11.2 %copy-start.7 = (f32[2,512]{1,0:T(2,128)S(1)}, f32[2,512]{1,0:T(2,128)}, u32[]{:S(2)}) copy-start(f32[2,512]{1,0:T(2,128)} %param.35) | copy-start | bytes 12292
  11.4 49.6 %all-to-all-start = ((bf16[16,6,32,256]{3,2,1,0:T(8,128)(2,1)}), bf16[16,6,32,256]{3,2,1,0:T(8,128)(2,1)S(1)}, u32[]{:S(2)}, u32[]{:S(2)}) async-start(bf16[16,6,32,256]{3,2,1,0:T(8,128)(2,1)} %copy.128), calls=%async_computation | async-start | bytes 3145728 | tf_op jit(solution)/shard_map/all_to_all | solution.py:197
  22.6 160.3 %all-gather.3.cloned.1.call-start = ((), (), s32[]{:S(2)}) async-start(), calls=%async_computation.2 | async-start | bytes 2433024 | tf_op jit(solution)/shard_map/all_gather | solution.py:159
  61.2 1.7 copy-start.5
  62.0 5.6 %copy-start.8 = (s32[32]{0:T(128)S(1)}, s32[32]{0:T(128)}, u32[]{:S(2)}) copy-start(s32[32]{0:T(128)} %param.37) | copy-start | bytes 388
  63.0 28.2 %copy-start = (bf16[2,16,32,256]{3,2,1,0:T(8,128)(2,1)}, bf16[2,16,32,256]{3,2,1,0:T(8,128)(2,1)S(1)}, u32[]{:S(2)}) copy-start(bf16[2,16,32,256]{3,2,1,0:T(8,128)(2,1)S(1)} %copy.129) | copy-start | bytes 1572868
  63.0 16.3 %collective-permute-start = (bf16[2,512,256]{2,1,0:T(8,128)(2,1)S(1)}, bf16[2,512,256]{2,1,0:T(8,128)(2,1)}, u32[]{:S(2)}, u32[]{:S(2)}) collective-permute-start(bf16[2,512,256]{2,1,0:T(8,128)(2,1)S(1)} %bitcast.121), channel_id=1, source_target_pairs={{0,16},{16,32},{32,48},{48,64},{64,80},{80,96},{96,112},{112,128},... | collective-permute-start | bytes 1572872 | tf_op jit(solution)/shard_map/ppermute | solution.py:15
  65.0 18.8 %collective-permute-start.2 = (bf16[2,512,256]{2,1,0:T(8,128)(2,1)S(1)}, bf16[2,512,256]{2,1,0:T(8,128)(2,1)}, u32[]{:S(2)}, u32[]{:S(2)}) collective-permute-start(bf16[2,512,256]{2,1,0:T(8,128)(2,1)S(1)} %bitcast.122), channel_id=1, source_target_pairs={{0,128},{16,144},{32,160},{48,176},{64,192},{80,208},{96,224},{112... | collective-permute-start | bytes 1572872 | tf_op jit(solution)/shard_map/ppermute | solution.py:15
  79.3 27.9 %collective-permute-start.1 = (bf16[2,512,256]{2,1,0:T(8,128)(2,1)}, bf16[2,512,256]{2,1,0:T(8,128)(2,1)}, u32[]{:S(2)}, u32[]{:S(2)}) collective-permute-start(bf16[2,512,256]{2,1,0:T(8,128)(2,1)} %collective-permute-done), channel_id=1, source_target_pairs={{0,16},{16,32},{32,48},{48,64},{64,80},{80,96},{96,112},{112,128},... | collective-permute-start | bytes 1572872 | tf_op jit(solution)/shard_map/ppermute | solution.py:15
  83.7 37.8 %collective-permute-start.3 = (bf16[2,512,256]{2,1,0:T(8,128)(2,1)}, bf16[2,512,256]{2,1,0:T(8,128)(2,1)}, u32[]{:S(2)}, u32[]{:S(2)}) collective-permute-start(bf16[2,512,256]{2,1,0:T(8,128)(2,1)} %collective-permute-done.2), channel_id=1, source_target_pairs={{0,496},{16,0},{32,16},{48,32},{64,48},{80,64},{96,80},{112,96},{1... | collective-permute-start | bytes 1572872 | tf_op jit(solution)/shard_map/ppermute | solution.py:15
  121.5 22.1 %collective-permute-start.4 = (bf16[2,512,256]{2,1,0:T(8,128)(2,1)}, bf16[2,512,256]{2,1,0:T(8,128)(2,1)}, u32[]{:S(2)}, u32[]{:S(2)}) collective-permute-start(bf16[2,512,256]{2,1,0:T(8,128)(2,1)} %collective-permute-done.1), channel_id=1, source_target_pairs={{0,16},{16,32},{32,48},{48,64},{64,80},{80,96},{96,112},{112,128},... | collective-permute-start | bytes 1572872 | tf_op jit(solution)/shard_map/ppermute | solution.py:15
  125.0 22.5 %collective-permute-start.5 = (bf16[2,512,256]{2,1,0:T(8,128)(2,1)}, bf16[2,512,256]{2,1,0:T(8,128)(2,1)}, u32[]{:S(2)}, u32[]{:S(2)}) collective-permute-start(bf16[2,512,256]{2,1,0:T(8,128)(2,1)} %collective-permute-done.3), channel_id=1, source_target_pairs={{0,496},{16,0},{32,16},{48,32},{64,48},{80,64},{96,80},{112,96},{1... | collective-permute-start | bytes 1572872 | tf_op jit(solution)/shard_map/ppermute | solution.py:15
  147.5 22.1 %collective-permute-start.6 = (bf16[2,512,256]{2,1,0:T(8,128)(2,1)}, bf16[2,512,256]{2,1,0:T(8,128)(2,1)}, u32[]{:S(2)}, u32[]{:S(2)}) collective-permute-start(bf16[2,512,256]{2,1,0:T(8,128)(2,1)} %collective-permute-done.4), channel_id=1, source_target_pairs={{0,16},{16,32},{32,48},{48,64},{64,80},{80,96},{96,112},{112,128},... | collective-permute-start | bytes 1572872 | tf_op jit(solution)/shard_map/ppermute | solution.py:15
  149.7 19.8 %collective-permute-start.7 = (bf16[2,512,256]{2,1,0:T(8,128)(2,1)}, bf16[2,512,256]{2,1,0:T(8,128)(2,1)}, u32[]{:S(2)}, u32[]{:S(2)}) collective-permute-start(bf16[2,512,256]{2,1,0:T(8,128)(2,1)} %collective-permute-done.5), channel_id=1, source_target_pairs={{0,496},{16,0},{32,16},{48,32},{64,48},{80,64},{96,80},{112,96},{1... | collective-permute-start | bytes 1572872 | tf_op jit(solution)/shard_map/ppermute | solution.py:15
  186.0 2.2 %copy-start.6 = (bf16[512,2,128]{2,1,0:T(2,128)(2,1)S(1)}, bf16[512,2,128]{2,1,0:T(2,128)(2,1)}, u32[]{:S(2)}) copy-start(bf16[512,2,128]{2,1,0:T(2,128)(2,1)} %copy-done.5) | copy-start | bytes 786436
  188.3 1.1 copy-start.9
Sparse Core Ops, SparseCore 0:
  63.1 79.9 all-gather.2

commit v4 on v3

--- a/solution.py
+++ b/solution.py
@@ -23,30 +23,38 @@
     q_doc, k_doc, q_pos, k_pos, q_ref, kv_ref, m_in, l_in, acc_in, m_out, l_out, acc_out
 ):
     heads_dev = m_in.shape[0]
+    rows = q_ref.shape[0]
     head_width = q_ref.shape[1] // heads_dev
-    k_ref = kv_ref.at[0]
-    v_ref = kv_ref.at[1]
-    allowed = (q_doc[:, :1] == k_doc[:1, :]) & (k_pos[:1, :] <= q_pos[:, :1])
-    for h in range(heads_dev):
-        cols = slice(h * head_width, (h + 1) * head_width)
-        scores = lax.dot_general(
-            q_ref[:, cols],
-            k_ref[:, cols],
-            (((1,), (1,)), ((), ())),
-            preferred_element_type=jnp.float32,
-        )
-        scores = jnp.where(allowed, scores * (1.0 / head_width**0.5), -1e30)
-        run_max = m_in[h][:, :1]
-        new_max = jnp.maximum(run_max, jnp.max(scores, axis=1, keepdims=True))
-        correction = jnp.exp(run_max - new_max)
-        probs = jnp.where(allowed, jnp.exp(scores - new_max), 0.0)
-        new_total = l_in[h][:, :1] * correction + jnp.sum(probs, axis=1, keepdims=True)
-        product = jnp.dot(
-            probs.astype(jnp.bfloat16), v_ref[:, cols], preferred_element_type=jnp.float32
-        )
-        acc_out[:, cols] = acc_in[:, cols] * correction + product
-        m_out[h] = jnp.broadcast_to(new_max, m_out.shape[1:])
-        l_out[h] = jnp.broadcast_to(new_total, l_out.shape[1:])
+    chunk = 128
+    key_doc = k_doc[:1, :]
+    key_pos = k_pos[:1, :]
+
+    def body(i, carry):
+        r = pl.ds(pl.multiple_of(i * chunk, chunk), chunk)
+        allowed = (q_doc[r, :1] == key_doc) & (key_pos <= q_pos[r, :1])
+        for h in range(heads_dev):
+            cols = slice(h * head_width, (h + 1) * head_width)
+            scores = lax.dot_general(
+                q_ref[r, cols],
+                kv_ref[0, :, cols],
+                (((1,), (1,)), ((), ())),
+                preferred_element_type=jnp.float32,
+            )
+            scores = jnp.where(allowed, scores * (1.0 / head_width**0.5), -1e30)
+            run_max = m_in[h, r, :1]
+            new_max = jnp.maximum(run_max, jnp.max(scores, axis=1, keepdims=True))
+            correction = jnp.exp(run_max - new_max)
+            probs = jnp.exp(scores - new_max)
+            new_total = l_in[h, r, :1] * correction + jnp.sum(probs, axis=1, keepdims=True)
+            product = jnp.dot(
+                probs.astype(jnp.bfloat16), kv_ref[1, :, cols], preferred_element_type=jnp.float32
+            )
+            acc_out[r, cols] = acc_in[r, cols] * correction + product
+            m_out[h, r, :] = jnp.broadcast_to(new_max, (chunk, m_out.shape[2]))
+            l_out[h, r, :] = jnp.broadcast_to(new_total, (chunk, l_out.shape[2]))
+        return carry
+
+    lax.fori_loop(0, rows // chunk, body, 0)
 
 
 def online_block(running, kv_pair, queries, query_doc, query_pos, key_doc, key_pos):

time: 223 us -> 228 us (1.022)
  the two profiles are of different devices: /device:TPU:63 before, /device:TPU:5 now
where the time goes in v4:
time: 228 us; the launch traced here: 227 us
  waiting for transfers between devices  72.4 us (32%)
  starting transfers between devices  39.5 us (17%)
  Pallas kernels  36.1 us (16%)
  between operations  24.7 us (11%)
  blocking collectives  24 us (11%)
  local copies, waits for them, and re-layouts  22.1 us (10%)
  other arithmetic  4.41 us (2%)
  matrix products  3.55 us (2%)
    all_to_all x1, waiting for transfers between devices, to_heads(): got = lax.all_to_all(send, 'head', split_axis=0, concat_axis=0, tiled=True)  36.7 us
    pallas_call x8, Pallas kernels, online_block(): pl.pallas_call(online_block_kernel, out_shape=(jax.ShapeDtypeStruct(run_m...  36.1 us
    ppermute x8, waiting for transfers between devices, shifted(): return lax.ppermute(block, axis, route)  35.7 us
    ppermute x8, starting transfers between devices, shifted(): return lax.ppermute(block, axis, route)  28.3 us
    all_to_all x1, blocking collectives, to_tokens(): got = lax.all_to_all(send, 'head', split_axis=0, concat_axis=0, tiled=True)  24 us
    all_to_all x1, starting transfers between devices, to_heads(): got = lax.all_to_all(send, 'head', split_axis=0, concat_axis=0, tiled=True)  11.1 us
    broadcast_in_dim x8, local copies, waits for them, and re-layouts, absorb(): jnp.broadcast_to(key_doc[None, :], (8, row_count))  4.83 us
    broadcast_in_dim x8, local copies, waits for them, and re-layouts, absorb(): jnp.broadcast_to(key_pos[None, :], (8, row_count))  4.78 us
  transfers between devices with their start and end apart: 10, of which 4 were waited for; matrix products, arithmetic and copies ran while one was open for 7% of the time, Pallas kernels for 16%

profile of v4, /device:TPU:5, one launch (start us, length us, event | category | flops | bytes accessed | tf_op | source)
XLA Modules:
  0.0 227.2 jit_solution(9609222597483072756)
XLA Ops:
  9.7 1.7 copy.128
  11.4 11.1 %all-to-all-start = ((bf16[16,6,32,256]{3,2,1,0:T(8,128)(2,1)}), bf16[16,6,32,256]{3,2,1,0:T(8,128)(2,1)S(1)}, u32[]{:S(2)}, u32[]{:S(2)}) async-start(bf16[16,6,32,256]{3,2,1,0:T(8,128)(2,1)} %copy.128), calls=%async_computation | async-start | bytes 3145728 | tf_op jit(solution)/shard_map/all_to_all | solution.py:205
  24.3 36.7 %all-to-all-done = bf16[16,6,32,256]{3,2,1,0:T(8,128)(2,1)S(1)} async-done(((bf16[16,6,32,256]{3,2,1,0:T(8,128)(2,1)}), bf16[16,6,32,256]{3,2,1,0:T(8,128)(2,1)S(1)}, u32[]{:S(2)}, u32[]{:S(2)}) %all-to-all-start) | async-done | bytes 1572896 | tf_op jit(solution)/shard_map/all_to_all | solution.py:205
  63.0 3.2 %collective-permute-start = (bf16[2,512,256]{2,1,0:T(8,128)(2,1)S(1)}, bf16[2,512,256]{2,1,0:T(8,128)(2,1)}, u32[]{:S(2)}, u32[]{:S(2)}) collective-permute-start(bf16[2,512,256]{2,1,0:T(8,128)(2,1)S(1)} %bitcast.121), channel_id=1, source_target_pairs={{0,16},{16,32},{32,48},{48,64},{64,80},{80,96},{96,112},{112,128},... | collective-permute-start | bytes 1572872 | tf_op jit(solution)/shard_map/ppermute | solution.py:15
  66.3 2.8 %collective-permute-start.2 = (bf16[2,512,256]{2,1,0:T(8,128)(2,1)S(1)}, bf16[2,512,256]{2,1,0:T(8,128)(2,1)}, u32[]{:S(2)}, u32[]{:S(2)}) collective-permute-start(bf16[2,512,256]{2,1,0:T(8,128)(2,1)S(1)} %bitcast.122), channel_id=1, source_target_pairs={{0,128},{16,144},{32,160},{48,176},{64,192},{80,208},{96,224},{112... | collective-permute-start | bytes 1572872 | tf_op jit(solution)/shard_map/ppermute | solution.py:15
  69.4 12.1 %collective-permute-done = bf16[2,512,256]{2,1,0:T(8,128)(2,1)} collective-permute-done((bf16[2,512,256]{2,1,0:T(8,128)(2,1)S(1)}, bf16[2,512,256]{2,1,0:T(8,128)(2,1)}, u32[]{:S(2)}, u32[]{:S(2)}) %collective-permute-start) | collective-permute-done | bytes 524320 | tf_op jit(solution)/shard_map/ppermute | solution.py:15
  81.5 1.9 collective-permute-start.1
  83.4 21.3 %collective-permute-done.2 = bf16[2,512,256]{2,1,0:T(8,128)(2,1)} collective-permute-done((bf16[2,512,256]{2,1,0:T(8,128)(2,1)S(1)}, bf16[2,512,256]{2,1,0:T(8,128)(2,1)}, u32[]{:S(2)}, u32[]{:S(2)}) %collective-permute-start.2) | collective-permute-done | bytes 524320 | tf_op jit(solution)/shard_map/ppermute | solution.py:15
  104.7 1.9 collective-permute-start.3
  112.2 4.5 %shard_map.104 = (f32[2,512,128]{2,1,0:T(8,128)S(1)}, f32[2,512,128]{2,1,0:T(8,128)S(1)}, f32[512,256]{1,0:T(8,128)S(1)}) custom-call(s32[512,128]{1,0:T(8,128)S(1)} %broadcast_in_dim.84.q_doc, s32[8,512]{1,0:T(8,128)} %broadcast_in_dim.85.k_doc, s32[512,128]{1,0:T(8,128)S(1)} %broadcast_in_dim.86.q_pos, ...), custom_call_target="tpu_custom_call", output_to_operand_aliasing={{0}: (6, {}), {1}: (7, {}), {2}: (8, {})} | custom-call | flops 268435456 | bytes 3145728 | tf_op jit(solution)/shard_map/pallas_call | solution.py:65
  116.7 5.8 %conditional.8 = ((f32[2,512,128]{2,1,0:T(8,128)S(1)}, f32[2,512,128]{2,1,0:T(8,128)S(1)}, f32[512,256]{1,0:T(8,128)S(1)})) conditional(s32[]{:T(128)} %convert_element_type.140, (f32[2,512,128]{2,1,0:T(8,128)S(1)}, f32[2,512,128]{2,1,0:T(8,128)S(1)}, f32[512,256]{1,0:T(8,128)S(1)}) %shard_map.104, (s32[]{:T(128)}, s32[32]{0:T(128)S(1)}, ...), branch_computations={%region_6.7_spmd, %region_7.9_spmd} | conditional | flops 268485120 | bytes 3192984 | solution.py:125
  118.0 4.5 %branch_1_fun.9 = (f32[2,512,128]{2,1,0:T(8,128)S(1)}, f32[2,512,128]{2,1,0:T(8,128)S(1)}, f32[512,256]{1,0:T(8,128)S(1)}) custom-call(s32[512,128]{1,0:T(8,128)S(1)} %get-tuple-element.227.q_doc, s32[8,512]{1,0:T(8,128)} %broadcast_in_dim.24.k_doc, ...), custom_call_target="tpu_custom_call", output_to_operand_aliasing={{0}: (6, {}), {1}: (7, {}), {2}: (8, {})} | custom-call | flops 268435456 | bytes 3145728 | tf_op jit(solution)/shard_map/cond/branch_1_fun/pallas_call | solution.py:65
  122.6 9.2 %collective-permute-start.4 = (bf16[2,512,256]{2,1,0:T(8,128)(2,1)}, bf16[2,512,256]{2,1,0:T(8,128)(2,1)}, u32[]{:S(2)}, u32[]{:S(2)}) collective-permute-start(bf16[2,512,256]{2,1,0:T(8,128)(2,1)} %collective-permute-done.1), channel_id=1, source_target_pairs={{0,16},{16,32},{32,48},{48,64},{64,80},{80,96},{96,112},{112,128},... | collective-permute-start | bytes 1572872 | tf_op jit(solution)/shard_map/ppermute | solution.py:15
  131.8 1.9 collective-permute-start.5
  136.2 5.8 %conditional.10 = ((f32[2,512,128]{2,1,0:T(8,128)S(1)}, f32[2,512,128]{2,1,0:T(8,128)S(1)}, f32[512,256]{1,0:T(8,128)S(1)})) conditional(s32[]{:T(128)} %convert_element_type.144, (f32[2,512,128]{2,1,0:T(8,128)S(1)}, f32[2,512,128]{2,1,0:T(8,128)S(1)}, f32[512,256]{1,0:T(8,128)S(1)}) %get-tuple-element.455, (s32[]{:T(128)}, s32[32]{0:T(128)S(1)}, ...), branch_computations={%region_14.15_spmd, %region_15.17_spmd} | conditional | flops 268485120 | bytes 3192984 | solution.py:125
  137.6 4.5 %branch_1_fun.11 = (f32[2,512,128]{2,1,0:T(8,128)S(1)}, f32[2,512,128]{2,1,0:T(8,128)S(1)}, f32[512,256]{1,0:T(8,128)S(1)}) custom-call(s32[512,128]{1,0:T(8,128)S(1)} %get-tuple-element.245.q_doc, s32[8,512]{1,0:T(8,128)} %broadcast_in_dim.36.k_doc, ...), custom_call_target="tpu_custom_call", output_to_operand_aliasing={{0}: (6, {}), {1}: (7, {}), {2}: (8, {})} | custom-call | flops 268435456 | bytes 3145728 | tf_op jit(solution)/shard_map/cond/branch_1_fun/pallas_call | solution.py:65
  142.1 5.8 %conditional.11 = ((f32[2,512,128]{2,1,0:T(8,128)S(1)}, f32[2,512,128]{2,1,0:T(8,128)S(1)}, f32[512,256]{1,0:T(8,128)S(1)})) conditional(s32[]{:T(128)} %convert_element_type.142, (f32[2,512,128]{2,1,0:T(8,128)S(1)}, f32[2,512,128]{2,1,0:T(8,128)S(1)}, f32[512,256]{1,0:T(8,128)S(1)}) %get-tuple-element.456, (s32[]{:T(128)}, s32[32]{0:T(128)S(1)}, ...), branch_computations={%region_17.18_spmd, %region_18.20_spmd} | conditional | flops 268485120 | bytes 3192984 | solution.py:125
  143.4 4.5 %branch_1_fun.12 = (f32[2,512,128]{2,1,0:T(8,128)S(1)}, f32[2,512,128]{2,1,0:T(8,128)S(1)}, f32[512,256]{1,0:T(8,128)S(1)}) custom-call(s32[512,128]{1,0:T(8,128)S(1)} %get-tuple-element.254.q_doc, s32[8,512]{1,0:T(8,128)} %broadcast_in_dim.40.k_doc, ...), custom_call_target="tpu_custom_call", output_to_operand_aliasing={{0}: (6, {}), {1}: (7, {}), {2}: (8, {})} | custom-call | flops 268435456 | bytes 3145728 | tf_op jit(solution)/shard_map/cond/branch_1_fun/pallas_call | solution.py:65
  147.9 2.3 collective-permute-done.5
  150.2 2.6 %collective-permute-start.6 = (bf16[2,512,256]{2,1,0:T(8,128)(2,1)}, bf16[2,512,256]{2,1,0:T(8,128)(2,1)}, u32[]{:S(2)}, u32[]{:S(2)}) collective-permute-start(bf16[2,512,256]{2,1,0:T(8,128)(2,1)} %collective-permute-done.4), channel_id=1, source_target_pairs={{0,16},{16,32},{32,48},{48,64},{64,80},{80,96},{96,112},{112,128},... | collective-permute-start | bytes 1572872 | tf_op jit(solution)/shard_map/ppermute | solution.py:15
  152.8 4.8 %collective-permute-start.7 = (bf16[2,512,256]{2,1,0:T(8,128)(2,1)}, bf16[2,512,256]{2,1,0:T(8,128)(2,1)}, u32[]{:S(2)}, u32[]{:S(2)}) collective-permute-start(bf16[2,512,256]{2,1,0:T(8,128)(2,1)} %collective-permute-done.5), channel_id=1, source_target_pairs={{0,496},{16,0},{32,16},{48,32},{64,48},{80,64},{96,80},{112,96},{1... | collective-permute-start | bytes 1572872 | tf_op jit(solution)/shard_map/ppermute | solution.py:15
  162.8 5.8 %conditional.12 = ((f32[2,512,128]{2,1,0:T(8,128)S(1)}, f32[2,512,128]{2,1,0:T(8,128)S(1)}, f32[512,256]{1,0:T(8,128)S(1)})) conditional(s32[]{:T(128)} %convert_element_type.148, (f32[2,512,128]{2,1,0:T(8,128)S(1)}, f32[2,512,128]{2,1,0:T(8,128)S(1)}, f32[512,256]{1,0:T(8,128)S(1)}) %get-tuple-element.457, (s32[]{:T(128)}, s32[32]{0:T(128)S(1)}, ...), branch_computations={%region_22.23_spmd, %region_23.25_spmd} | conditional | flops 268485120 | bytes 3192984 | solution.py:125
  164.1 4.5 %branch_1_fun.13 = (f32[2,512,128]{2,1,0:T(8,128)S(1)}, f32[2,512,128]{2,1,0:T(8,128)S(1)}, f32[512,256]{1,0:T(8,128)S(1)}) custom-call(s32[512,128]{1,0:T(8,128)S(1)} %get-tuple-element.263.q_doc, s32[8,512]{1,0:T(8,128)} %broadcast_in_dim.42.k_doc, ...), custom_call_target="tpu_custom_call", output_to_operand_aliasing={{0}: (6, {}), {1}: (7, {}), {2}: (8, {})} | custom-call | flops 268435456 | bytes 3145728 | tf_op jit(solution)/shard_map/cond/branch_1_fun/pallas_call | solution.py:65
  168.6 5.8 %conditional.13 = ((f32[2,512,128]{2,1,0:T(8,128)S(1)}, f32[2,512,128]{2,1,0:T(8,128)S(1)}, f32[512,256]{1,0:T(8,128)S(1)})) conditional(s32[]{:T(128)} %convert_element_type.146, (f32[2,512,128]{2,1,0:T(8,128)S(1)}, f32[2,512,128]{2,1,0:T(8,128)S(1)}, f32[512,256]{1,0:T(8,128)S(1)}) %get-tuple-element.458, (s32[]{:T(128)}, s32[32]{0:T(128)S(1)}, ...), branch_computations={%region_25.26_spmd, %region_26.28_spmd} | conditional | flops 268485120 | bytes 3192984 | solution.py:125
  170.0 4.5 %branch_1_fun.14 = (f32[2,512,128]{2,1,0:T(8,128)S(1)}, f32[2,512,128]{2,1,0:T(8,128)S(1)}, f32[512,256]{1,0:T(8,128)S(1)}) custom-call(s32[512,128]{1,0:T(8,128)S(1)} %get-tuple-element.272.q_doc, s32[8,512]{1,0:T(8,128)} %broadcast_in_dim.56.k_doc, ...), custom_call_target="tpu_custom_call", output_to_operand_aliasing={{0}: (6, {}), {1}: (7, {}), {2}: (8, {})} | custom-call | flops 268435456 | bytes 3145728 | tf_op jit(solution)/shard_map/cond/branch_1_fun/pallas_call | solution.py:65
  174.5 5.8 %conditional.14 = ((f32[2,512,128]{2,1,0:T(8,128)S(1)}, f32[2,512,128]{2,1,0:T(8,128)S(1)}, f32[512,256]{1,0:T(8,128)S(1)})) conditional(s32[]{:T(128)} %convert_element_type.136, (f32[2,512,128]{2,1,0:T(8,128)S(1)}, f32[2,512,128]{2,1,0:T(8,128)S(1)}, f32[512,256]{1,0:T(8,128)S(1)}) %get-tuple-element.459, (s32[]{:T(128)}, s32[32]{0:T(128)S(1)}, ...), branch_computations={%region_28.29_spmd, %region_29.31_spmd} | conditional | flops 268485120 | bytes 3192984 | solution.py:125
  175.8 4.5 %branch_1_fun.15 = (f32[2,512,128]{2,1,0:T(8,128)S(1)}, f32[2,512,128]{2,1,0:T(8,128)S(1)}, f32[512,256]{1,0:T(8,128)S(1)}) custom-call(s32[512,128]{1,0:T(8,128)S(1)} %get-tuple-element.281.q_doc, s32[8,512]{1,0:T(8,128)} %broadcast_in_dim.58.k_doc, ...), custom_call_target="tpu_custom_call", output_to_operand_aliasing={{0}: (6, {}), {1}: (7, {}), {2}: (8, {})} | custom-call | flops 268435456 | bytes 3145728 | tf_op jit(solution)/shard_map/cond/branch_1_fun/pallas_call | solution.py:65
  180.3 6.0 %conditional.15 = ((f32[2,512,128]{2,1,0:T(8,128)S(1)}, f32[512,256]{1,0:T(8,128)S(1)})) conditional(s32[]{:T(128)} %convert_element_type.134, (f32[2,512,128]{2,1,0:T(8,128)S(1)}, f32[512,256]{1,0:T(8,128)S(1)}) %tuple.82, (s32[]{:T(128)}, s32[32]{0:T(128)S(1)}, s32[512,128]{1,0:T(8,128)S(1)}, s32[512,128]{1,0:T(8,128)S(1)}, ...), branch_computations={%region_31.32_spmd, %region_32.34_spmd} | conditional | flops 268485120 | bytes 3193000 | solution.py:125
  181.7 4.5 %branch_1_fun.16 = (f32[2,512,128]{2,1,0:T(8,128)S(1)}, f32[2,512,128]{2,1,0:T(8,128)S(1)}, f32[512,256]{1,0:T(8,128)S(1)}) custom-call(s32[512,128]{1,0:T(8,128)S(1)} %get-tuple-element.290.q_doc, s32[8,512]{1,0:T(8,128)} %broadcast_in_dim.60.k_doc, ...), custom_call_target="tpu_custom_call", output_to_operand_aliasing={{0}: (6, {}), {1}: (7, {}), {2}: (8, {})} | custom-call | flops 268435456 | bytes 3145728 | tf_op jit(solution)/shard_map/cond/branch_1_fun/pallas_call | solution.py:65
  188.9 1.7 slice.131
  191.0 1.8 fusion
  194.9 24.0 %all_to_all.10 = bf16[16,2,32,256]{3,2,1,0:T(8,128)(2,1)S(1)} all-to-all(bf16[16,2,32,256]{3,2,1,0:T(8,128)(2,1)S(1)} %copy.142), channel_id=1, replica_groups=mesh['ctx'=32,'head'=16] {'head'}, dimensions={0} | all-to-all | bytes 1048576 | tf_op jit(solution)/shard_map/all_to_all | solution.py:212
  (138 shorter events, 24.9 us)
Async XLA Ops:
  7.2 2.2 copy-start.1
  7.2 2.2 copy-start.2
  7.2 2.3 copy-start.3
  7.2 2.3 %copy-start.4 = (bf16[32,4096]{1,0:T(8,128)(2,1)S(1)}, bf16[32,4096]{1,0:T(8,128)(2,1)}, u32[]{:S(2)}) copy-start(bf16[32,4096]{1,0:T(8,128)(2,1)} %param.34) | copy-start | bytes 786436
  11.4 11.2 %copy-start.7 = (f32[2,512]{1,0:T(2,128)S(1)}, f32[2,512]{1,0:T(2,128)}, u32[]{:S(2)}) copy-start(f32[2,512]{1,0:T(2,128)} %param.35) | copy-start | bytes 12292
  11.4 49.6 %all-to-all-start = ((bf16[16,6,32,256]{3,2,1,0:T(8,128)(2,1)}), bf16[16,6,32,256]{3,2,1,0:T(8,128)(2,1)S(1)}, u32[]{:S(2)}, u32[]{:S(2)}) async-start(bf16[16,6,32,256]{3,2,1,0:T(8,128)(2,1)} %copy.128), calls=%async_computation | async-start | bytes 3145728 | tf_op jit(solution)/shard_map/all_to_all | solution.py:205
  22.6 165.3 %all-gather.3.cloned.1.call-start = ((), (), s32[]{:S(2)}) async-start(), calls=%async_computation.2 | async-start | bytes 2433024 | tf_op jit(solution)/shard_map/all_gather | solution.py:167
  61.2 1.7 copy-start.5
  62.0 7.2 %copy-start.8 = (s32[32]{0:T(128)S(1)}, s32[32]{0:T(128)}, u32[]{:S(2)}) copy-start(s32[32]{0:T(128)} %param.37) | copy-start | bytes 388
  63.0 49.2 %copy-start = (bf16[2,16,32,256]{3,2,1,0:T(8,128)(2,1)}, bf16[2,16,32,256]{3,2,1,0:T(8,128)(2,1)S(1)}, u32[]{:S(2)}) copy-start(bf16[2,16,32,256]{3,2,1,0:T(8,128)(2,1)S(1)} %copy.129) | copy-start | bytes 1572868
  63.0 18.4 %collective-permute-start = (bf16[2,512,256]{2,1,0:T(8,128)(2,1)S(1)}, bf16[2,512,256]{2,1,0:T(8,128)(2,1)}, u32[]{:S(2)}, u32[]{:S(2)}) collective-permute-start(bf16[2,512,256]{2,1,0:T(8,128)(2,1)S(1)} %bitcast.121), channel_id=1, source_target_pairs={{0,16},{16,32},{32,48},{48,64},{64,80},{80,96},{96,112},{112,128},... | collective-permute-start | bytes 1572872 | tf_op jit(solution)/shard_map/ppermute | solution.py:15
  66.3 38.5 %collective-permute-start.2 = (bf16[2,512,256]{2,1,0:T(8,128)(2,1)S(1)}, bf16[2,512,256]{2,1,0:T(8,128)(2,1)}, u32[]{:S(2)}, u32[]{:S(2)}) collective-permute-start(bf16[2,512,256]{2,1,0:T(8,128)(2,1)S(1)} %bitcast.122), channel_id=1, source_target_pairs={{0,128},{16,144},{32,160},{48,176},{64,192},{80,208},{96,224},{112... | collective-permute-start | bytes 1572872 | tf_op jit(solution)/shard_map/ppermute | solution.py:15
  81.5 41.1 %collective-permute-start.1 = (bf16[2,512,256]{2,1,0:T(8,128)(2,1)}, bf16[2,512,256]{2,1,0:T(8,128)(2,1)}, u32[]{:S(2)}, u32[]{:S(2)}) collective-permute-start(bf16[2,512,256]{2,1,0:T(8,128)(2,1)} %collective-permute-done), channel_id=1, source_target_pairs={{0,16},{16,32},{32,48},{48,64},{64,80},{80,96},{96,112},{112,128},... | collective-permute-start | bytes 1572872 | tf_op jit(solution)/shard_map/ppermute | solution.py:15
  104.7 17.9 %collective-permute-start.3 = (bf16[2,512,256]{2,1,0:T(8,128)(2,1)}, bf16[2,512,256]{2,1,0:T(8,128)(2,1)}, u32[]{:S(2)}, u32[]{:S(2)}) collective-permute-start(bf16[2,512,256]{2,1,0:T(8,128)(2,1)} %collective-permute-done.2), channel_id=1, source_target_pairs={{0,496},{16,0},{32,16},{48,32},{64,48},{80,64},{96,80},{112,96},{1... | collective-permute-start | bytes 1572872 | tf_op jit(solution)/shard_map/ppermute | solution.py:15
  122.6 25.3 %collective-permute-start.4 = (bf16[2,512,256]{2,1,0:T(8,128)(2,1)}, bf16[2,512,256]{2,1,0:T(8,128)(2,1)}, u32[]{:S(2)}, u32[]{:S(2)}) collective-permute-start(bf16[2,512,256]{2,1,0:T(8,128)(2,1)} %collective-permute-done.1), channel_id=1, source_target_pairs={{0,16},{16,32},{32,48},{48,64},{64,80},{80,96},{96,112},{112,128},... | collective-permute-start | bytes 1572872 | tf_op jit(solution)/shard_map/ppermute | solution.py:15
  131.8 18.4 %collective-permute-start.5 = (bf16[2,512,256]{2,1,0:T(8,128)(2,1)}, bf16[2,512,256]{2,1,0:T(8,128)(2,1)}, u32[]{:S(2)}, u32[]{:S(2)}) collective-permute-start(bf16[2,512,256]{2,1,0:T(8,128)(2,1)} %collective-permute-done.3), channel_id=1, source_target_pairs={{0,496},{16,0},{32,16},{48,32},{64,48},{80,64},{96,80},{112,96},{1... | collective-permute-start | bytes 1572872 | tf_op jit(solution)/shard_map/ppermute | solution.py:15
  150.2 24.3 %collective-permute-start.6 = (bf16[2,512,256]{2,1,0:T(8,128)(2,1)}, bf16[2,512,256]{2,1,0:T(8,128)(2,1)}, u32[]{:S(2)}, u32[]{:S(2)}) collective-permute-start(bf16[2,512,256]{2,1,0:T(8,128)(2,1)} %collective-permute-done.4), channel_id=1, source_target_pairs={{0,16},{16,32},{32,48},{48,64},{64,80},{80,96},{96,112},{112,128},... | collective-permute-start | bytes 1572872 | tf_op jit(solution)/shard_map/ppermute | solution.py:15
  152.8 21.7 %collective-permute-start.7 = (bf16[2,512,256]{2,1,0:T(8,128)(2,1)}, bf16[2,512,256]{2,1,0:T(8,128)(2,1)}, u32[]{:S(2)}, u32[]{:S(2)}) collective-permute-start(bf16[2,512,256]{2,1,0:T(8,128)(2,1)} %collective-permute-done.5), channel_id=1, source_target_pairs={{0,496},{16,0},{32,16},{48,32},{64,48},{80,64},{96,80},{112,96},{1... | collective-permute-start | bytes 1572872 | tf_op jit(solution)/shard_map/ppermute | solution.py:15
  191.0 2.2 copy-start.6
  193.2 1.1 copy-start.9
Sparse Core Ops, SparseCore 0:
  63.1 80.2 all-gather.2

commit v5 on v4

--- a/solution.py
+++ b/solution.py
@@ -132,6 +132,8 @@
     ahead = shifted(kv_pair, "ctx", 1)
     behind = shifted(kv_pair, "ctx", reach) if bwd_offsets else None
     for i in range(max(len(fwd_offsets), len(bwd_offsets))):
+        if i == 0:
+            ahead, running = lax.optimization_barrier((ahead, running))
         ahead_next = shifted(ahead, "ctx", 1) if i + 1 < len(fwd_offsets) else None
         behind_next = shifted(behind, "ctx", -1) if i + 1 < len(bwd_offsets) else None
         if i < len(fwd_offsets):
@@ -227,8 +229,9 @@
         rest[1], rest[2], rest[3], decay_log, norm_gain, row_count, heads_dev, head_width
     )
     soft_out = soft_attention(rest[0], kv_soft, doc_lengths, row_count, heads_dev, head_width)
-    returned = to_tokens([soft_out, light_out], parts)
-    return (returned[0], returned[1])
+    light_back = to_tokens([light_out], parts)[0]
+    soft_back = to_tokens([soft_out], parts)[0]
+    return (soft_back, light_back)
 
 
 def solution(mesh):

time: 228 us -> 226 us (level)
  the two profiles are of different devices: /device:TPU:5 before, /device:TPU:63 now
where the time goes in v5:
time: 226 us; the launch traced here: 225 us
  waiting for transfers between devices  94.9 us (42%)
  starting transfers between devices  43.2 us (19%)
  Pallas kernels  31.5 us (14%)
  between operations  24.8 us (11%)
  local copies, waits for them, and re-layouts  21.7 us (10%)
  other arithmetic  4.96 us (2%)
  matrix products  3.55 us (2%)
    ppermute x8, waiting for transfers between devices, shifted(): return lax.ppermute(block, axis, route)  43.5 us
    all_to_all x1, waiting for transfers between devices, to_heads(): got = lax.all_to_all(send, 'head', split_axis=0, concat_axis=0, tiled=True)  36.7 us
    pallas_call x7, Pallas kernels, online_block(): pl.pallas_call(online_block_kernel, out_shape=(jax.ShapeDtypeStruct(run_m...  31.5 us
    ppermute x8, starting transfers between devices, shifted(): return lax.ppermute(block, axis, route)  21.3 us
    all_to_all x2, waiting for transfers between devices, to_tokens(): got = lax.all_to_all(send, 'head', split_axis=0, concat_axis=0, tiled=True)  14.7 us
    all_to_all x1, starting transfers between devices, to_heads(): got = lax.all_to_all(send, 'head', split_axis=0, concat_axis=0, tiled=True)  11.1 us
    all_to_all x2, starting transfers between devices, to_tokens(): got = lax.all_to_all(send, 'head', split_axis=0, concat_axis=0, tiled=True)  10.7 us
  transfers between devices with their start and end apart: 12, of which 8 were waited for; matrix products, arithmetic and copies ran while one was open for 10% of the time, Pallas kernels for 14%

profile of v5, /device:TPU:63, one launch (start us, length us, event | category | flops | bytes accessed | tf_op | source)
XLA Modules:
  0.0 224.7 jit_solution(14417191809803960229)
XLA Ops:
  11.4 11.1 %all-to-all-start = ((bf16[16,6,32,256]{3,2,1,0:T(8,128)(2,1)}), bf16[16,6,32,256]{3,2,1,0:T(8,128)(2,1)S(1)}, u32[]{:S(2)}, u32[]{:S(2)}) async-start(bf16[16,6,32,256]{3,2,1,0:T(8,128)(2,1)} %copy.130), calls=%async_computation | async-start | bytes 3145728 | tf_op jit(solution)/shard_map/all_to_all | solution.py:207
  24.3 36.7 %all-to-all-done = bf16[16,6,32,256]{3,2,1,0:T(8,128)(2,1)S(1)} async-done(((bf16[16,6,32,256]{3,2,1,0:T(8,128)(2,1)}), bf16[16,6,32,256]{3,2,1,0:T(8,128)(2,1)S(1)}, u32[]{:S(2)}, u32[]{:S(2)}) %all-to-all-start) | async-done | bytes 1572896 | tf_op jit(solution)/shard_map/all_to_all | solution.py:207
  63.3 1.9 collective-permute-start
  65.2 2.5 %collective-permute-start.2 = (bf16[2,512,256]{2,1,0:T(8,128)(2,1)S(1)}, bf16[2,512,256]{2,1,0:T(8,128)(2,1)}, u32[]{:S(2)}, u32[]{:S(2)}) collective-permute-start(bf16[2,512,256]{2,1,0:T(8,128)(2,1)S(1)} %bitcast.127), channel_id=1, source_target_pairs={{0,128},{16,144},{32,160},{48,176},{64,192},{80,208},{96,224},{112... | collective-permute-start | bytes 1572872 | tf_op jit(solution)/shard_map/ppermute | solution.py:15
  70.3 4.5 %shard_map.104 = (f32[2,512,128]{2,1,0:T(8,128)S(1)}, f32[2,512,128]{2,1,0:T(8,128)S(1)}, f32[512,256]{1,0:T(8,128)S(1)}) custom-call(s32[512,128]{1,0:T(8,128)S(1)} %broadcast_in_dim.84.q_doc, s32[8,512]{1,0:T(8,128)} %broadcast_in_dim.85.k_doc, s32[512,128]{1,0:T(8,128)S(1)} %broadcast_in_dim.86.q_pos, ...), custom_call_target="tpu_custom_call", output_to_operand_aliasing={{0}: (6, {}), {1}: (7, {}), {2}: (8, {})} | custom-call | flops 268435456 | bytes 3145728 | tf_op jit(solution)/shard_map/pallas_call | solution.py:65
  74.8 4.8 %collective-permute-done = bf16[2,512,256]{2,1,0:T(8,128)(2,1)} collective-permute-done((bf16[2,512,256]{2,1,0:T(8,128)(2,1)S(1)}, bf16[2,512,256]{2,1,0:T(8,128)(2,1)}, u32[]{:S(2)}, u32[]{:S(2)}) %collective-permute-start) | collective-permute-done | bytes 524320 | tf_op jit(solution)/shard_map/ppermute | solution.py:15
  79.6 4.4 %collective-permute-start.1 = (bf16[2,512,256]{2,1,0:T(8,128)(2,1)}, bf16[2,512,256]{2,1,0:T(8,128)(2,1)}, u32[]{:S(2)}, u32[]{:S(2)}) collective-permute-start(bf16[2,512,256]{2,1,0:T(8,128)(2,1)} %collective-permute-done), channel_id=1, source_target_pairs={{0,16},{16,32},{32,48},{48,64},{64,80},{80,96},{96,112},{112,128},... | collective-permute-start | bytes 1572872 | tf_op jit(solution)/shard_map/ppermute | solution.py:15
  84.0 1.9 collective-permute-start.3
  89.0 5.8 %conditional.8 = ((f32[2,512,128]{2,1,0:T(8,128)S(1)}, f32[2,512,128]{2,1,0:T(8,128)S(1)}, f32[512,256]{1,0:T(8,128)S(1)})) conditional(s32[]{:T(128)} %convert_element_type.140, (f32[2,512,128]{2,1,0:T(8,128)S(1)}, f32[2,512,128]{2,1,0:T(8,128)S(1)}, f32[512,256]{1,0:T(8,128)S(1)}) %shard_map.104, (s32[]{:T(128)}, s32[32]{0:T(128)S(1)}, ...), branch_computations={%region_6.7_spmd, %region_7.9_spmd} | conditional | flops 268485120 | bytes 3192984 | solution.py:125
  90.4 4.5 %branch_1_fun.9 = (f32[2,512,128]{2,1,0:T(8,128)S(1)}, f32[2,512,128]{2,1,0:T(8,128)S(1)}, f32[512,256]{1,0:T(8,128)S(1)}) custom-call(s32[512,128]{1,0:T(8,128)S(1)} %get-tuple-element.227.q_doc, s32[8,512]{1,0:T(8,128)} %broadcast_in_dim.24.k_doc, ...), custom_call_target="tpu_custom_call", output_to_operand_aliasing={{0}: (6, {}), {1}: (7, {}), {2}: (8, {})} | custom-call | flops 268435456 | bytes 3145728 | tf_op jit(solution)/shard_map/cond/branch_1_fun/pallas_call | solution.py:65
  94.9 2.2 collective-permute-done.1
  97.1 24.8 %collective-permute-done.3 = bf16[2,512,256]{2,1,0:T(8,128)(2,1)} collective-permute-done((bf16[2,512,256]{2,1,0:T(8,128)(2,1)}, bf16[2,512,256]{2,1,0:T(8,128)(2,1)}, u32[]{:S(2)}, u32[]{:S(2)}) %collective-permute-start.3) | collective-permute-done | bytes 524320 | tf_op jit(solution)/shard_map/ppermute | solution.py:15
  121.9 3.3 %collective-permute-start.4 = (bf16[2,512,256]{2,1,0:T(8,128)(2,1)}, bf16[2,512,256]{2,1,0:T(8,128)(2,1)}, u32[]{:S(2)}, u32[]{:S(2)}) collective-permute-start(bf16[2,512,256]{2,1,0:T(8,128)(2,1)} %collective-permute-done.1), channel_id=1, source_target_pairs={{0,16},{16,32},{32,48},{48,64},{64,80},{80,96},{96,112},{112,128},... | collective-permute-start | bytes 1572872 | tf_op jit(solution)/shard_map/ppermute | solution.py:15
  125.3 1.9 collective-permute-start.5
  129.8 5.8 %conditional.10 = ((f32[2,512,128]{2,1,0:T(8,128)S(1)}, f32[2,512,128]{2,1,0:T(8,128)S(1)}, f32[512,256]{1,0:T(8,128)S(1)})) conditional(s32[]{:T(128)} %convert_element_type.144, (f32[2,512,128]{2,1,0:T(8,128)S(1)}, f32[2,512,128]{2,1,0:T(8,128)S(1)}, f32[512,256]{1,0:T(8,128)S(1)}) %get-tuple-element.461, (s32[]{:T(128)}, s32[32]{0:T(128)S(1)}, ...), branch_computations={%region_14.15_spmd, %region_15.17_spmd} | conditional | flops 268485120 | bytes 3192984 | solution.py:125
  131.1 4.5 %branch_1_fun.11 = (f32[2,512,128]{2,1,0:T(8,128)S(1)}, f32[2,512,128]{2,1,0:T(8,128)S(1)}, f32[512,256]{1,0:T(8,128)S(1)}) custom-call(s32[512,128]{1,0:T(8,128)S(1)} %get-tuple-element.245.q_doc, s32[8,512]{1,0:T(8,128)} %broadcast_in_dim.36.k_doc, ...), custom_call_target="tpu_custom_call", output_to_operand_aliasing={{0}: (6, {}), {1}: (7, {}), {2}: (8, {})} | custom-call | flops 268435456 | bytes 3145728 | tf_op jit(solution)/shard_map/cond/branch_1_fun/pallas_call | solution.py:65
  135.7 7.3 %collective-permute-done.4 = bf16[2,512,256]{2,1,0:T(8,128)(2,1)} collective-permute-done((bf16[2,512,256]{2,1,0:T(8,128)(2,1)}, bf16[2,512,256]{2,1,0:T(8,128)(2,1)}, u32[]{:S(2)}, u32[]{:S(2)}) %collective-permute-start.4) | collective-permute-done | bytes 524320 | tf_op jit(solution)/shard_map/ppermute | solution.py:15
  143.0 4.3 %collective-permute-done.5 = bf16[2,512,256]{2,1,0:T(8,128)(2,1)} collective-permute-done((bf16[2,512,256]{2,1,0:T(8,128)(2,1)}, bf16[2,512,256]{2,1,0:T(8,128)(2,1)}, u32[]{:S(2)}, u32[]{:S(2)}) %collective-permute-start.5) | collective-permute-done | bytes 524320 | tf_op jit(solution)/shard_map/ppermute | solution.py:15
  147.3 3.0 %collective-permute-start.6 = (bf16[2,512,256]{2,1,0:T(8,128)(2,1)}, bf16[2,512,256]{2,1,0:T(8,128)(2,1)}, u32[]{:S(2)}, u32[]{:S(2)}) collective-permute-start(bf16[2,512,256]{2,1,0:T(8,128)(2,1)} %collective-permute-done.4), channel_id=1, source_target_pairs={{0,16},{16,32},{32,48},{48,64},{64,80},{80,96},{96,112},{112,128},... | collective-permute-start | bytes 1572872 | tf_op jit(solution)/shard_map/ppermute | solution.py:15
  150.3 2.3 %collective-permute-start.7 = (bf16[2,512,256]{2,1,0:T(8,128)(2,1)}, bf16[2,512,256]{2,1,0:T(8,128)(2,1)}, u32[]{:S(2)}, u32[]{:S(2)}) collective-permute-start(bf16[2,512,256]{2,1,0:T(8,128)(2,1)} %collective-permute-done.5), channel_id=1, source_target_pairs={{0,496},{16,0},{32,16},{48,32},{64,48},{80,64},{96,80},{112,96},{1... | collective-permute-start | bytes 1572872 | tf_op jit(solution)/shard_map/ppermute | solution.py:15
  157.8 5.8 %conditional.12 = ((f32[2,512,128]{2,1,0:T(8,128)S(1)}, f32[2,512,128]{2,1,0:T(8,128)S(1)}, f32[512,256]{1,0:T(8,128)S(1)})) conditional(s32[]{:T(128)} %convert_element_type.148, (f32[2,512,128]{2,1,0:T(8,128)S(1)}, f32[2,512,128]{2,1,0:T(8,128)S(1)}, f32[512,256]{1,0:T(8,128)S(1)}) %get-tuple-element.463, (s32[]{:T(128)}, s32[32]{0:T(128)S(1)}, ...), branch_computations={%region_22.23_spmd, %region_23.25_spmd} | conditional | flops 268485120 | bytes 3192984 | solution.py:125
  159.1 4.5 %branch_1_fun.13 = (f32[2,512,128]{2,1,0:T(8,128)S(1)}, f32[2,512,128]{2,1,0:T(8,128)S(1)}, f32[512,256]{1,0:T(8,128)S(1)}) custom-call(s32[512,128]{1,0:T(8,128)S(1)} %get-tuple-element.263.q_doc, s32[8,512]{1,0:T(8,128)} %broadcast_in_dim.42.k_doc, ...), custom_call_target="tpu_custom_call", output_to_operand_aliasing={{0}: (6, {}), {1}: (7, {}), {2}: (8, {})} | custom-call | flops 268435456 | bytes 3145728 | tf_op jit(solution)/shard_map/cond/branch_1_fun/pallas_call | solution.py:65
  163.6 5.8 %conditional.13 = ((f32[2,512,128]{2,1,0:T(8,128)S(1)}, f32[2,512,128]{2,1,0:T(8,128)S(1)}, f32[512,256]{1,0:T(8,128)S(1)})) conditional(s32[]{:T(128)} %convert_element_type.146, (f32[2,512,128]{2,1,0:T(8,128)S(1)}, f32[2,512,128]{2,1,0:T(8,128)S(1)}, f32[512,256]{1,0:T(8,128)S(1)}) %get-tuple-element.464, (s32[]{:T(128)}, s32[32]{0:T(128)S(1)}, ...), branch_computations={%region_25.26_spmd, %region_26.28_spmd} | conditional | flops 268485120 | bytes 3192984 | solution.py:125
  164.9 4.5 %branch_1_fun.14 = (f32[2,512,128]{2,1,0:T(8,128)S(1)}, f32[2,512,128]{2,1,0:T(8,128)S(1)}, f32[512,256]{1,0:T(8,128)S(1)}) custom-call(s32[512,128]{1,0:T(8,128)S(1)} %get-tuple-element.272.q_doc, s32[8,512]{1,0:T(8,128)} %broadcast_in_dim.56.k_doc, ...), custom_call_target="tpu_custom_call", output_to_operand_aliasing={{0}: (6, {}), {1}: (7, {}), {2}: (8, {})} | custom-call | flops 268435456 | bytes 3145728 | tf_op jit(solution)/shard_map/cond/branch_1_fun/pallas_call | solution.py:65
  169.5 5.8 %conditional.14 = ((f32[2,512,128]{2,1,0:T(8,128)S(1)}, f32[2,512,128]{2,1,0:T(8,128)S(1)}, f32[512,256]{1,0:T(8,128)S(1)})) conditional(s32[]{:T(128)} %convert_element_type.136, (f32[2,512,128]{2,1,0:T(8,128)S(1)}, f32[2,512,128]{2,1,0:T(8,128)S(1)}, f32[512,256]{1,0:T(8,128)S(1)}) %get-tuple-element.465, (s32[]{:T(128)}, s32[32]{0:T(128)S(1)}, ...), branch_computations={%region_28.29_spmd, %region_29.31_spmd} | conditional | flops 268485120 | bytes 3192984 | solution.py:125
  170.8 4.5 %branch_1_fun.15 = (f32[2,512,128]{2,1,0:T(8,128)S(1)}, f32[2,512,128]{2,1,0:T(8,128)S(1)}, f32[512,256]{1,0:T(8,128)S(1)}) custom-call(s32[512,128]{1,0:T(8,128)S(1)} %get-tuple-element.281.q_doc, s32[8,512]{1,0:T(8,128)} %broadcast_in_dim.58.k_doc, ...), custom_call_target="tpu_custom_call", output_to_operand_aliasing={{0}: (6, {}), {1}: (7, {}), {2}: (8, {})} | custom-call | flops 268435456 | bytes 3145728 | tf_op jit(solution)/shard_map/cond/branch_1_fun/pallas_call | solution.py:65
  175.3 5.8 %conditional.15 = ((f32[2,512,128]{2,1,0:T(8,128)S(1)}, f32[512,256]{1,0:T(8,128)S(1)})) conditional(s32[]{:T(128)} %convert_element_type.134, (f32[2,512,128]{2,1,0:T(8,128)S(1)}, f32[512,256]{1,0:T(8,128)S(1)}) %tuple.86, (s32[]{:T(128)}, s32[32]{0:T(128)S(1)}, s32[512,128]{1,0:T(8,128)S(1)}, s32[512,128]{1,0:T(8,128)S(1)}, ...), branch_computations={%region_31.32_spmd, %region_32.34_spmd} | conditional | flops 268485120 | bytes 3193000 | solution.py:125
  176.6 4.5 %branch_1_fun.16 = (f32[2,512,128]{2,1,0:T(8,128)S(1)}, f32[2,512,128]{2,1,0:T(8,128)S(1)}, f32[512,256]{1,0:T(8,128)S(1)}) custom-call(s32[512,128]{1,0:T(8,128)S(1)} %get-tuple-element.290.q_doc, s32[8,512]{1,0:T(8,128)} %broadcast_in_dim.60.k_doc, ...), custom_call_target="tpu_custom_call", output_to_operand_aliasing={{0}: (6, {}), {1}: (7, {}), {2}: (8, {})} | custom-call | flops 268435456 | bytes 3145728 | tf_op jit(solution)/shard_map/cond/branch_1_fun/pallas_call | solution.py:65
  183.4 7.3 %all-to-all-start.1 = ((bf16[16,1,32,256]{3,2,1,0:T(8,128)(2,1)}), bf16[16,1,32,256]{3,2,1,0:T(8,128)(2,1)S(1)}, u32[]{:S(2)}, u32[]{:S(2)}) async-start(bf16[16,1,32,256]{3,2,1,0:T(8,128)(2,1)} %fusion.14), calls=%async_computation.1 | async-start | bytes 524288 | tf_op jit(solution)/shard_map/all_to_all | solution.py:214
  198.3 4.0 %all-to-all-done.1 = bf16[16,1,32,256]{3,2,1,0:T(8,128)(2,1)S(1)} async-done(((bf16[16,1,32,256]{3,2,1,0:T(8,128)(2,1)}), bf16[16,1,32,256]{3,2,1,0:T(8,128)(2,1)S(1)}, u32[]{:S(2)}, u32[]{:S(2)}) %all-to-all-start.1) | async-done | bytes 262176 | tf_op jit(solution)/shard_map/all_to_all | solution.py:214
  202.3 3.4 %all-to-all-start.2 = ((bf16[16,1,32,256]{3,2,1,0:T(8,128)(2,1)}), bf16[16,1,32,256]{3,2,1,0:T(8,128)(2,1)S(1)}, u32[]{:S(2)}, u32[]{:S(2)}) async-start(bf16[16,1,32,256]{3,2,1,0:T(8,128)(2,1)} %bitcast.38), calls=%async_computation.2 | async-start | bytes 524288 | tf_op jit(solution)/shard_map/all_to_all | solution.py:214
  206.5 10.7 %all-to-all-done.2 = bf16[16,1,32,256]{3,2,1,0:T(8,128)(2,1)S(1)} async-done(((bf16[16,1,32,256]{3,2,1,0:T(8,128)(2,1)}), bf16[16,1,32,256]{3,2,1,0:T(8,128)(2,1)S(1)}, u32[]{:S(2)}, u32[]{:S(2)}) %all-to-all-start.2) | async-done | bytes 262176 | tf_op jit(solution)/shard_map/all_to_all | solution.py:214
  (132 shorter events, 30.3 us)
Async XLA Ops:
  7.2 2.2 copy-start.1
  7.2 2.2 copy-start.2
  7.2 2.3 %copy-start.3 = (bf16[32,4096]{1,0:T(8,128)(2,1)S(1)}, bf16[32,4096]{1,0:T(8,128)(2,1)}, u32[]{:S(2)}) copy-start(bf16[32,4096]{1,0:T(8,128)(2,1)} %param.33) | copy-start | bytes 786436
  7.2 2.3 %copy-start.4 = (bf16[32,4096]{1,0:T(8,128)(2,1)S(1)}, bf16[32,4096]{1,0:T(8,128)(2,1)}, u32[]{:S(2)}) copy-start(bf16[32,4096]{1,0:T(8,128)(2,1)} %param.34) | copy-start | bytes 786436
  11.4 11.2 %copy-start.7 = (f32[2,512]{1,0:T(2,128)S(1)}, f32[2,512]{1,0:T(2,128)}, u32[]{:S(2)}) copy-start(f32[2,512]{1,0:T(2,128)} %param.35) | copy-start | bytes 12292
  11.4 49.6 %all-to-all-start = ((bf16[16,6,32,256]{3,2,1,0:T(8,128)(2,1)}), bf16[16,6,32,256]{3,2,1,0:T(8,128)(2,1)S(1)}, u32[]{:S(2)}, u32[]{:S(2)}) async-start(bf16[16,6,32,256]{3,2,1,0:T(8,128)(2,1)} %copy.130), calls=%async_computation | async-start | bytes 3145728 | tf_op jit(solution)/shard_map/all_to_all | solution.py:207
  22.5 168.1 %all-gather.3.cloned.1.call-start = ((), (), s32[]{:S(2)}) async-start(), calls=%async_computation.3 | async-start | bytes 2433024 | tf_op jit(solution)/shard_map/all_gather | solution.py:169
  61.1 1.9 copy-start.8
  61.2 2.0 copy-start.5
  63.3 7.0 %copy-start = (bf16[2,16,32,256]{3,2,1,0:T(8,128)(2,1)}, bf16[2,16,32,256]{3,2,1,0:T(8,128)(2,1)S(1)}, u32[]{:S(2)}) copy-start(bf16[2,16,32,256]{3,2,1,0:T(8,128)(2,1)S(1)} %copy.131) | copy-start | bytes 1572868
  63.3 16.3 %collective-permute-start = (bf16[2,512,256]{2,1,0:T(8,128)(2,1)S(1)}, bf16[2,512,256]{2,1,0:T(8,128)(2,1)}, u32[]{:S(2)}, u32[]{:S(2)}) collective-permute-start(bf16[2,512,256]{2,1,0:T(8,128)(2,1)S(1)} %bitcast.126), channel_id=1, source_target_pairs={{0,16},{16,32},{32,48},{48,64},{64,80},{80,96},{96,112},{112,128},... | collective-permute-start | bytes 1572872 | tf_op jit(solution)/shard_map/ppermute | solution.py:15
  65.2 18.8 %collective-permute-start.2 = (bf16[2,512,256]{2,1,0:T(8,128)(2,1)S(1)}, bf16[2,512,256]{2,1,0:T(8,128)(2,1)}, u32[]{:S(2)}, u32[]{:S(2)}) collective-permute-start(bf16[2,512,256]{2,1,0:T(8,128)(2,1)S(1)} %bitcast.127), channel_id=1, source_target_pairs={{0,128},{16,144},{32,160},{48,176},{64,192},{80,208},{96,224},{112... | collective-permute-start | bytes 1572872 | tf_op jit(solution)/shard_map/ppermute | solution.py:15
  79.6 17.5 %collective-permute-start.1 = (bf16[2,512,256]{2,1,0:T(8,128)(2,1)}, bf16[2,512,256]{2,1,0:T(8,128)(2,1)}, u32[]{:S(2)}, u32[]{:S(2)}) collective-permute-start(bf16[2,512,256]{2,1,0:T(8,128)(2,1)} %collective-permute-done), channel_id=1, source_target_pairs={{0,16},{16,32},{32,48},{48,64},{64,80},{80,96},{96,112},{112,128},... | collective-permute-start | bytes 1572872 | tf_op jit(solution)/shard_map/ppermute | solution.py:15
  84.0 37.9 %collective-permute-start.3 = (bf16[2,512,256]{2,1,0:T(8,128)(2,1)}, bf16[2,512,256]{2,1,0:T(8,128)(2,1)}, u32[]{:S(2)}, u32[]{:S(2)}) collective-permute-start(bf16[2,512,256]{2,1,0:T(8,128)(2,1)} %collective-permute-done.2), channel_id=1, source_target_pairs={{0,496},{16,0},{32,16},{48,32},{64,48},{80,64},{96,80},{112,96},{1... | collective-permute-start | bytes 1572872 | tf_op jit(solution)/shard_map/ppermute | solution.py:15
  121.9 21.0 %collective-permute-start.4 = (bf16[2,512,256]{2,1,0:T(8,128)(2,1)}, bf16[2,512,256]{2,1,0:T(8,128)(2,1)}, u32[]{:S(2)}, u32[]{:S(2)}) collective-permute-start(bf16[2,512,256]{2,1,0:T(8,128)(2,1)} %collective-permute-done.1), channel_id=1, source_target_pairs={{0,16},{16,32},{32,48},{48,64},{64,80},{80,96},{96,112},{112,128},... | collective-permute-start | bytes 1572872 | tf_op jit(solution)/shard_map/ppermute | solution.py:15
  125.3 22.0 %collective-permute-start.5 = (bf16[2,512,256]{2,1,0:T(8,128)(2,1)}, bf16[2,512,256]{2,1,0:T(8,128)(2,1)}, u32[]{:S(2)}, u32[]{:S(2)}) collective-permute-start(bf16[2,512,256]{2,1,0:T(8,128)(2,1)} %collective-permute-done.3), channel_id=1, source_target_pairs={{0,496},{16,0},{32,16},{48,32},{64,48},{80,64},{96,80},{112,96},{1... | collective-permute-start | bytes 1572872 | tf_op jit(solution)/shard_map/ppermute | solution.py:15
  147.3 22.2 %collective-permute-start.6 = (bf16[2,512,256]{2,1,0:T(8,128)(2,1)}, bf16[2,512,256]{2,1,0:T(8,128)(2,1)}, u32[]{:S(2)}, u32[]{:S(2)}) collective-permute-start(bf16[2,512,256]{2,1,0:T(8,128)(2,1)} %collective-permute-done.4), channel_id=1, source_target_pairs={{0,16},{16,32},{32,48},{48,64},{64,80},{80,96},{96,112},{112,128},... | collective-permute-start | bytes 1572872 | tf_op jit(solution)/shard_map/ppermute | solution.py:15
  150.3 19.2 %collective-permute-start.7 = (bf16[2,512,256]{2,1,0:T(8,128)(2,1)}, bf16[2,512,256]{2,1,0:T(8,128)(2,1)}, u32[]{:S(2)}, u32[]{:S(2)}) collective-permute-start(bf16[2,512,256]{2,1,0:T(8,128)(2,1)} %collective-permute-done.5), channel_id=1, source_target_pairs={{0,496},{16,0},{32,16},{48,32},{64,48},{80,64},{96,80},{112,96},{1... | collective-permute-start | bytes 1572872 | tf_op jit(solution)/shard_map/ppermute | solution.py:15
  183.4 19.0 %all-to-all-start.1 = ((bf16[16,1,32,256]{3,2,1,0:T(8,128)(2,1)}), bf16[16,1,32,256]{3,2,1,0:T(8,128)(2,1)S(1)}, u32[]{:S(2)}, u32[]{:S(2)}) async-start(bf16[16,1,32,256]{3,2,1,0:T(8,128)(2,1)} %fusion.14), calls=%async_computation.1 | async-start | bytes 524288 | tf_op jit(solution)/shard_map/all_to_all | solution.py:214
  193.9 2.2 copy-start.6
  196.1 1.1 copy-start.9
  202.3 14.8 %all-to-all-start.2 = ((bf16[16,1,32,256]{3,2,1,0:T(8,128)(2,1)}), bf16[16,1,32,256]{3,2,1,0:T(8,128)(2,1)S(1)}, u32[]{:S(2)}, u32[]{:S(2)}) async-start(bf16[16,1,32,256]{3,2,1,0:T(8,128)(2,1)} %bitcast.38), calls=%async_computation.2 | async-start | bytes 524288 | tf_op jit(solution)/shard_map/all_to_all | solution.py:214
Sparse Core Ops, SparseCore 0:
  63.0 80.0 all-gather.2

commit v6 on v4

--- a/solution.py
+++ b/solution.py
@@ -132,6 +132,8 @@
     ahead = shifted(kv_pair, "ctx", 1)
     behind = shifted(kv_pair, "ctx", reach) if bwd_offsets else None
     for i in range(max(len(fwd_offsets), len(bwd_offsets))):
+        if i == 0:
+            ahead, running = lax.optimization_barrier((ahead, running))
         ahead_next = shifted(ahead, "ctx", 1) if i + 1 < len(fwd_offsets) else None
         behind_next = shifted(behind, "ctx", -1) if i + 1 < len(bwd_offsets) else None
         if i < len(fwd_offsets):
@@ -158,28 +160,19 @@
     vals_here = v_rows.reshape(row_count, heads_dev, head_width)
     weighted = (keys_here * jnp.exp(block_end - cumul).T[:, :, None]).astype(jnp.bfloat16)
     update = jnp.einsum("thd,the->hde", weighted, vals_here, preferred_element_type=jnp.float32)
-    end_hi = block_end.astype(jnp.bfloat16)
-    end_lo = (block_end - end_hi.astype(jnp.float32)).astype(jnp.bfloat16)
-    extra = jnp.zeros((heads_dev, 16, head_width), jnp.bfloat16)
-    extra = extra.at[:, 0, :].set(jnp.broadcast_to(end_hi, (heads_dev, head_width)))
-    extra = extra.at[:, 1, :].set(jnp.broadcast_to(end_lo, (heads_dev, head_width)))
-    packed = jnp.concatenate([update.astype(jnp.bfloat16), extra], axis=1)
-    gathered = lax.all_gather(packed, "ctx")
-    ends = gathered[:, :, head_width, 0].astype(jnp.float32) + gathered[
-        :, :, head_width + 1, 0
-    ].astype(jnp.float32)
-    blocks = jnp.arange(size, dtype=jnp.int32)
-    between = (blocks[:, None] < blocks[None, :]) & (blocks[None, :] < own_index)
-    exponent = jnp.einsum(
-        "cb,bh->ch", between.astype(jnp.float32), ends, precision=lax.Precision.HIGHEST
-    )
-    weight = jnp.where((blocks < own_index)[:, None], jnp.exp(exponent), 0.0)
-    entering = jnp.einsum(
-        "ch,chde->hde",
-        weight,
-        gathered[:, :, :head_width, :].astype(jnp.float32),
-        precision=lax.Precision.HIGHEST,
-    )
+    carried = jnp.concatenate(
+        [update, jnp.broadcast_to(block_end[:, :, None], (heads_dev, 8, head_width))], axis=1
+    )
+    shift = 1
+    while shift < size:
+        route = [(i, i + shift) for i in range(size - shift)]
+        earlier = lax.ppermute(carried, "ctx", route)
+        own_log = carried[:, head_width, 0]
+        state = jnp.exp(own_log)[:, None, None] * earlier[:, :head_width] + carried[:, :head_width]
+        logs = earlier[:, head_width:] + carried[:, head_width:]
+        carried = jnp.concatenate([state, logs], axis=1)
+        shift *= 2
+    entering = lax.ppermute(carried, "ctx", [(i, i + 1) for i in range(size - 1)])[:, :head_width]
     state_low = entering.astype(jnp.bfloat16)
     token_ids = jnp.arange(row_count, dtype=jnp.int32)
     causal = token_ids[None, :] <= token_ids[:, None]

time: 228 us -> 235 us (1.031)
  the two profiles are of different devices: /device:TPU:5 before, /device:TPU:61 now
where the time goes in v6:
time: 235 us; the launch traced here: 233 us
  starting transfers between devices  71.4 us (30%)
  waiting for transfers between devices  50.3 us (21%)
  Pallas kernels  40.6 us (17%)
  local copies, waits for them, and re-layouts  23.4 us (10%)
  blocking collectives  21.7 us (9%)
  other arithmetic  10.8 us (5%)
  between operations  10.8 us (5%)
  matrix products  4.29 us (2%)
    pallas_call x9, Pallas kernels, online_block(): pl.pallas_call(online_block_kernel, out_shape=(jax.ShapeDtypeStruct(run_m...  40.6 us
    ppermute x8, starting transfers between devices, shifted(): return lax.ppermute(block, axis, route)  37.9 us
    all_to_all x1, waiting for transfers between devices, to_heads(): got = lax.all_to_all(send, 'head', split_axis=0, concat_axis=0, tiled=True)  34.9 us
    all_to_all x1, blocking collectives, to_tokens(): got = lax.all_to_all(send, 'head', split_axis=0, concat_axis=0, tiled=True)  21.7 us
    ppermute x5, starting transfers between devices, lightning(): earlier = lax.ppermute(carried, 'ctx', route)  16.9 us
    ppermute x5, waiting for transfers between devices, lightning(): earlier = lax.ppermute(carried, 'ctx', route)  11.3 us
    all_to_all x1, starting transfers between devices, to_heads(): got = lax.all_to_all(send, 'head', split_axis=0, concat_axis=0, tiled=True)  11.1 us
    broadcast_in_dim x9, local copies, waits for them, and re-layouts, absorb(): jnp.broadcast_to(key_doc[None, :], (8, row_count))  5.48 us
  transfers between devices with their start and end apart: 15, of which 5 were waited for; matrix products, arithmetic and copies ran while one was open for 11% of the time, Pallas kernels for 14%

profile of v6, /device:TPU:61, one launch (start us, length us, event | category | flops | bytes accessed | tf_op | source)
XLA Modules:
  0.0 233.5 jit_solution(3985449901046203317)
XLA Ops:
  4.9 11.1 %all-to-all-start = ((bf16[16,6,32,256]{3,2,1,0:T(8,128)(2,1)}), bf16[16,6,32,256]{3,2,1,0:T(8,128)(2,1)S(1)}, u32[]{:S(2)}, u32[]{:S(2)}) async-start(bf16[16,6,32,256]{3,2,1,0:T(8,128)(2,1)} %copy.123), calls=%async_computation | async-start | bytes 3145728 | tf_op jit(solution)/shard_map/all_to_all | solution.py:198
  19.5 34.9 %all-to-all-done = bf16[16,6,32,256]{3,2,1,0:T(8,128)(2,1)S(1)} async-done(((bf16[16,6,32,256]{3,2,1,0:T(8,128)(2,1)}), bf16[16,6,32,256]{3,2,1,0:T(8,128)(2,1)S(1)}, u32[]{:S(2)}, u32[]{:S(2)}) %all-to-all-start) | async-done | bytes 1572896 | tf_op jit(solution)/shard_map/all_to_all | solution.py:198
  58.6 5.5 %collective-permute-done.8 = f32[2,136,128]{2,1,0:T(8,128)S(1)} collective-permute-done((f32[2,136,128]{2,1,0:T(8,128)S(1)}, f32[2,136,128]{2,1,0:T(8,128)S(1)}, u32[]{:S(2)}, u32[]{:S(2)}) %collective-permute-start.8) | collective-permute-done | bytes 139296 | tf_op jit(solution)/shard_map/ppermute | solution.py:169
  64.2 3.1 %collective-permute-start.9 = (f32[2,136,128]{2,1,0:T(8,128)S(1)}, f32[2,136,128]{2,1,0:T(8,128)S(1)}, u32[]{:S(2)}, u32[]{:S(2)}) collective-permute-start(f32[2,136,128]{2,1,0:T(8,128)S(1)} %pad_maximum_fusion.2), channel_id=1, source_target_pairs={{0,32},{16,48},{32,64},{48,80},{64,96},{80,112},{96,128},{112,144}... | collective-permute-start | bytes 417800 | tf_op jit(solution)/shard_map/ppermute | solution.py:169
  67.4 5.8 %collective-permute-done.9 = f32[2,136,128]{2,1,0:T(8,128)S(1)} collective-permute-done((f32[2,136,128]{2,1,0:T(8,128)S(1)}, f32[2,136,128]{2,1,0:T(8,128)S(1)}, u32[]{:S(2)}, u32[]{:S(2)}) %collective-permute-start.9) | collective-permute-done | bytes 139296 | tf_op jit(solution)/shard_map/ppermute | solution.py:169
  73.4 7.4 %collective-permute-start.10 = (f32[2,136,128]{2,1,0:T(8,128)S(1)}, f32[2,136,128]{2,1,0:T(8,128)S(1)}, u32[]{:S(2)}, u32[]{:S(2)}) collective-permute-start(f32[2,136,128]{2,1,0:T(8,128)S(1)} %pad_maximum_fusion.3), channel_id=1, source_target_pairs={{0,64},{16,80},{32,96},{48,112},{64,128},{80,144},{96,160},{112,17... | collective-permute-start | bytes 417800 | tf_op jit(solution)/shard_map/ppermute | solution.py:169
  81.0 6.4 %collective-permute-start = (bf16[2,512,256]{2,1,0:T(8,128)(2,1)S(1)}, bf16[2,512,256]{2,1,0:T(8,128)(2,1)}, u32[]{:S(2)}, u32[]{:S(2)}) collective-permute-start(bf16[2,512,256]{2,1,0:T(8,128)(2,1)S(1)} %bitcast.107), channel_id=1, source_target_pairs={{0,16},{16,32},{32,48},{48,64},{64,80},{80,96},{96,112},{112,128},... | collective-permute-start | bytes 1572872 | tf_op jit(solution)/shard_map/ppermute | solution.py:15
  90.4 3.1 %collective-permute-start.11 = (f32[2,136,128]{2,1,0:T(8,128)}, f32[2,136,128]{2,1,0:T(8,128)}, u32[]{:S(2)}, u32[]{:S(2)}) collective-permute-start(f32[2,136,128]{2,1,0:T(8,128)} %pad_maximum_fusion.4), channel_id=1, source_target_pairs={{0,128},{16,144},{32,160},{48,176},{64,192},{80,208},{96,224},{112... | collective-permute-start | bytes 417800 | tf_op jit(solution)/shard_map/ppermute | solution.py:169
  95.1 4.5 %shard_map.104 = (f32[2,512,128]{2,1,0:T(8,128)S(1)}, f32[2,512,128]{2,1,0:T(8,128)S(1)}, f32[512,256]{1,0:T(8,128)S(1)}) custom-call(s32[512,128]{1,0:T(8,128)S(1)} %broadcast_in_dim.72.q_doc, s32[8,512]{1,0:T(8,128)} %broadcast_in_dim.73.k_doc, s32[512,128]{1,0:T(8,128)S(1)} %broadcast_in_dim.74.q_pos, ...), custom_call_target="tpu_custom_call", output_to_operand_aliasing={{0}: (6, {}), {1}: (7, {}), {2}: (8, {})} | custom-call | flops 268435456 | bytes 3145728 | tf_op jit(solution)/shard_map/pallas_call | solution.py:65
  100.6 6.3 %collective-permute-start.1 = (bf16[2,512,256]{2,1,0:T(8,128)(2,1)}, bf16[2,512,256]{2,1,0:T(8,128)(2,1)}, u32[]{:S(2)}, u32[]{:S(2)}) collective-permute-start(bf16[2,512,256]{2,1,0:T(8,128)(2,1)} %collective-permute-done), channel_id=1, source_target_pairs={{0,16},{16,32},{32,48},{48,64},{64,80},{80,96},{96,112},{112,128},... | collective-permute-start | bytes 1572872 | tf_op jit(solution)/shard_map/ppermute | solution.py:15
  124.3 6.4 %conditional.8 = ((f32[2,512,128]{2,1,0:T(8,128)S(1)}, f32[2,512,128]{2,1,0:T(8,128)S(1)}, f32[512,256]{1,0:T(8,128)S(1)})) conditional(s32[]{:T(128)} %convert_element_type.116, (f32[2,512,128]{2,1,0:T(8,128)S(1)}, f32[2,512,128]{2,1,0:T(8,128)S(1)}, f32[512,256]{1,0:T(8,128)S(1)}) %shard_map.104, (s32[]{:T(128)}, s32[32]{0:T(128)}, ...), branch_computations={%region_6.7_spmd, %region_7.9_spmd} | conditional | flops 268485120 | bytes 3192984 | solution.py:125
  126.3 4.5 %branch_1_fun.9 = (f32[2,512,128]{2,1,0:T(8,128)S(1)}, f32[2,512,128]{2,1,0:T(8,128)S(1)}, f32[512,256]{1,0:T(8,128)S(1)}) custom-call(s32[512,128]{1,0:T(8,128)S(1)} %get-tuple-element.203.q_doc, s32[8,512]{1,0:T(8,128)} %broadcast_in_dim.8.k_doc, ...), custom_call_target="tpu_custom_call", output_to_operand_aliasing={{0}: (6, {}), {1}: (7, {}), {2}: (8, {})} | custom-call | flops 268435456 | bytes 3145728 | tf_op jit(solution)/shard_map/cond/branch_1_fun/pallas_call | solution.py:65
  130.8 6.4 %conditional.9 = ((f32[2,512,128]{2,1,0:T(8,128)S(1)}, f32[2,512,128]{2,1,0:T(8,128)S(1)}, f32[512,256]{1,0:T(8,128)S(1)})) conditional(s32[]{:T(128)} %convert_element_type.114, (f32[2,512,128]{2,1,0:T(8,128)S(1)}, f32[2,512,128]{2,1,0:T(8,128)S(1)}, f32[512,256]{1,0:T(8,128)S(1)}) %get-tuple-element.434, (s32[]{:T(128)}, s32[32]{0:T(128)}, ...), branch_computations={%region_9.10_spmd, %region_10.12_spmd} | conditional | flops 268485120 | bytes 3192984 | solution.py:125
  132.7 4.5 %branch_1_fun.10 = (f32[2,512,128]{2,1,0:T(8,128)S(1)}, f32[2,512,128]{2,1,0:T(8,128)S(1)}, f32[512,256]{1,0:T(8,128)S(1)}) custom-call(s32[512,128]{1,0:T(8,128)S(1)} %get-tuple-element.212.q_doc, s32[8,512]{1,0:T(8,128)} %broadcast_in_dim.12.k_doc, ...), custom_call_target="tpu_custom_call", output_to_operand_aliasing={{0}: (6, {}), {1}: (7, {}), {2}: (8, {})} | custom-call | flops 268435456 | bytes 3145728 | tf_op jit(solution)/shard_map/cond/branch_1_fun/pallas_call | solution.py:65
  138.3 3.2 %collective-permute-done.3 = bf16[2,512,256]{2,1,0:T(8,128)(2,1)} collective-permute-done((bf16[2,512,256]{2,1,0:T(8,128)(2,1)}, bf16[2,512,256]{2,1,0:T(8,128)(2,1)}, u32[]{:S(2)}, u32[]{:S(2)}) %collective-permute-start.3) | collective-permute-done | bytes 524320 | tf_op jit(solution)/shard_map/ppermute | solution.py:15
  141.5 14.0 %collective-permute-start.4 = (bf16[2,512,256]{2,1,0:T(8,128)(2,1)}, bf16[2,512,256]{2,1,0:T(8,128)(2,1)}, u32[]{:S(2)}, u32[]{:S(2)}) collective-permute-start(bf16[2,512,256]{2,1,0:T(8,128)(2,1)} %collective-permute-done.1), channel_id=1, source_target_pairs={{0,16},{16,32},{32,48},{48,64},{64,80},{80,96},{96,112},{112,128},... | collective-permute-start | bytes 1572872 | tf_op jit(solution)/shard_map/ppermute | solution.py:15
  158.2 5.5 %collective-permute-start.13 = (bf16[2,136,128]{2,1,0:T(8,128)(2,1)S(1)}, bf16[2,136,128]{2,1,0:T(8,128)(2,1)}, u32[]{:S(2)}, u32[]{:S(2)}) collective-permute-start(bf16[2,136,128]{2,1,0:T(8,128)(2,1)S(1)} %pad_maximum_fusion.6), channel_id=1, source_target_pairs={{0,16},{16,32},{32,48},{48,64},{64,80},{80,96},{96,112},{112,128},... | collective-permute-start | bytes 208904 | tf_op jit(solution)/shard_map/ppermute | solution.py:175
  163.7 2.6 %fusion.1 = f32[512,2,128]{0,2,1:T(8,128)} fusion(f32[2,512]{1,0:T(2,128)} %bitcast.132, pred[512,512]{1,0:T(8,128)(4,1)S(1)} %iota_compare_fusion, bf16[512,2,128]{2,1,0:T(2,128)(2,1)S(1)} %reshape_squeeze.11, bf16[512,2,128]{2,1,0:T(2,128)(2,1)S(1)} %reshape_squeeze.9, bf16[512,2,128]{2,1,0:T(2,128)(2,1)S(1)} %reshape_squeeze.10), kind=kOutput, calls=%fused_computation.26 | convolution fusion | flops 270532608 | bytes 1576960 | tf_op jit(solution)/shard_map/hts,shd->thd/dot_general | solution.py:182
  166.3 5.8 %conditional.10 = ((f32[2,512,128]{2,1,0:T(8,128)S(1)}, f32[2,512,128]{2,1,0:T(8,128)S(1)}, f32[512,256]{1,0:T(8,128)S(1)})) conditional(s32[]{:T(128)} %convert_element_type.120, (f32[2,512,128]{2,1,0:T(8,128)S(1)}, f32[2,512,128]{2,1,0:T(8,128)S(1)}, f32[512,256]{1,0:T(8,128)S(1)}) %get-tuple-element.435, (s32[]{:T(128)}, s32[32]{0:T(128)S(1)}, ...), branch_computations={%region_14.15_spmd, %region_15.17_spmd} | conditional | flops 268485120 | bytes 3192984 | solution.py:125
  167.6 4.5 %branch_1_fun.11 = (f32[2,512,128]{2,1,0:T(8,128)S(1)}, f32[2,512,128]{2,1,0:T(8,128)S(1)}, f32[512,256]{1,0:T(8,128)S(1)}) custom-call(s32[512,128]{1,0:T(8,128)S(1)} %get-tuple-element.221.q_doc, s32[8,512]{1,0:T(8,128)} %broadcast_in_dim.16.k_doc, ...), custom_call_target="tpu_custom_call", output_to_operand_aliasing={{0}: (6, {}), {1}: (7, {}), {2}: (8, {})} | custom-call | flops 268435456 | bytes 3145728 | tf_op jit(solution)/shard_map/cond/branch_1_fun/pallas_call | solution.py:65
  172.2 5.9 %conditional.11 = ((f32[2,512,128]{2,1,0:T(8,128)S(1)}, f32[2,512,128]{2,1,0:T(8,128)S(1)}, f32[512,256]{1,0:T(8,128)S(1)})) conditional(s32[]{:T(128)} %convert_element_type.118, (f32[2,512,128]{2,1,0:T(8,128)S(1)}, f32[2,512,128]{2,1,0:T(8,128)S(1)}, f32[512,256]{1,0:T(8,128)S(1)}) %get-tuple-element.436, (s32[]{:T(128)}, s32[32]{0:T(128)S(1)}, ...), branch_computations={%region_17.18_spmd, %region_18.20_spmd} | conditional | flops 268485120 | bytes 3192984 | solution.py:125
  173.5 4.5 %branch_1_fun.12 = (f32[2,512,128]{2,1,0:T(8,128)S(1)}, f32[2,512,128]{2,1,0:T(8,128)S(1)}, f32[512,256]{1,0:T(8,128)S(1)}) custom-call(s32[512,128]{1,0:T(8,128)S(1)} %get-tuple-element.230.q_doc, s32[8,512]{1,0:T(8,128)} %broadcast_in_dim.20.k_doc, ...), custom_call_target="tpu_custom_call", output_to_operand_aliasing={{0}: (6, {}), {1}: (7, {}), {2}: (8, {})} | custom-call | flops 268435456 | bytes 3145728 | tf_op jit(solution)/shard_map/cond/branch_1_fun/pallas_call | solution.py:65
  180.0 3.4 %collective-permute-start.7 = (bf16[2,512,256]{2,1,0:T(8,128)(2,1)}, bf16[2,512,256]{2,1,0:T(8,128)(2,1)}, u32[]{:S(2)}, u32[]{:S(2)}) collective-permute-start(bf16[2,512,256]{2,1,0:T(8,128)(2,1)} %collective-permute-done.5), channel_id=1, source_target_pairs={{0,496},{16,0},{32,16},{48,32},{64,48},{80,64},{96,80},{112,96},{1... | collective-permute-start | bytes 1572872 | tf_op jit(solution)/shard_map/ppermute | solution.py:15
  185.2 5.9 %conditional.12 = ((f32[2,512,128]{2,1,0:T(8,128)S(1)}, f32[2,512,128]{2,1,0:T(8,128)S(1)}, f32[512,256]{1,0:T(8,128)S(1)})) conditional(s32[]{:T(128)} %convert_element_type.124, (f32[2,512,128]{2,1,0:T(8,128)S(1)}, f32[2,512,128]{2,1,0:T(8,128)S(1)}, f32[512,256]{1,0:T(8,128)S(1)}) %get-tuple-element.437, (s32[]{:T(128)}, s32[32]{0:T(128)S(1)}, ...), branch_computations={%region_22.23_spmd, %region_23.25_spmd} | conditional | flops 268485120 | bytes 3192984 | solution.py:125
  186.6 4.5 %branch_1_fun.13 = (f32[2,512,128]{2,1,0:T(8,128)S(1)}, f32[2,512,128]{2,1,0:T(8,128)S(1)}, f32[512,256]{1,0:T(8,128)S(1)}) custom-call(s32[512,128]{1,0:T(8,128)S(1)} %get-tuple-element.239.q_doc, s32[8,512]{1,0:T(8,128)} %broadcast_in_dim.28.k_doc, ...), custom_call_target="tpu_custom_call", output_to_operand_aliasing={{0}: (6, {}), {1}: (7, {}), {2}: (8, {})} | custom-call | flops 268435456 | bytes 3145728 | tf_op jit(solution)/shard_map/cond/branch_1_fun/pallas_call | solution.py:65
  191.1 5.9 %conditional.13 = ((f32[2,512,128]{2,1,0:T(8,128)S(1)}, f32[2,512,128]{2,1,0:T(8,128)S(1)}, f32[512,256]{1,0:T(8,128)S(1)})) conditional(s32[]{:T(128)} %convert_element_type.122, (f32[2,512,128]{2,1,0:T(8,128)S(1)}, f32[2,512,128]{2,1,0:T(8,128)S(1)}, f32[512,256]{1,0:T(8,128)S(1)}) %get-tuple-element.438, (s32[]{:T(128)}, s32[32]{0:T(128)S(1)}, ...), branch_computations={%region_25.26_spmd, %region_26.28_spmd} | conditional | flops 268485120 | bytes 3192984 | solution.py:125
  192.4 4.5 %branch_1_fun.14 = (f32[2,512,128]{2,1,0:T(8,128)S(1)}, f32[2,512,128]{2,1,0:T(8,128)S(1)}, f32[512,256]{1,0:T(8,128)S(1)}) custom-call(s32[512,128]{1,0:T(8,128)S(1)} %get-tuple-element.248.q_doc, s32[8,512]{1,0:T(8,128)} %broadcast_in_dim.32.k_doc, ...), custom_call_target="tpu_custom_call", output_to_operand_aliasing={{0}: (6, {}), {1}: (7, {}), {2}: (8, {})} | custom-call | flops 268435456 | bytes 3145728 | tf_op jit(solution)/shard_map/cond/branch_1_fun/pallas_call | solution.py:65
  196.9 5.9 %conditional.14 = ((f32[2,512,128]{2,1,0:T(8,128)S(1)}, f32[2,512,128]{2,1,0:T(8,128)S(1)}, f32[512,256]{1,0:T(8,128)S(1)})) conditional(s32[]{:T(128)} %convert_element_type.112, (f32[2,512,128]{2,1,0:T(8,128)S(1)}, f32[2,512,128]{2,1,0:T(8,128)S(1)}, f32[512,256]{1,0:T(8,128)S(1)}) %get-tuple-element.439, (s32[]{:T(128)}, s32[32]{0:T(128)S(1)}, ...), branch_computations={%region_28.29_spmd, %region_29.31_spmd} | conditional | flops 268485120 | bytes 3192984 | solution.py:125
  198.3 4.5 %branch_1_fun.15 = (f32[2,512,128]{2,1,0:T(8,128)S(1)}, f32[2,512,128]{2,1,0:T(8,128)S(1)}, f32[512,256]{1,0:T(8,128)S(1)}) custom-call(s32[512,128]{1,0:T(8,128)S(1)} %get-tuple-element.257.q_doc, s32[8,512]{1,0:T(8,128)} %broadcast_in_dim.36.k_doc, ...), custom_call_target="tpu_custom_call", output_to_operand_aliasing={{0}: (6, {}), {1}: (7, {}), {2}: (8, {})} | custom-call | flops 268435456 | bytes 3145728 | tf_op jit(solution)/shard_map/cond/branch_1_fun/pallas_call | solution.py:65
  202.8 5.9 %conditional.15 = ((f32[2,512,128]{2,1,0:T(8,128)S(1)}, f32[512,256]{1,0:T(8,128)S(1)})) conditional(s32[]{:T(128)} %convert_element_type.110, (f32[2,512,128]{2,1,0:T(8,128)S(1)}, f32[512,256]{1,0:T(8,128)S(1)}) %tuple.78, (s32[]{:T(128)}, s32[32]{0:T(128)S(1)}, s32[512,128]{1,0:T(8,128)S(1)}, s32[512,128]{1,0:T(8,128)S(1)}, ...), branch_computations={%region_31.32_spmd, %region_32.34_spmd} | conditional | flops 268485120 | bytes 3193000 | solution.py:125
  204.1 4.5 %branch_1_fun.16 = (f32[2,512,128]{2,1,0:T(8,128)S(1)}, f32[2,512,128]{2,1,0:T(8,128)S(1)}, f32[512,256]{1,0:T(8,128)S(1)}) custom-call(s32[512,128]{1,0:T(8,128)S(1)} %get-tuple-element.266.q_doc, s32[8,512]{1,0:T(8,128)} %broadcast_in_dim.40.k_doc, ...), custom_call_target="tpu_custom_call", output_to_operand_aliasing={{0}: (6, {}), {1}: (7, {}), {2}: (8, {})} | custom-call | flops 268435456 | bytes 3145728 | tf_op jit(solution)/shard_map/cond/branch_1_fun/pallas_call | solution.py:65
  210.3 21.7 %all_to_all.10 = bf16[16,2,32,256]{3,2,1,0:T(8,128)(2,1)S(1)} all-to-all(bf16[16,2,32,256]{3,2,1,0:T(8,128)(2,1)S(1)} %copy.136), channel_id=1, replica_groups=mesh['ctx'=32,'head'=16] {'head'}, dimensions={0} | all-to-all | bytes 1048576 | tf_op jit(solution)/shard_map/all_to_all | solution.py:205
  (167 shorter events, 47.9 us)
Async XLA Ops:
  0.6 2.2 copy-start.1
  0.6 2.2 copy-start.2
  0.7 2.3 copy-start.3
  0.7 2.3 copy-start.4
  4.9 11.1 %copy-start.11 = (s32[32]{0:T(128)S(1)}, s32[32]{0:T(128)}, u32[]{:S(2)}) copy-start(s32[32]{0:T(128)} %param.33) | copy-start | bytes 388
  4.9 11.4 %copy-start.10 = (f32[2,512]{1,0:T(2,128)S(1)}, f32[2,512]{1,0:T(2,128)}, u32[]{:S(2)}) copy-start(f32[2,512]{1,0:T(2,128)} %param.31) | copy-start | bytes 12292
  4.9 49.6 %all-to-all-start = ((bf16[16,6,32,256]{3,2,1,0:T(8,128)(2,1)}), bf16[16,6,32,256]{3,2,1,0:T(8,128)(2,1)S(1)}, u32[]{:S(2)}, u32[]{:S(2)}) async-start(bf16[16,6,32,256]{3,2,1,0:T(8,128)(2,1)} %copy.123), calls=%async_computation | async-start | bytes 3145728 | tf_op jit(solution)/shard_map/all_to_all | solution.py:198
  17.4 0.6 copy-start.9
  19.5 61.4 %copy-start.5 = (s32[32]{0:T(128)}, s32[32]{0:T(128)S(1)}, u32[]{:S(2)}) copy-start(s32[32]{0:T(128)S(1)} %get-tuple-element.377) | copy-start | bytes 388
  56.5 7.5 %collective-permute-start.8 = (f32[2,136,128]{2,1,0:T(8,128)S(1)}, f32[2,136,128]{2,1,0:T(8,128)S(1)}, u32[]{:S(2)}, u32[]{:S(2)}) collective-permute-start(f32[2,136,128]{2,1,0:T(8,128)S(1)} %pad_maximum_fusion.1), channel_id=1, source_target_pairs={{0,16},{16,32},{32,48},{48,64},{64,80},{80,96},{96,112},{112,128},... | collective-permute-start | bytes 417800 | tf_op jit(solution)/shard_map/ppermute | solution.py:169
  64.2 9.0 %collective-permute-start.9 = (f32[2,136,128]{2,1,0:T(8,128)S(1)}, f32[2,136,128]{2,1,0:T(8,128)S(1)}, u32[]{:S(2)}, u32[]{:S(2)}) collective-permute-start(f32[2,136,128]{2,1,0:T(8,128)S(1)} %pad_maximum_fusion.2), channel_id=1, source_target_pairs={{0,32},{16,48},{32,64},{48,80},{64,96},{80,112},{96,128},{112,144}... | collective-permute-start | bytes 417800 | tf_op jit(solution)/shard_map/ppermute | solution.py:169
  73.4 16.2 %collective-permute-start.10 = (f32[2,136,128]{2,1,0:T(8,128)S(1)}, f32[2,136,128]{2,1,0:T(8,128)S(1)}, u32[]{:S(2)}, u32[]{:S(2)}) collective-permute-start(f32[2,136,128]{2,1,0:T(8,128)S(1)} %pad_maximum_fusion.3), channel_id=1, source_target_pairs={{0,64},{16,80},{32,96},{48,112},{64,128},{80,144},{96,160},{112,17... | collective-permute-start | bytes 417800 | tf_op jit(solution)/shard_map/ppermute | solution.py:169
  81.0 14.1 %copy-start = (bf16[2,16,32,256]{3,2,1,0:T(8,128)(2,1)}, bf16[2,16,32,256]{3,2,1,0:T(8,128)(2,1)S(1)}, u32[]{:S(2)}) copy-start(bf16[2,16,32,256]{3,2,1,0:T(8,128)(2,1)S(1)} %copy.124) | copy-start | bytes 1572868
  81.0 19.6 %collective-permute-start = (bf16[2,512,256]{2,1,0:T(8,128)(2,1)S(1)}, bf16[2,512,256]{2,1,0:T(8,128)(2,1)}, u32[]{:S(2)}, u32[]{:S(2)}) collective-permute-start(bf16[2,512,256]{2,1,0:T(8,128)(2,1)S(1)} %bitcast.107), channel_id=1, source_target_pairs={{0,16},{16,32},{32,48},{48,64},{64,80},{80,96},{96,112},{112,128},... | collective-permute-start | bytes 1572872 | tf_op jit(solution)/shard_map/ppermute | solution.py:15
  87.4 19.6 %collective-permute-start.2 = (bf16[2,512,256]{2,1,0:T(8,128)(2,1)S(1)}, bf16[2,512,256]{2,1,0:T(8,128)(2,1)}, u32[]{:S(2)}, u32[]{:S(2)}) collective-permute-start(bf16[2,512,256]{2,1,0:T(8,128)(2,1)S(1)} %bitcast.108), channel_id=1, source_target_pairs={{0,128},{16,144},{32,160},{48,176},{64,192},{80,208},{96,224},{112... | collective-permute-start | bytes 1572872 | tf_op jit(solution)/shard_map/ppermute | solution.py:15
  90.4 18.5 %collective-permute-start.11 = (f32[2,136,128]{2,1,0:T(8,128)}, f32[2,136,128]{2,1,0:T(8,128)}, u32[]{:S(2)}, u32[]{:S(2)}) collective-permute-start(f32[2,136,128]{2,1,0:T(8,128)} %pad_maximum_fusion.4), channel_id=1, source_target_pairs={{0,128},{16,144},{32,160},{48,176},{64,192},{80,208},{96,224},{112... | collective-permute-start | bytes 417800 | tf_op jit(solution)/shard_map/ppermute | solution.py:169
  93.5 0.9 copy-start.7
  100.6 37.7 %collective-permute-start.1 = (bf16[2,512,256]{2,1,0:T(8,128)(2,1)}, bf16[2,512,256]{2,1,0:T(8,128)(2,1)}, u32[]{:S(2)}, u32[]{:S(2)}) collective-permute-start(bf16[2,512,256]{2,1,0:T(8,128)(2,1)} %collective-permute-done), channel_id=1, source_target_pairs={{0,16},{16,32},{32,48},{48,64},{64,80},{80,96},{96,112},{112,128},... | collective-permute-start | bytes 1572872 | tf_op jit(solution)/shard_map/ppermute | solution.py:15
  107.0 34.5 %collective-permute-start.3 = (bf16[2,512,256]{2,1,0:T(8,128)(2,1)}, bf16[2,512,256]{2,1,0:T(8,128)(2,1)}, u32[]{:S(2)}, u32[]{:S(2)}) collective-permute-start(bf16[2,512,256]{2,1,0:T(8,128)(2,1)} %collective-permute-done.2), channel_id=1, source_target_pairs={{0,496},{16,0},{32,16},{48,32},{64,48},{80,64},{96,80},{112,96},{1... | collective-permute-start | bytes 1572872 | tf_op jit(solution)/shard_map/ppermute | solution.py:15
  111.3 26.1 %collective-permute-start.12 = (f32[2,136,128]{2,1,0:T(8,128)}, f32[2,136,128]{2,1,0:T(8,128)}, u32[]{:S(2)}, u32[]{:S(2)}) collective-permute-start(f32[2,136,128]{2,1,0:T(8,128)} %pad_maximum_fusion.5), channel_id=1, source_target_pairs={{0,256},{16,272},{32,288},{48,304},{64,320},{80,336},{96,352},{112... | collective-permute-start | bytes 417800 | tf_op jit(solution)/shard_map/ppermute | solution.py:169
  141.5 36.5 %collective-permute-start.4 = (bf16[2,512,256]{2,1,0:T(8,128)(2,1)}, bf16[2,512,256]{2,1,0:T(8,128)(2,1)}, u32[]{:S(2)}, u32[]{:S(2)}) collective-permute-start(bf16[2,512,256]{2,1,0:T(8,128)(2,1)} %collective-permute-done.1), channel_id=1, source_target_pairs={{0,16},{16,32},{32,48},{48,64},{64,80},{80,96},{96,112},{112,128},... | collective-permute-start | bytes 1572872 | tf_op jit(solution)/shard_map/ppermute | solution.py:15
  155.6 22.5 %collective-permute-start.5 = (bf16[2,512,256]{2,1,0:T(8,128)(2,1)}, bf16[2,512,256]{2,1,0:T(8,128)(2,1)}, u32[]{:S(2)}, u32[]{:S(2)}) collective-permute-start(bf16[2,512,256]{2,1,0:T(8,128)(2,1)} %collective-permute-done.3), channel_id=1, source_target_pairs={{0,496},{16,0},{32,16},{48,32},{64,48},{80,64},{96,80},{112,96},{1... | collective-permute-start | bytes 1572872 | tf_op jit(solution)/shard_map/ppermute | solution.py:15
  158.2 8.1 %copy-start.6 = (s32[32]{0:T(128)S(1)}, s32[32]{0:T(128)}, u32[]{:S(2)}) copy-start(s32[32]{0:T(128)} %copy-done.5) | copy-start | bytes 388
  158.2 25.1 %collective-permute-start.13 = (bf16[2,136,128]{2,1,0:T(8,128)(2,1)S(1)}, bf16[2,136,128]{2,1,0:T(8,128)(2,1)}, u32[]{:S(2)}, u32[]{:S(2)}) collective-permute-start(bf16[2,136,128]{2,1,0:T(8,128)(2,1)S(1)} %pad_maximum_fusion.6), channel_id=1, source_target_pairs={{0,16},{16,32},{32,48},{48,64},{64,80},{80,96},{96,112},{112,128},... | collective-permute-start | bytes 208904 | tf_op jit(solution)/shard_map/ppermute | solution.py:175
  172.1 11.2 %copy-start.8 = (f32[512,2]{0,1:T(2,128)S(1)}, f32[512,2]{0,1:T(2,128)}, u32[]{:S(2)}) copy-start(f32[512,2]{0,1:T(2,128)} %get-tuple-element.385) | copy-start | bytes 12292
  172.2 12.6 %copy-start.12 = (f32[256]{0:T(256)S(1)}, f32[256]{0:T(256)}, u32[]{:S(2)}) copy-start(f32[256]{0:T(256)} %param.32) | copy-start | bytes 3076
  178.0 18.9 %collective-permute-start.6 = (bf16[2,512,256]{2,1,0:T(8,128)(2,1)}, bf16[2,512,256]{2,1,0:T(8,128)(2,1)}, u32[]{:S(2)}, u32[]{:S(2)}) collective-permute-start(bf16[2,512,256]{2,1,0:T(8,128)(2,1)} %collective-permute-done.4), channel_id=1, source_target_pairs={{0,16},{16,32},{32,48},{48,64},{64,80},{80,96},{96,112},{112,128},... | collective-permute-start | bytes 1572872 | tf_op jit(solution)/shard_map/ppermute | solution.py:15
  180.0 17.0 %collective-permute-start.7 = (bf16[2,512,256]{2,1,0:T(8,128)(2,1)}, bf16[2,512,256]{2,1,0:T(8,128)(2,1)}, u32[]{:S(2)}, u32[]{:S(2)}) collective-permute-start(bf16[2,512,256]{2,1,0:T(8,128)(2,1)} %collective-permute-done.5), channel_id=1, source_target_pairs={{0,496},{16,0},{32,16},{48,32},{64,48},{80,64},{96,80},{112,96},{1... | collective-permute-start | bytes 1572872 | tf_op jit(solution)/shard_map/ppermute | solution.py:15

commit v7 on v4

--- a/solution.py
+++ b/solution.py
@@ -132,6 +132,8 @@
     ahead = shifted(kv_pair, "ctx", 1)
     behind = shifted(kv_pair, "ctx", reach) if bwd_offsets else None
     for i in range(max(len(fwd_offsets), len(bwd_offsets))):
+        if i == 0:
+            ahead, running = lax.optimization_barrier((ahead, running))
         ahead_next = shifted(ahead, "ctx", 1) if i + 1 < len(fwd_offsets) else None
         behind_next = shifted(behind, "ctx", -1) if i + 1 < len(bwd_offsets) else None
         if i < len(fwd_offsets):

time: 228 us -> 219 us (0.961)
  the two profiles are of different devices: /device:TPU:5 before, /device:TPU:11 now
where the time goes in v7:
time: 219 us; the launch traced here: 218 us
  starting transfers between devices  56.5 us (26%)
  waiting for transfers between devices  53.7 us (25%)
  Pallas kernels  31.6 us (14%)
  between operations  24.3 us (11%)
  blocking collectives  22.7 us (10%)
  local copies, waits for them, and re-layouts  20.9 us (10%)
  other arithmetic  4.35 us (2%)
  matrix products  3.55 us (2%)
    ppermute x8, starting transfers between devices, shifted(): return lax.ppermute(block, axis, route)  45.3 us
    all_to_all x1, waiting for transfers between devices, to_heads(): got = lax.all_to_all(send, 'head', split_axis=0, concat_axis=0, tiled=True)  36.7 us
    pallas_call x7, Pallas kernels, online_block(): pl.pallas_call(online_block_kernel, out_shape=(jax.ShapeDtypeStruct(run_m...  31.6 us
    all_to_all x1, blocking collectives, to_tokens(): got = lax.all_to_all(send, 'head', split_axis=0, concat_axis=0, tiled=True)  22.7 us
    ppermute x8, waiting for transfers between devices, shifted(): return lax.ppermute(block, axis, route)  17 us
    all_to_all x1, starting transfers between devices, to_heads(): got = lax.all_to_all(send, 'head', split_axis=0, concat_axis=0, tiled=True)  11.1 us
  transfers between devices with their start and end apart: 10, of which 5 were waited for; matrix products, arithmetic and copies ran while one was open for 7% of the time, Pallas kernels for 14%

profile of v7, /device:TPU:11, one launch (start us, length us, event | category | flops | bytes accessed | tf_op | source)
XLA Modules:
  0.0 217.9 jit_solution(15539916477594693699)
XLA Ops:
  7.2 1.1 copy.151
  9.7 1.7 copy.128
  11.4 11.1 %all-to-all-start = ((bf16[16,6,32,256]{3,2,1,0:T(8,128)(2,1)}), bf16[16,6,32,256]{3,2,1,0:T(8,128)(2,1)S(1)}, u32[]{:S(2)}, u32[]{:S(2)}) async-start(bf16[16,6,32,256]{3,2,1,0:T(8,128)(2,1)} %copy.128), calls=%async_computation | async-start | bytes 3145728 | tf_op jit(solution)/shard_map/all_to_all | solution.py:207
  24.3 36.7 %all-to-all-done = bf16[16,6,32,256]{3,2,1,0:T(8,128)(2,1)S(1)} async-done(((bf16[16,6,32,256]{3,2,1,0:T(8,128)(2,1)}), bf16[16,6,32,256]{3,2,1,0:T(8,128)(2,1)S(1)}, u32[]{:S(2)}, u32[]{:S(2)}) %all-to-all-start) | async-done | bytes 1572896 | tf_op jit(solution)/shard_map/all_to_all | solution.py:207
  63.3 3.2 %collective-permute-start = (bf16[2,512,256]{2,1,0:T(8,128)(2,1)S(1)}, bf16[2,512,256]{2,1,0:T(8,128)(2,1)}, u32[]{:S(2)}, u32[]{:S(2)}) collective-permute-start(bf16[2,512,256]{2,1,0:T(8,128)(2,1)S(1)} %bitcast.121), channel_id=1, source_target_pairs={{0,16},{16,32},{32,48},{48,64},{64,80},{80,96},{96,112},{112,128},... | collective-permute-start | bytes 1572872 | tf_op jit(solution)/shard_map/ppermute | solution.py:15
  66.6 3.1 %collective-permute-start.2 = (bf16[2,512,256]{2,1,0:T(8,128)(2,1)S(1)}, bf16[2,512,256]{2,1,0:T(8,128)(2,1)}, u32[]{:S(2)}, u32[]{:S(2)}) collective-permute-start(bf16[2,512,256]{2,1,0:T(8,128)(2,1)S(1)} %bitcast.122), channel_id=1, source_target_pairs={{0,128},{16,144},{32,160},{48,176},{64,192},{80,208},{96,224},{112... | collective-permute-start | bytes 1572872 | tf_op jit(solution)/shard_map/ppermute | solution.py:15
  72.2 4.5 %shard_map.104 = (f32[2,512,128]{2,1,0:T(8,128)S(1)}, f32[2,512,128]{2,1,0:T(8,128)S(1)}, f32[512,256]{1,0:T(8,128)S(1)}) custom-call(s32[512,128]{1,0:T(8,128)S(1)} %broadcast_in_dim.84.q_doc, s32[8,512]{1,0:T(8,128)} %broadcast_in_dim.85.k_doc, s32[512,128]{1,0:T(8,128)S(1)} %broadcast_in_dim.86.q_pos, ...), custom_call_target="tpu_custom_call", output_to_operand_aliasing={{0}: (6, {}), {1}: (7, {}), {2}: (8, {})} | custom-call | flops 268435456 | bytes 3145728 | tf_op jit(solution)/shard_map/pallas_call | solution.py:65
  76.7 2.9 %collective-permute-done = bf16[2,512,256]{2,1,0:T(8,128)(2,1)} collective-permute-done((bf16[2,512,256]{2,1,0:T(8,128)(2,1)S(1)}, bf16[2,512,256]{2,1,0:T(8,128)(2,1)}, u32[]{:S(2)}, u32[]{:S(2)}) %collective-permute-start) | collective-permute-done | bytes 524320 | tf_op jit(solution)/shard_map/ppermute | solution.py:15
  79.7 3.2 %collective-permute-start.1 = (bf16[2,512,256]{2,1,0:T(8,128)(2,1)}, bf16[2,512,256]{2,1,0:T(8,128)(2,1)}, u32[]{:S(2)}, u32[]{:S(2)}) collective-permute-start(bf16[2,512,256]{2,1,0:T(8,128)(2,1)} %collective-permute-done), channel_id=1, source_target_pairs={{0,16},{16,32},{32,48},{48,64},{64,80},{80,96},{96,112},{112,128},... | collective-permute-start | bytes 1572872 | tf_op jit(solution)/shard_map/ppermute | solution.py:15
  82.9 24.2 %collective-permute-start.3 = (bf16[2,512,256]{2,1,0:T(8,128)(2,1)}, bf16[2,512,256]{2,1,0:T(8,128)(2,1)}, u32[]{:S(2)}, u32[]{:S(2)}) collective-permute-start(bf16[2,512,256]{2,1,0:T(8,128)(2,1)} %collective-permute-done.2), channel_id=1, source_target_pairs={{0,496},{16,0},{32,16},{48,32},{64,48},{80,64},{96,80},{112,96},{1... | collective-permute-start | bytes 1572872 | tf_op jit(solution)/shard_map/ppermute | solution.py:15
  110.0 5.8 %conditional.8 = ((f32[2,512,128]{2,1,0:T(8,128)S(1)}, f32[2,512,128]{2,1,0:T(8,128)S(1)}, f32[512,256]{1,0:T(8,128)S(1)})) conditional(s32[]{:T(128)} %convert_element_type.140, (f32[2,512,128]{2,1,0:T(8,128)S(1)}, f32[2,512,128]{2,1,0:T(8,128)S(1)}, f32[512,256]{1,0:T(8,128)S(1)}) %shard_map.104, (s32[]{:T(128)}, s32[32]{0:T(128)S(1)}, ...), branch_computations={%region_6.7_spmd, %region_7.9_spmd} | conditional | flops 268485120 | bytes 3192984 | solution.py:125
  111.3 4.5 %branch_1_fun.9 = (f32[2,512,128]{2,1,0:T(8,128)S(1)}, f32[2,512,128]{2,1,0:T(8,128)S(1)}, f32[512,256]{1,0:T(8,128)S(1)}) custom-call(s32[512,128]{1,0:T(8,128)S(1)} %get-tuple-element.227.q_doc, s32[8,512]{1,0:T(8,128)} %broadcast_in_dim.24.k_doc, ...), custom_call_target="tpu_custom_call", output_to_operand_aliasing={{0}: (6, {}), {1}: (7, {}), {2}: (8, {})} | custom-call | flops 268435456 | bytes 3145728 | tf_op jit(solution)/shard_map/cond/branch_1_fun/pallas_call | solution.py:65
  115.8 3.8 %collective-permute-done.3 = bf16[2,512,256]{2,1,0:T(8,128)(2,1)} collective-permute-done((bf16[2,512,256]{2,1,0:T(8,128)(2,1)}, bf16[2,512,256]{2,1,0:T(8,128)(2,1)}, u32[]{:S(2)}, u32[]{:S(2)}) %collective-permute-start.3) | collective-permute-done | bytes 524320 | tf_op jit(solution)/shard_map/ppermute | solution.py:15
  119.7 1.9 collective-permute-start.4
  121.6 4.1 %collective-permute-start.5 = (bf16[2,512,256]{2,1,0:T(8,128)(2,1)}, bf16[2,512,256]{2,1,0:T(8,128)(2,1)}, u32[]{:S(2)}, u32[]{:S(2)}) collective-permute-start(bf16[2,512,256]{2,1,0:T(8,128)(2,1)} %collective-permute-done.3), channel_id=1, source_target_pairs={{0,496},{16,0},{32,16},{48,32},{64,48},{80,64},{96,80},{112,96},{1... | collective-permute-start | bytes 1572872 | tf_op jit(solution)/shard_map/ppermute | solution.py:15
  128.0 5.8 %conditional.10 = ((f32[2,512,128]{2,1,0:T(8,128)S(1)}, f32[2,512,128]{2,1,0:T(8,128)S(1)}, f32[512,256]{1,0:T(8,128)S(1)})) conditional(s32[]{:T(128)} %convert_element_type.144, (f32[2,512,128]{2,1,0:T(8,128)S(1)}, f32[2,512,128]{2,1,0:T(8,128)S(1)}, f32[512,256]{1,0:T(8,128)S(1)}) %get-tuple-element.463, (s32[]{:T(128)}, s32[32]{0:T(128)S(1)}, ...), branch_computations={%region_14.15_spmd, %region_15.17_spmd} | conditional | flops 268485120 | bytes 3192984 | solution.py:125
  129.3 4.5 %branch_1_fun.11 = (f32[2,512,128]{2,1,0:T(8,128)S(1)}, f32[2,512,128]{2,1,0:T(8,128)S(1)}, f32[512,256]{1,0:T(8,128)S(1)}) custom-call(s32[512,128]{1,0:T(8,128)S(1)} %get-tuple-element.245.q_doc, s32[8,512]{1,0:T(8,128)} %broadcast_in_dim.36.k_doc, ...), custom_call_target="tpu_custom_call", output_to_operand_aliasing={{0}: (6, {}), {1}: (7, {}), {2}: (8, {})} | custom-call | flops 268435456 | bytes 3145728 | tf_op jit(solution)/shard_map/cond/branch_1_fun/pallas_call | solution.py:65
  133.9 7.0 %collective-permute-done.4 = bf16[2,512,256]{2,1,0:T(8,128)(2,1)} collective-permute-done((bf16[2,512,256]{2,1,0:T(8,128)(2,1)}, bf16[2,512,256]{2,1,0:T(8,128)(2,1)}, u32[]{:S(2)}, u32[]{:S(2)}) %collective-permute-start.4) | collective-permute-done | bytes 524320 | tf_op jit(solution)/shard_map/ppermute | solution.py:15
  140.9 3.2 %collective-permute-done.5 = bf16[2,512,256]{2,1,0:T(8,128)(2,1)} collective-permute-done((bf16[2,512,256]{2,1,0:T(8,128)(2,1)}, bf16[2,512,256]{2,1,0:T(8,128)(2,1)}, u32[]{:S(2)}, u32[]{:S(2)}) %collective-permute-start.5) | collective-permute-done | bytes 524320 | tf_op jit(solution)/shard_map/ppermute | solution.py:15
  144.1 1.9 collective-permute-start.6
  146.0 3.7 %collective-permute-start.7 = (bf16[2,512,256]{2,1,0:T(8,128)(2,1)}, bf16[2,512,256]{2,1,0:T(8,128)(2,1)}, u32[]{:S(2)}, u32[]{:S(2)}) collective-permute-start(bf16[2,512,256]{2,1,0:T(8,128)(2,1)} %collective-permute-done.5), channel_id=1, source_target_pairs={{0,496},{16,0},{32,16},{48,32},{64,48},{80,64},{96,80},{112,96},{1... | collective-permute-start | bytes 1572872 | tf_op jit(solution)/shard_map/ppermute | solution.py:15
  154.8 5.8 %conditional.12 = ((f32[2,512,128]{2,1,0:T(8,128)S(1)}, f32[2,512,128]{2,1,0:T(8,128)S(1)}, f32[512,256]{1,0:T(8,128)S(1)})) conditional(s32[]{:T(128)} %convert_element_type.148, (f32[2,512,128]{2,1,0:T(8,128)S(1)}, f32[2,512,128]{2,1,0:T(8,128)S(1)}, f32[512,256]{1,0:T(8,128)S(1)}) %get-tuple-element.465, (s32[]{:T(128)}, s32[32]{0:T(128)S(1)}, ...), branch_computations={%region_22.23_spmd, %region_23.25_spmd} | conditional | flops 268485120 | bytes 3192984 | solution.py:125
  156.1 4.5 %branch_1_fun.13 = (f32[2,512,128]{2,1,0:T(8,128)S(1)}, f32[2,512,128]{2,1,0:T(8,128)S(1)}, f32[512,256]{1,0:T(8,128)S(1)}) custom-call(s32[512,128]{1,0:T(8,128)S(1)} %get-tuple-element.263.q_doc, s32[8,512]{1,0:T(8,128)} %broadcast_in_dim.42.k_doc, ...), custom_call_target="tpu_custom_call", output_to_operand_aliasing={{0}: (6, {}), {1}: (7, {}), {2}: (8, {})} | custom-call | flops 268435456 | bytes 3145728 | tf_op jit(solution)/shard_map/cond/branch_1_fun/pallas_call | solution.py:65
  160.6 5.8 %conditional.13 = ((f32[2,512,128]{2,1,0:T(8,128)S(1)}, f32[2,512,128]{2,1,0:T(8,128)S(1)}, f32[512,256]{1,0:T(8,128)S(1)})) conditional(s32[]{:T(128)} %convert_element_type.146, (f32[2,512,128]{2,1,0:T(8,128)S(1)}, f32[2,512,128]{2,1,0:T(8,128)S(1)}, f32[512,256]{1,0:T(8,128)S(1)}) %get-tuple-element.466, (s32[]{:T(128)}, s32[32]{0:T(128)S(1)}, ...), branch_computations={%region_25.26_spmd, %region_26.28_spmd} | conditional | flops 268485120 | bytes 3192984 | solution.py:125
  161.9 4.5 %branch_1_fun.14 = (f32[2,512,128]{2,1,0:T(8,128)S(1)}, f32[2,512,128]{2,1,0:T(8,128)S(1)}, f32[512,256]{1,0:T(8,128)S(1)}) custom-call(s32[512,128]{1,0:T(8,128)S(1)} %get-tuple-element.272.q_doc, s32[8,512]{1,0:T(8,128)} %broadcast_in_dim.56.k_doc, ...), custom_call_target="tpu_custom_call", output_to_operand_aliasing={{0}: (6, {}), {1}: (7, {}), {2}: (8, {})} | custom-call | flops 268435456 | bytes 3145728 | tf_op jit(solution)/shard_map/cond/branch_1_fun/pallas_call | solution.py:65
  166.5 5.8 %conditional.14 = ((f32[2,512,128]{2,1,0:T(8,128)S(1)}, f32[2,512,128]{2,1,0:T(8,128)S(1)}, f32[512,256]{1,0:T(8,128)S(1)})) conditional(s32[]{:T(128)} %convert_element_type.136, (f32[2,512,128]{2,1,0:T(8,128)S(1)}, f32[2,512,128]{2,1,0:T(8,128)S(1)}, f32[512,256]{1,0:T(8,128)S(1)}) %get-tuple-element.467, (s32[]{:T(128)}, s32[32]{0:T(128)S(1)}, ...), branch_computations={%region_28.29_spmd, %region_29.31_spmd} | conditional | flops 268485120 | bytes 3192984 | solution.py:125
  167.8 4.5 %branch_1_fun.15 = (f32[2,512,128]{2,1,0:T(8,128)S(1)}, f32[2,512,128]{2,1,0:T(8,128)S(1)}, f32[512,256]{1,0:T(8,128)S(1)}) custom-call(s32[512,128]{1,0:T(8,128)S(1)} %get-tuple-element.281.q_doc, s32[8,512]{1,0:T(8,128)} %broadcast_in_dim.58.k_doc, ...), custom_call_target="tpu_custom_call", output_to_operand_aliasing={{0}: (6, {}), {1}: (7, {}), {2}: (8, {})} | custom-call | flops 268435456 | bytes 3145728 | tf_op jit(solution)/shard_map/cond/branch_1_fun/pallas_call | solution.py:65
  172.3 6.0 %conditional.15 = ((f32[2,512,128]{2,1,0:T(8,128)S(1)}, f32[512,256]{1,0:T(8,128)S(1)})) conditional(s32[]{:T(128)} %convert_element_type.134, (f32[2,512,128]{2,1,0:T(8,128)S(1)}, f32[512,256]{1,0:T(8,128)S(1)}) %tuple.86, (s32[]{:T(128)}, s32[32]{0:T(128)S(1)}, s32[512,128]{1,0:T(8,128)S(1)}, s32[512,128]{1,0:T(8,128)S(1)}, ...), branch_computations={%region_31.32_spmd, %region_32.34_spmd} | conditional | flops 268485120 | bytes 3193000 | solution.py:125
  173.6 4.5 %branch_1_fun.16 = (f32[2,512,128]{2,1,0:T(8,128)S(1)}, f32[2,512,128]{2,1,0:T(8,128)S(1)}, f32[512,256]{1,0:T(8,128)S(1)}) custom-call(s32[512,128]{1,0:T(8,128)S(1)} %get-tuple-element.290.q_doc, s32[8,512]{1,0:T(8,128)} %broadcast_in_dim.60.k_doc, ...), custom_call_target="tpu_custom_call", output_to_operand_aliasing={{0}: (6, {}), {1}: (7, {}), {2}: (8, {})} | custom-call | flops 268435456 | bytes 3145728 | tf_op jit(solution)/shard_map/cond/branch_1_fun/pallas_call | solution.py:65
  180.9 1.7 slice.131
  183.0 1.8 fusion
  186.9 22.7 %all_to_all.10 = bf16[16,2,32,256]{3,2,1,0:T(8,128)(2,1)S(1)} all-to-all(bf16[16,2,32,256]{3,2,1,0:T(8,128)(2,1)S(1)} %copy.142), channel_id=1, replica_groups=mesh['ctx'=32,'head'=16] {'head'}, dimensions={0} | all-to-all | bytes 1048576 | tf_op jit(solution)/shard_map/all_to_all | solution.py:214
  (132 shorter events, 22.5 us)
Async XLA Ops:
  7.2 2.2 copy-start.1
  7.2 2.2 %copy-start.2 = (bf16[32,4096]{1,0:T(8,128)(2,1)S(1)}, bf16[32,4096]{1,0:T(8,128)(2,1)}, u32[]{:S(2)}) copy-start(bf16[32,4096]{1,0:T(8,128)(2,1)} %param.32) | copy-start | bytes 786436
  7.2 2.3 %copy-start.3 = (bf16[32,4096]{1,0:T(8,128)(2,1)S(1)}, bf16[32,4096]{1,0:T(8,128)(2,1)}, u32[]{:S(2)}) copy-start(bf16[32,4096]{1,0:T(8,128)(2,1)} %param.33) | copy-start | bytes 786436
  7.2 2.3 %copy-start.4 = (bf16[32,4096]{1,0:T(8,128)(2,1)S(1)}, bf16[32,4096]{1,0:T(8,128)(2,1)}, u32[]{:S(2)}) copy-start(bf16[32,4096]{1,0:T(8,128)(2,1)} %param.34) | copy-start | bytes 786436
  11.4 11.2 %copy-start.7 = (f32[2,512]{1,0:T(2,128)S(1)}, f32[2,512]{1,0:T(2,128)}, u32[]{:S(2)}) copy-start(f32[2,512]{1,0:T(2,128)} %param.35) | copy-start | bytes 12292
  11.4 49.6 %all-to-all-start = ((bf16[16,6,32,256]{3,2,1,0:T(8,128)(2,1)}), bf16[16,6,32,256]{3,2,1,0:T(8,128)(2,1)S(1)}, u32[]{:S(2)}, u32[]{:S(2)}) async-start(bf16[16,6,32,256]{3,2,1,0:T(8,128)(2,1)} %copy.128), calls=%async_computation | async-start | bytes 3145728 | tf_op jit(solution)/shard_map/all_to_all | solution.py:207
  22.6 157.3 %all-gather.3.cloned.1.call-start = ((), (), s32[]{:S(2)}) async-start(), calls=%async_computation.2 | async-start | bytes 2433024 | tf_op jit(solution)/shard_map/all_gather | solution.py:169
  61.1 1.9 copy-start.8
  61.3 2.0 copy-start.5
  63.3 8.9 %copy-start = (bf16[2,16,32,256]{3,2,1,0:T(8,128)(2,1)}, bf16[2,16,32,256]{3,2,1,0:T(8,128)(2,1)S(1)}, u32[]{:S(2)}) copy-start(bf16[2,16,32,256]{3,2,1,0:T(8,128)(2,1)S(1)} %copy.129) | copy-start | bytes 1572868
  63.3 16.3 %collective-permute-start = (bf16[2,512,256]{2,1,0:T(8,128)(2,1)S(1)}, bf16[2,512,256]{2,1,0:T(8,128)(2,1)}, u32[]{:S(2)}, u32[]{:S(2)}) collective-permute-start(bf16[2,512,256]{2,1,0:T(8,128)(2,1)S(1)} %bitcast.121), channel_id=1, source_target_pairs={{0,16},{16,32},{32,48},{48,64},{64,80},{80,96},{96,112},{112,128},... | collective-permute-start | bytes 1572872 | tf_op jit(solution)/shard_map/ppermute | solution.py:15
  66.6 16.3 %collective-permute-start.2 = (bf16[2,512,256]{2,1,0:T(8,128)(2,1)S(1)}, bf16[2,512,256]{2,1,0:T(8,128)(2,1)}, u32[]{:S(2)}, u32[]{:S(2)}) collective-permute-start(bf16[2,512,256]{2,1,0:T(8,128)(2,1)S(1)} %bitcast.122), channel_id=1, source_target_pairs={{0,128},{16,144},{32,160},{48,176},{64,192},{80,208},{96,224},{112... | collective-permute-start | bytes 1572872 | tf_op jit(solution)/shard_map/ppermute | solution.py:15
  79.7 36.2 %collective-permute-start.1 = (bf16[2,512,256]{2,1,0:T(8,128)(2,1)}, bf16[2,512,256]{2,1,0:T(8,128)(2,1)}, u32[]{:S(2)}, u32[]{:S(2)}) collective-permute-start(bf16[2,512,256]{2,1,0:T(8,128)(2,1)} %collective-permute-done), channel_id=1, source_target_pairs={{0,16},{16,32},{32,48},{48,64},{64,80},{80,96},{96,112},{112,128},... | collective-permute-start | bytes 1572872 | tf_op jit(solution)/shard_map/ppermute | solution.py:15
  82.9 36.8 %collective-permute-start.3 = (bf16[2,512,256]{2,1,0:T(8,128)(2,1)}, bf16[2,512,256]{2,1,0:T(8,128)(2,1)}, u32[]{:S(2)}, u32[]{:S(2)}) collective-permute-start(bf16[2,512,256]{2,1,0:T(8,128)(2,1)} %collective-permute-done.2), channel_id=1, source_target_pairs={{0,496},{16,0},{32,16},{48,32},{64,48},{80,64},{96,80},{112,96},{1... | collective-permute-start | bytes 1572872 | tf_op jit(solution)/shard_map/ppermute | solution.py:15
  119.7 21.2 %collective-permute-start.4 = (bf16[2,512,256]{2,1,0:T(8,128)(2,1)}, bf16[2,512,256]{2,1,0:T(8,128)(2,1)}, u32[]{:S(2)}, u32[]{:S(2)}) collective-permute-start(bf16[2,512,256]{2,1,0:T(8,128)(2,1)} %collective-permute-done.1), channel_id=1, source_target_pairs={{0,16},{16,32},{32,48},{48,64},{64,80},{80,96},{96,112},{112,128},... | collective-permute-start | bytes 1572872 | tf_op jit(solution)/shard_map/ppermute | solution.py:15
  121.6 22.5 %collective-permute-start.5 = (bf16[2,512,256]{2,1,0:T(8,128)(2,1)}, bf16[2,512,256]{2,1,0:T(8,128)(2,1)}, u32[]{:S(2)}, u32[]{:S(2)}) collective-permute-start(bf16[2,512,256]{2,1,0:T(8,128)(2,1)} %collective-permute-done.3), channel_id=1, source_target_pairs={{0,496},{16,0},{32,16},{48,32},{64,48},{80,64},{96,80},{112,96},{1... | collective-permute-start | bytes 1572872 | tf_op jit(solution)/shard_map/ppermute | solution.py:15
  144.1 22.4 %collective-permute-start.6 = (bf16[2,512,256]{2,1,0:T(8,128)(2,1)}, bf16[2,512,256]{2,1,0:T(8,128)(2,1)}, u32[]{:S(2)}, u32[]{:S(2)}) collective-permute-start(bf16[2,512,256]{2,1,0:T(8,128)(2,1)} %collective-permute-done.4), channel_id=1, source_target_pairs={{0,16},{16,32},{32,48},{48,64},{64,80},{80,96},{96,112},{112,128},... | collective-permute-start | bytes 1572872 | tf_op jit(solution)/shard_map/ppermute | solution.py:15
  146.0 20.5 %collective-permute-start.7 = (bf16[2,512,256]{2,1,0:T(8,128)(2,1)}, bf16[2,512,256]{2,1,0:T(8,128)(2,1)}, u32[]{:S(2)}, u32[]{:S(2)}) collective-permute-start(bf16[2,512,256]{2,1,0:T(8,128)(2,1)} %collective-permute-done.5), channel_id=1, source_target_pairs={{0,496},{16,0},{32,16},{48,32},{64,48},{80,64},{96,80},{112,96},{1... | collective-permute-start | bytes 1572872 | tf_op jit(solution)/shard_map/ppermute | solution.py:15
  183.0 2.2 %copy-start.6 = (bf16[512,2,128]{2,1,0:T(2,128)(2,1)S(1)}, bf16[512,2,128]{2,1,0:T(2,128)(2,1)}, u32[]{:S(2)}) copy-start(bf16[512,2,128]{2,1,0:T(2,128)(2,1)} %copy-done.5) | copy-start | bytes 786436
  185.2 1.1 copy-start.9
Sparse Core Ops, SparseCore 0:
  63.0 80.2 all-gather.2

commit v8 on v7

--- a/solution.py
+++ b/solution.py
@@ -103,32 +103,26 @@
         jnp.zeros((row_count, heads_dev * head_width), jnp.float32),
     )
 
-    def absorb(running, block, source):
-        key_pos = source * row_count + jnp.arange(row_count, dtype=jnp.int32)
-        key_doc = doc_index(key_pos, starts)
-        return online_block(
-            running,
-            block,
-            q_rows,
-            query_doc_wide,
-            query_pos_wide,
-            jnp.broadcast_to(key_doc[None, :], (8, row_count)),
-            jnp.broadcast_to(key_pos[None, :], (8, row_count)),
-        )
-
-    def absorb_if_needed(running, block, offset):
-        source = own_index - offset
-        last_doc = doc_index(jnp.full((1,), source * row_count + row_count - 1, jnp.int32), starts)[
-            0
-        ]
-        needed = (source >= 0) & (last_doc == query_doc[0])
-        return lax.cond(
-            needed, lambda r: absorb(r, block, source), lambda r: r, running
-        )
-
     fwd_offsets = list(range(1, forward_steps + 1))
     bwd_offsets = list(range(reach, forward_steps, -1))
-    running = absorb(running, kv_pair, own_index)
+    offsets = [0] + fwd_offsets + bwd_offsets
+    sources = own_index - jnp.array(offsets, jnp.int32)
+    key_pos_all = sources[:, None] * row_count + jnp.arange(row_count, dtype=jnp.int32)[None, :]
+    key_doc_all = doc_index(key_pos_all.reshape(-1), starts).reshape(len(offsets), row_count)
+    needed_all = (sources >= 0) & (key_doc_all[:, -1] == query_doc[0])
+    needed_all = needed_all | (sources == own_index)
+    key_doc_all = jnp.where(needed_all[:, None], key_doc_all, -1)
+    key_doc_tab = jnp.broadcast_to(key_doc_all[:, None, :], (len(offsets), 8, row_count))
+    key_pos_tab = jnp.broadcast_to(key_pos_all[:, None, :], (len(offsets), 8, row_count))
+    slot = {offset: j for j, offset in enumerate(offsets)}
+
+    def absorb(running, block, offset):
+        j = slot[offset]
+        return online_block(
+            running, block, q_rows, query_doc_wide, query_pos_wide, key_doc_tab[j], key_pos_tab[j]
+        )
+
+    running = absorb(running, kv_pair, 0)
     ahead = shifted(kv_pair, "ctx", 1)
     behind = shifted(kv_pair, "ctx", reach) if bwd_offsets else None
     for i in range(max(len(fwd_offsets), len(bwd_offsets))):
@@ -137,9 +131,9 @@
         ahead_next = shifted(ahead, "ctx", 1) if i + 1 < len(fwd_offsets) else None
         behind_next = shifted(behind, "ctx", -1) if i + 1 < len(bwd_offsets) else None
         if i < len(fwd_offsets):
-            running = absorb_if_needed(running, ahead, fwd_offsets[i])
+            running = absorb(running, ahead, fwd_offsets[i])
         if i < len(bwd_offsets):
-            running = absorb_if_needed(running, behind, bwd_offsets[i])
+            running = absorb(running, behind, bwd_offsets[i])
         ahead_next, behind_next, running = lax.optimization_barrier(
             (ahead_next, behind_next, running)
         )

time: 219 us -> 233 us (1.064)
  the two profiles are of different devices: /device:TPU:11 before, /device:TPU:1 now
where the time goes in v8:
time: 233 us; the launch traced here: 232 us
  waiting for transfers between devices  61.8 us (27%)
  Pallas kernels  56 us (24%)
  starting transfers between devices  39.5 us (17%)
  local copies, waits for them, and re-layouts  29.1 us (12%)
  blocking collectives  23.6 us (10%)
  between operations  14.7 us (6%)
  other arithmetic  4.21 us (2%)
  matrix products  3.55 us (2%)
    pallas_call x9, Pallas kernels, online_block(): pl.pallas_call(online_block_kernel, out_shape=(jax.ShapeDtypeStruct(run_m...  56 us
    all_to_all x1, waiting for transfers between devices, to_heads(): got = lax.all_to_all(send, 'head', split_axis=0, concat_axis=0, tiled=True)  36.7 us
    ppermute x8, starting transfers between devices, shifted(): return lax.ppermute(block, axis, route)  27.5 us
    ppermute x8, waiting for transfers between devices, shifted(): return lax.ppermute(block, axis, route)  25 us
    all_to_all x1, blocking collectives, to_tokens(): got = lax.all_to_all(send, 'head', split_axis=0, concat_axis=0, tiled=True)  23.6 us
    all_to_all x1, starting transfers between devices, to_heads(): got = lax.all_to_all(send, 'head', split_axis=0, concat_axis=0, tiled=True)  12 us
    broadcast_in_dim x9, local copies, waits for them, and re-layouts, soft_attention(): jnp.broadcast_to(key_doc_all[:, None, :], (len(offsets), 8, row_count))  5.49 us
    broadcast_in_dim x9, local copies, waits for them, and re-layouts, soft_attention(): jnp.broadcast_to(key_pos_all[:, None, :], (len(offsets), 8, row_count))  5.36 us
  transfers between devices with their start and end apart: 10, of which 4 were waited for; matrix products, arithmetic and copies ran while one was open for 9% of the time, Pallas kernels for 24%

profile of v8, /device:TPU:1, one launch (start us, length us, event | category | flops | bytes accessed | tf_op | source)
XLA Modules:
  0.0 232.5 jit_solution(5457010180856846605)
XLA Ops:
  7.2 1.1 copy.153
  8.3 1.0 copy.154
  9.7 1.7 copy.130
  11.5 12.0 %all-to-all-start = ((bf16[16,6,32,256]{3,2,1,0:T(8,128)(2,1)}), bf16[16,6,32,256]{3,2,1,0:T(8,128)(2,1)S(1)}, u32[]{:S(2)}, u32[]{:S(2)}) async-start(bf16[16,6,32,256]{3,2,1,0:T(8,128)(2,1)} %copy.130), calls=%async_computation | async-start | bytes 3145728 | tf_op jit(solution)/shard_map/all_to_all | solution.py:201
  25.1 36.7 %all-to-all-done = bf16[16,6,32,256]{3,2,1,0:T(8,128)(2,1)S(1)} async-done(((bf16[16,6,32,256]{3,2,1,0:T(8,128)(2,1)}), bf16[16,6,32,256]{3,2,1,0:T(8,128)(2,1)S(1)}, u32[]{:S(2)}, u32[]{:S(2)}) %all-to-all-start) | async-done | bytes 1572896 | tf_op jit(solution)/shard_map/all_to_all | solution.py:201
  65.8 0.9 fusion.21
  66.9 3.2 %collective-permute-start = (bf16[2,512,256]{2,1,0:T(8,128)(2,1)S(1)}, bf16[2,512,256]{2,1,0:T(8,128)(2,1)S(1)}, u32[]{:S(2)}, u32[]{:S(2)}) collective-permute-start(bf16[2,512,256]{2,1,0:T(8,128)(2,1)S(1)} %bitcast.124), channel_id=1, source_target_pairs={{0,16},{16,32},{32,48},{48,64},{64,80},{80,96},{96,112},{112,128},... | collective-permute-start | bytes 1572872 | tf_op jit(solution)/shard_map/ppermute | solution.py:15
  70.1 3.1 %collective-permute-start.2 = (bf16[2,512,256]{2,1,0:T(8,128)(2,1)S(1)}, bf16[2,512,256]{2,1,0:T(8,128)(2,1)S(1)}, u32[]{:S(2)}, u32[]{:S(2)}) collective-permute-start(bf16[2,512,256]{2,1,0:T(8,128)(2,1)S(1)} %bitcast.125), channel_id=1, source_target_pairs={{0,128},{16,144},{32,160},{48,176},{64,192},{80,208},{96,224},{112... | collective-permute-start | bytes 1572872 | tf_op jit(solution)/shard_map/ppermute | solution.py:15
  78.7 6.2 %shard_map.113 = (f32[2,512,128]{2,1,0:T(8,128)}, f32[2,512,128]{2,1,0:T(8,128)}, f32[512,256]{1,0:T(8,128)}) custom-call(s32[512,128]{1,0:T(8,128)} %broadcast_in_dim.163.q_doc, s32[8,512]{1,0:T(8,128)} %broadcast_in_dim.171.k_doc, s32[512,128]{1,0:T(8,128)} %broadcast_in_dim.167.q_pos, ...), custom_call_target="tpu_custom_call", output_to_operand_aliasing={{0}: (6, {}), {1}: (7, {}), {2}: (8, {})} | custom-call | flops 268435456 | bytes 3145728 | tf_op jit(solution)/shard_map/pallas_call | solution.py:65
  84.9 1.6 collective-permute-done.kv_ref
  86.5 1.9 collective-permute-start.1
  88.5 21.5 %collective-permute-done.2.kv_ref = bf16[2,512,256]{2,1,0:T(8,128)(2,1)S(1)} collective-permute-done((bf16[2,512,256]{2,1,0:T(8,128)(2,1)S(1)}, bf16[2,512,256]{2,1,0:T(8,128)(2,1)S(1)}, u32[]{:S(2)}, u32[]{:S(2)}) %collective-permute-start.2) | collective-permute-done | bytes 524320 | tf_op jit(solution)/shard_map/ppermute | solution.py:15
  110.0 1.9 collective-permute-start.3
  113.1 6.2 %shard_map.114 = (f32[2,512,128]{2,1,0:T(8,128)}, f32[2,512,128]{2,1,0:T(8,128)}, f32[512,256]{1,0:T(8,128)}) custom-call(s32[512,128]{1,0:T(8,128)} %broadcast_in_dim.163.q_doc, s32[8,512]{1,0:T(8,128)} %broadcast_in_dim.182.k_doc, s32[512,128]{1,0:T(8,128)} %broadcast_in_dim.167.q_pos, ...), custom_call_target="tpu_custom_call", output_to_operand_aliasing={{0}: (6, {}), {1}: (7, {}), {2}: (8, {})} | custom-call | flops 268435456 | bytes 3145728 | tf_op jit(solution)/shard_map/pallas_call | solution.py:65
  120.5 6.2 %shard_map.115 = (f32[2,512,128]{2,1,0:T(8,128)}, f32[2,512,128]{2,1,0:T(8,128)}, f32[512,256]{1,0:T(8,128)}) custom-call(s32[512,128]{1,0:T(8,128)} %broadcast_in_dim.163.q_doc, s32[8,512]{1,0:T(8,128)} %broadcast_in_dim.178.k_doc, s32[512,128]{1,0:T(8,128)} %broadcast_in_dim.167.q_pos, ...), custom_call_target="tpu_custom_call", output_to_operand_aliasing={{0}: (6, {}), {1}: (7, {}), {2}: (8, {})} | custom-call | flops 268435456 | bytes 3145728 | tf_op jit(solution)/shard_map/pallas_call | solution.py:65
  126.7 1.9 collective-permute-done.3.kv_ref
  128.6 1.9 collective-permute-start.4
  130.5 6.7 %collective-permute-start.5 = (bf16[2,512,256]{2,1,0:T(8,128)(2,1)S(1)}, bf16[2,512,256]{2,1,0:T(8,128)(2,1)S(1)}, u32[]{:S(2)}, u32[]{:S(2)}) collective-permute-start(bf16[2,512,256]{2,1,0:T(8,128)(2,1)S(1)} %collective-permute-done.3.kv_ref), channel_id=1, source_target_pairs={{0,496},{16,0},{32,16},{48,32},{64,48},{80,64},{96,80},{112,96},{1... | collective-permute-start | bytes 1572872 | tf_op jit(solution)/shard_map/ppermute | solution.py:15
  138.4 6.2 %shard_map.116 = (f32[2,512,128]{2,1,0:T(8,128)}, f32[2,512,128]{2,1,0:T(8,128)}, f32[512,256]{1,0:T(8,128)}) custom-call(s32[512,128]{1,0:T(8,128)} %broadcast_in_dim.163.q_doc, s32[8,512]{1,0:T(8,128)} %broadcast_in_dim.190.k_doc, s32[512,128]{1,0:T(8,128)} %broadcast_in_dim.167.q_pos, ...), custom_call_target="tpu_custom_call", output_to_operand_aliasing={{0}: (6, {}), {1}: (7, {}), {2}: (8, {})} | custom-call | flops 268435456 | bytes 3145728 | tf_op jit(solution)/shard_map/pallas_call | solution.py:65
  145.9 6.2 %shard_map.117 = (f32[2,512,128]{2,1,0:T(8,128)}, f32[2,512,128]{2,1,0:T(8,128)}, f32[512,256]{1,0:T(8,128)}) custom-call(s32[512,128]{1,0:T(8,128)} %broadcast_in_dim.163.q_doc, s32[8,512]{1,0:T(8,128)} %broadcast_in_dim.186.k_doc, s32[512,128]{1,0:T(8,128)} %broadcast_in_dim.167.q_pos, ...), custom_call_target="tpu_custom_call", output_to_operand_aliasing={{0}: (6, {}), {1}: (7, {}), {2}: (8, {})} | custom-call | flops 268435456 | bytes 3145728 | tf_op jit(solution)/shard_map/pallas_call | solution.py:65
  152.1 1.9 collective-permute-start.6
  154.0 6.9 %collective-permute-start.7 = (bf16[2,512,256]{2,1,0:T(8,128)(2,1)S(1)}, bf16[2,512,256]{2,1,0:T(8,128)(2,1)S(1)}, u32[]{:S(2)}, u32[]{:S(2)}) collective-permute-start(bf16[2,512,256]{2,1,0:T(8,128)(2,1)S(1)} %collective-permute-done.5.kv_ref), channel_id=1, source_target_pairs={{0,496},{16,0},{32,16},{48,32},{64,48},{80,64},{96,80},{112,96},{1... | collective-permute-start | bytes 1572872 | tf_op jit(solution)/shard_map/ppermute | solution.py:15
  162.3 6.2 %shard_map.118 = (f32[2,512,128]{2,1,0:T(8,128)}, f32[2,512,128]{2,1,0:T(8,128)}, f32[512,256]{1,0:T(8,128)}) custom-call(s32[512,128]{1,0:T(8,128)} %broadcast_in_dim.163.q_doc, s32[8,512]{1,0:T(8,128)} %broadcast_in_dim.198.k_doc, s32[512,128]{1,0:T(8,128)} %broadcast_in_dim.167.q_pos, ...), custom_call_target="tpu_custom_call", output_to_operand_aliasing={{0}: (6, {}), {1}: (7, {}), {2}: (8, {})} | custom-call | flops 268435456 | bytes 3145728 | tf_op jit(solution)/shard_map/pallas_call | solution.py:65
  169.7 6.2 %shard_map.119 = (f32[2,512,128]{2,1,0:T(8,128)}, f32[2,512,128]{2,1,0:T(8,128)}, f32[512,256]{1,0:T(8,128)}) custom-call(s32[512,128]{1,0:T(8,128)} %broadcast_in_dim.163.q_doc, s32[8,512]{1,0:T(8,128)} %broadcast_in_dim.194.k_doc, s32[512,128]{1,0:T(8,128)} %broadcast_in_dim.167.q_pos, ...), custom_call_target="tpu_custom_call", output_to_operand_aliasing={{0}: (6, {}), {1}: (7, {}), {2}: (8, {})} | custom-call | flops 268435456 | bytes 3145728 | tf_op jit(solution)/shard_map/pallas_call | solution.py:65
  177.2 6.2 %shard_map.120 = (f32[2,512,128]{2,1,0:T(8,128)}, f32[2,512,128]{2,1,0:T(8,128)}, f32[512,256]{1,0:T(8,128)}) custom-call(s32[512,128]{1,0:T(8,128)} %broadcast_in_dim.163.q_doc, s32[8,512]{1,0:T(8,128)} %broadcast_in_dim.202.k_doc, s32[512,128]{1,0:T(8,128)} %broadcast_in_dim.167.q_pos, ...), custom_call_target="tpu_custom_call", output_to_operand_aliasing={{0}: (6, {}), {1}: (7, {}), {2}: (8, {})} | custom-call | flops 268435456 | bytes 3145728 | tf_op jit(solution)/shard_map/pallas_call | solution.py:65
  184.6 6.2 %shard_map.121 = (f32[2,512,128]{2,1,0:T(8,128)}, f32[2,512,128]{2,1,0:T(8,128)}, f32[512,256]{1,0:T(8,128)}) custom-call(s32[512,128]{1,0:T(8,128)} %broadcast_in_dim.163.q_doc, s32[8,512]{1,0:T(8,128)} %broadcast_in_dim.166.k_doc, s32[512,128]{1,0:T(8,128)} %broadcast_in_dim.167.q_pos, ...), custom_call_target="tpu_custom_call", output_to_operand_aliasing={{0}: (6, {}), {1}: (7, {}), {2}: (8, {})} | custom-call | flops 268435456 | bytes 3145728 | tf_op jit(solution)/shard_map/pallas_call | solution.py:65
  190.9 1.3 slice_reduce_fusion
  193.5 1.0 fusion.28
  194.6 1.7 slice.255
  196.6 1.8 fusion
  198.9 1.1 multiply_reduce_fusion
  200.5 23.6 %all_to_all.10 = bf16[16,2,32,256]{3,2,1,0:T(8,128)(2,1)S(1)} all-to-all(bf16[16,2,32,256]{3,2,1,0:T(8,128)(2,1)S(1)} %copy.144), channel_id=1, replica_groups=mesh['ctx'=32,'head'=16] {'head'}, dimensions={0} | all-to-all | bytes 1048576 | tf_op jit(solution)/shard_map/all_to_all | solution.py:208
  (145 shorter events, 25.3 us)
Async XLA Ops:
  7.2 2.2 copy-start.10
  7.2 2.2 copy-start.11
  7.2 2.3 copy-start.12
  7.2 2.3 %copy-start.13 = (bf16[32,4096]{1,0:T(8,128)(2,1)S(1)}, bf16[32,4096]{1,0:T(8,128)(2,1)}, u32[]{:S(2)}) copy-start(bf16[32,4096]{1,0:T(8,128)(2,1)} %param.19) | copy-start | bytes 786436
  11.5 12.0 %copy-start.16 = (f32[2,512]{1,0:T(2,128)S(1)}, f32[2,512]{1,0:T(2,128)}, u32[]{:S(2)}) copy-start(f32[2,512]{1,0:T(2,128)} %param.20) | copy-start | bytes 12292
  11.5 50.4 %all-to-all-start = ((bf16[16,6,32,256]{3,2,1,0:T(8,128)(2,1)}), bf16[16,6,32,256]{3,2,1,0:T(8,128)(2,1)S(1)}, u32[]{:S(2)}, u32[]{:S(2)}) async-start(bf16[16,6,32,256]{3,2,1,0:T(8,128)(2,1)} %copy.130), calls=%async_computation | async-start | bytes 3145728 | tf_op jit(solution)/shard_map/all_to_all | solution.py:201
  23.4 170.1 %all-gather.3.cloned.1.call-start = ((), (), s32[]{:S(2)}) async-start(), calls=%async_computation.2 | async-start | bytes 2433024 | tf_op jit(solution)/shard_map/all_gather | solution.py:163
  62.6 1.8 copy-start.19
  62.7 1.9 copy-start.18
  62.8 4.1 %copy-start.14 = (bf16[512,2,128]{2,1,0:T(2,128)(2,1)}, bf16[512,2,128]{2,1,0:T(2,128)(2,1)S(1)}, u32[]{:S(2)}) copy-start(bf16[512,2,128]{2,1,0:T(2,128)(2,1)S(1)} %reshape_squeeze.9) | copy-start | bytes 786436
  66.9 11.8 %copy-start.1 = (bf16[2,16,32,256]{3,2,1,0:T(8,128)(2,1)}, bf16[2,16,32,256]{3,2,1,0:T(8,128)(2,1)S(1)}, u32[]{:S(2)}) copy-start(bf16[2,16,32,256]{3,2,1,0:T(8,128)(2,1)S(1)} %copy.131) | copy-start | bytes 1572868
  66.9 19.7 %collective-permute-start = (bf16[2,512,256]{2,1,0:T(8,128)(2,1)S(1)}, bf16[2,512,256]{2,1,0:T(8,128)(2,1)S(1)}, u32[]{:S(2)}, u32[]{:S(2)}) collective-permute-start(bf16[2,512,256]{2,1,0:T(8,128)(2,1)S(1)} %bitcast.124), channel_id=1, source_target_pairs={{0,16},{16,32},{32,48},{48,64},{64,80},{80,96},{96,112},{112,128},... | collective-permute-start | bytes 1572872 | tf_op jit(solution)/shard_map/ppermute | solution.py:15
  70.1 39.9 %collective-permute-start.2 = (bf16[2,512,256]{2,1,0:T(8,128)(2,1)S(1)}, bf16[2,512,256]{2,1,0:T(8,128)(2,1)S(1)}, u32[]{:S(2)}, u32[]{:S(2)}) collective-permute-start(bf16[2,512,256]{2,1,0:T(8,128)(2,1)S(1)} %bitcast.125), channel_id=1, source_target_pairs={{0,128},{16,144},{32,160},{48,176},{64,192},{80,208},{96,224},{112... | collective-permute-start | bytes 1572872 | tf_op jit(solution)/shard_map/ppermute | solution.py:15
  86.5 26.6 %copy-start.2 = (bf16[2,512,256]{2,1,0:T(8,128)(2,1)}, bf16[2,512,256]{2,1,0:T(8,128)(2,1)S(1)}, u32[]{:S(2)}) copy-start(bf16[2,512,256]{2,1,0:T(8,128)(2,1)S(1)} %collective-permute-done.kv_ref) | copy-start | bytes 1572868
  86.5 40.2 %collective-permute-start.1 = (bf16[2,512,256]{2,1,0:T(8,128)(2,1)S(1)}, bf16[2,512,256]{2,1,0:T(8,128)(2,1)S(1)}, u32[]{:S(2)}, u32[]{:S(2)}) collective-permute-start(bf16[2,512,256]{2,1,0:T(8,128)(2,1)S(1)} %collective-permute-done.kv_ref), channel_id=1, source_target_pairs={{0,16},{16,32},{32,48},{48,64},{64,80},{80,96},{96,112},{112,128},... | collective-permute-start | bytes 1572872 | tf_op jit(solution)/shard_map/ppermute | solution.py:15
  110.0 10.5 %copy-start.3 = (bf16[2,512,256]{2,1,0:T(8,128)(2,1)}, bf16[2,512,256]{2,1,0:T(8,128)(2,1)S(1)}, u32[]{:S(2)}) copy-start(bf16[2,512,256]{2,1,0:T(8,128)(2,1)S(1)} %collective-permute-done.2.kv_ref) | copy-start | bytes 1572868
  110.0 18.7 %collective-permute-start.3 = (bf16[2,512,256]{2,1,0:T(8,128)(2,1)S(1)}, bf16[2,512,256]{2,1,0:T(8,128)(2,1)S(1)}, u32[]{:S(2)}, u32[]{:S(2)}) collective-permute-start(bf16[2,512,256]{2,1,0:T(8,128)(2,1)S(1)} %collective-permute-done.2.kv_ref), channel_id=1, source_target_pairs={{0,496},{16,0},{32,16},{48,32},{64,48},{80,64},{96,80},{112,96},{1... | collective-permute-start | bytes 1572872 | tf_op jit(solution)/shard_map/ppermute | solution.py:15
  126.7 11.7 %copy-start.6 = (bf16[2,512,256]{2,1,0:T(8,128)(2,1)}, bf16[2,512,256]{2,1,0:T(8,128)(2,1)S(1)}, u32[]{:S(2)}) copy-start(bf16[2,512,256]{2,1,0:T(8,128)(2,1)S(1)} %collective-permute-done.1.kv_ref) | copy-start | bytes 1572868
  128.6 17.3 %copy-start.7 = (bf16[2,512,256]{2,1,0:T(8,128)(2,1)}, bf16[2,512,256]{2,1,0:T(8,128)(2,1)S(1)}, u32[]{:S(2)}) copy-start(bf16[2,512,256]{2,1,0:T(8,128)(2,1)S(1)} %collective-permute-done.3.kv_ref) | copy-start | bytes 1572868
  128.6 23.5 %collective-permute-start.4 = (bf16[2,512,256]{2,1,0:T(8,128)(2,1)S(1)}, bf16[2,512,256]{2,1,0:T(8,128)(2,1)S(1)}, u32[]{:S(2)}, u32[]{:S(2)}) collective-permute-start(bf16[2,512,256]{2,1,0:T(8,128)(2,1)S(1)} %collective-permute-done.1.kv_ref), channel_id=1, source_target_pairs={{0,16},{16,32},{32,48},{48,64},{64,80},{80,96},{96,112},{112,128},... | collective-permute-start | bytes 1572872 | tf_op jit(solution)/shard_map/ppermute | solution.py:15
  130.5 21.6 %collective-permute-start.5 = (bf16[2,512,256]{2,1,0:T(8,128)(2,1)S(1)}, bf16[2,512,256]{2,1,0:T(8,128)(2,1)S(1)}, u32[]{:S(2)}, u32[]{:S(2)}) collective-permute-start(bf16[2,512,256]{2,1,0:T(8,128)(2,1)S(1)} %collective-permute-done.3.kv_ref), channel_id=1, source_target_pairs={{0,496},{16,0},{32,16},{48,32},{64,48},{80,64},{96,80},{112,96},{1... | collective-permute-start | bytes 1572872 | tf_op jit(solution)/shard_map/ppermute | solution.py:15
  152.1 10.2 %copy-start.4 = (bf16[2,512,256]{2,1,0:T(8,128)(2,1)}, bf16[2,512,256]{2,1,0:T(8,128)(2,1)S(1)}, u32[]{:S(2)}) copy-start(bf16[2,512,256]{2,1,0:T(8,128)(2,1)S(1)} %collective-permute-done.4.kv_ref) | copy-start | bytes 1572868
  152.1 16.4 %copy-start.5 = (bf16[2,512,256]{2,1,0:T(8,128)(2,1)}, bf16[2,512,256]{2,1,0:T(8,128)(2,1)S(1)}, u32[]{:S(2)}) copy-start(bf16[2,512,256]{2,1,0:T(8,128)(2,1)S(1)} %collective-permute-done.5.kv_ref) | copy-start | bytes 1572868
  152.1 23.8 %collective-permute-start.6 = (bf16[2,512,256]{2,1,0:T(8,128)(2,1)S(1)}, bf16[2,512,256]{2,1,0:T(8,128)(2,1)S(1)}, u32[]{:S(2)}, u32[]{:S(2)}) collective-permute-start(bf16[2,512,256]{2,1,0:T(8,128)(2,1)S(1)} %collective-permute-done.4.kv_ref), channel_id=1, source_target_pairs={{0,16},{16,32},{32,48},{48,64},{64,80},{80,96},{96,112},{112,128},... | collective-permute-start | bytes 1572872 | tf_op jit(solution)/shard_map/ppermute | solution.py:15
  154.0 21.9 %collective-permute-start.7 = (bf16[2,512,256]{2,1,0:T(8,128)(2,1)S(1)}, bf16[2,512,256]{2,1,0:T(8,128)(2,1)S(1)}, u32[]{:S(2)}, u32[]{:S(2)}) collective-permute-start(bf16[2,512,256]{2,1,0:T(8,128)(2,1)S(1)} %collective-permute-done.5.kv_ref), channel_id=1, source_target_pairs={{0,496},{16,0},{32,16},{48,32},{64,48},{80,64},{96,80},{112,96},{1... | collective-permute-start | bytes 1572872 | tf_op jit(solution)/shard_map/ppermute | solution.py:15
  175.9 1.3 copy-start.9
  176.0 8.7 %copy-start.8 = (bf16[2,512,256]{2,1,0:T(8,128)(2,1)}, bf16[2,512,256]{2,1,0:T(8,128)(2,1)S(1)}, u32[]{:S(2)}) copy-start(bf16[2,512,256]{2,1,0:T(8,128)(2,1)S(1)} %collective-permute-done.7.kv_ref) | copy-start | bytes 1572868
  190.9 2.5 %copy-start = (f32[512,256]{1,0:T(8,128)S(1)}, f32[512,256]{1,0:T(8,128)}, u32[]{:S(2)}) copy-start(f32[512,256]{1,0:T(8,128)} %get-tuple-element.120) | copy-start | bytes 1572868
  196.6 2.2 copy-start.15
  198.8 1.1 copy-start.17
Sparse Core Ops, SparseCore 0:
  64.6 82.0 all-gather.2

commit v9 on v3

--- a/solution.py
+++ b/solution.py
@@ -124,6 +124,8 @@
     ahead = shifted(kv_pair, "ctx", 1)
     behind = shifted(kv_pair, "ctx", reach) if bwd_offsets else None
     for i in range(max(len(fwd_offsets), len(bwd_offsets))):
+        if i == 0:
+            ahead, running = lax.optimization_barrier((ahead, running))
         ahead_next = shifted(ahead, "ctx", 1) if i + 1 < len(fwd_offsets) else None
         behind_next = shifted(behind, "ctx", -1) if i + 1 < len(bwd_offsets) else None
         if i < len(fwd_offsets):

time: 223 us -> 224 us (level)
  the two profiles are of different devices: /device:TPU:63 before, /device:TPU:7 now
where the time goes in v9:
time: 224 us; the launch traced here: 223 us
  waiting for transfers between devices  67.2 us (30%)
  Pallas kernels  40.1 us (18%)
  starting transfers between devices  35.8 us (16%)
  between operations  24.3 us (11%)
  blocking collectives  23.4 us (10%)
  local copies, waits for them, and re-layouts  23.3 us (10%)
  other arithmetic  4.55 us (2%)
  matrix products  3.55 us (2%)
    pallas_call x9, Pallas kernels, online_block(): pl.pallas_call(online_block_kernel, out_shape=(jax.ShapeDtypeStruct(run_m...  40.1 us
    all_to_all x1, waiting for transfers between devices, to_heads(): got = lax.all_to_all(send, 'head', split_axis=0, concat_axis=0, tiled=True)  36.7 us
    ppermute x8, waiting for transfers between devices, shifted(): return lax.ppermute(block, axis, route)  30.4 us
    ppermute x8, starting transfers between devices, shifted(): return lax.ppermute(block, axis, route)  24.6 us
    all_to_all x1, blocking collectives, to_tokens(): got = lax.all_to_all(send, 'head', split_axis=0, concat_axis=0, tiled=True)  23.4 us
    all_to_all x1, starting transfers between devices, to_heads(): got = lax.all_to_all(send, 'head', split_axis=0, concat_axis=0, tiled=True)  11.1 us
    broadcast_in_dim x9, local copies, waits for them, and re-layouts, absorb(): jnp.broadcast_to(key_doc[None, :], (8, row_count))  5.43 us
    broadcast_in_dim x9, local copies, waits for them, and re-layouts, absorb(): jnp.broadcast_to(key_pos[None, :], (8, row_count))  5.38 us
  transfers between devices with their start and end apart: 10, of which 6 were waited for; matrix products, arithmetic and copies ran while one was open for 8% of the time, Pallas kernels for 18%

profile of v9, /device:TPU:7, one launch (start us, length us, event | category | flops | bytes accessed | tf_op | source)
XLA Modules:
  0.0 222.8 jit_solution(597040002282068168)
XLA Ops:
  11.4 11.1 %all-to-all-start = ((bf16[16,6,32,256]{3,2,1,0:T(8,128)(2,1)}), bf16[16,6,32,256]{3,2,1,0:T(8,128)(2,1)S(1)}, u32[]{:S(2)}, u32[]{:S(2)}) async-start(bf16[16,6,32,256]{3,2,1,0:T(8,128)(2,1)} %copy.128), calls=%async_computation | async-start | bytes 3145728 | tf_op jit(solution)/shard_map/all_to_all | solution.py:199
  24.3 36.7 %all-to-all-done = bf16[16,6,32,256]{3,2,1,0:T(8,128)(2,1)S(1)} async-done(((bf16[16,6,32,256]{3,2,1,0:T(8,128)(2,1)}), bf16[16,6,32,256]{3,2,1,0:T(8,128)(2,1)S(1)}, u32[]{:S(2)}, u32[]{:S(2)}) %all-to-all-start) | async-done | bytes 1572896 | tf_op jit(solution)/shard_map/all_to_all | solution.py:199
  63.3 3.2 %collective-permute-start = (bf16[2,512,256]{2,1,0:T(8,128)(2,1)S(1)}, bf16[2,512,256]{2,1,0:T(8,128)(2,1)}, u32[]{:S(2)}, u32[]{:S(2)}) collective-permute-start(bf16[2,512,256]{2,1,0:T(8,128)(2,1)S(1)} %bitcast.121), channel_id=1, source_target_pairs={{0,16},{16,32},{32,48},{48,64},{64,80},{80,96},{96,112},{112,128},... | collective-permute-start | bytes 1572872 | tf_op jit(solution)/shard_map/ppermute | solution.py:15
  66.6 2.1 collective-permute-start.2
  71.2 4.5 %shard_map.104 = (f32[2,512,128]{2,1,0:T(8,128)S(1)}, f32[2,512,128]{2,1,0:T(8,128)S(1)}, f32[512,256]{1,0:T(8,128)S(1)}) custom-call(s32[512,128]{1,0:T(8,128)S(1)} %broadcast_in_dim.84.q_doc, s32[8,512]{1,0:T(8,128)} %broadcast_in_dim.85.k_doc, s32[512,128]{1,0:T(8,128)S(1)} %broadcast_in_dim.86.q_pos, ...), custom_call_target="tpu_custom_call", output_to_operand_aliasing={{0}: (6, {}), {1}: (7, {}), {2}: (8, {})} | custom-call | flops 268435456 | bytes 3145728 | tf_op jit(solution)/shard_map/pallas_call | solution.py:57
  75.7 6.1 %collective-permute-done = bf16[2,512,256]{2,1,0:T(8,128)(2,1)} collective-permute-done((bf16[2,512,256]{2,1,0:T(8,128)(2,1)S(1)}, bf16[2,512,256]{2,1,0:T(8,128)(2,1)}, u32[]{:S(2)}, u32[]{:S(2)}) %collective-permute-start) | collective-permute-done | bytes 524320 | tf_op jit(solution)/shard_map/ppermute | solution.py:15
  81.8 1.9 collective-permute-start.1
  83.7 21.3 %collective-permute-done.2 = bf16[2,512,256]{2,1,0:T(8,128)(2,1)} collective-permute-done((bf16[2,512,256]{2,1,0:T(8,128)(2,1)S(1)}, bf16[2,512,256]{2,1,0:T(8,128)(2,1)}, u32[]{:S(2)}, u32[]{:S(2)}) %collective-permute-start.2) | collective-permute-done | bytes 524320 | tf_op jit(solution)/shard_map/ppermute | solution.py:15
  105.0 1.9 collective-permute-start.3
  109.8 5.8 %conditional.8 = ((f32[2,512,128]{2,1,0:T(8,128)S(1)}, f32[2,512,128]{2,1,0:T(8,128)S(1)}, f32[512,256]{1,0:T(8,128)S(1)})) conditional(s32[]{:T(128)} %convert_element_type.140, (f32[2,512,128]{2,1,0:T(8,128)S(1)}, f32[2,512,128]{2,1,0:T(8,128)S(1)}, f32[512,256]{1,0:T(8,128)S(1)}) %shard_map.104, (s32[]{:T(128)}, s32[32]{0:T(128)S(1)}, ...), branch_computations={%region_6.7_spmd, %region_7.9_spmd} | conditional | flops 268485120 | bytes 3192984 | solution.py:117
  111.2 4.5 %branch_1_fun.9 = (f32[2,512,128]{2,1,0:T(8,128)S(1)}, f32[2,512,128]{2,1,0:T(8,128)S(1)}, f32[512,256]{1,0:T(8,128)S(1)}) custom-call(s32[512,128]{1,0:T(8,128)S(1)} %get-tuple-element.227.q_doc, s32[8,512]{1,0:T(8,128)} %broadcast_in_dim.24.k_doc, ...), custom_call_target="tpu_custom_call", output_to_operand_aliasing={{0}: (6, {}), {1}: (7, {}), {2}: (8, {})} | custom-call | flops 268435456 | bytes 3145728 | tf_op jit(solution)/shard_map/cond/branch_1_fun/pallas_call | solution.py:57
  115.6 5.8 %conditional.9 = ((f32[2,512,128]{2,1,0:T(8,128)S(1)}, f32[2,512,128]{2,1,0:T(8,128)S(1)}, f32[512,256]{1,0:T(8,128)S(1)})) conditional(s32[]{:T(128)} %convert_element_type.138, (f32[2,512,128]{2,1,0:T(8,128)S(1)}, f32[2,512,128]{2,1,0:T(8,128)S(1)}, f32[512,256]{1,0:T(8,128)S(1)}) %get-tuple-element.462, (s32[]{:T(128)}, s32[32]{0:T(128)S(1)}, ...), branch_computations={%region_9.10_spmd, %region_10.12_spmd} | conditional | flops 268485120 | bytes 3192984 | solution.py:117
  116.9 4.5 %branch_1_fun.10 = (f32[2,512,128]{2,1,0:T(8,128)S(1)}, f32[2,512,128]{2,1,0:T(8,128)S(1)}, f32[512,256]{1,0:T(8,128)S(1)}) custom-call(s32[512,128]{1,0:T(8,128)S(1)} %get-tuple-element.236.q_doc, s32[8,512]{1,0:T(8,128)} %broadcast_in_dim.28.k_doc, ...), custom_call_target="tpu_custom_call", output_to_operand_aliasing={{0}: (6, {}), {1}: (7, {}), {2}: (8, {})} | custom-call | flops 268435456 | bytes 3145728 | tf_op jit(solution)/shard_map/cond/branch_1_fun/pallas_call | solution.py:57
  121.8 1.9 collective-permute-start.4
  123.7 5.5 %collective-permute-start.5 = (bf16[2,512,256]{2,1,0:T(8,128)(2,1)}, bf16[2,512,256]{2,1,0:T(8,128)(2,1)}, u32[]{:S(2)}, u32[]{:S(2)}) collective-permute-start(bf16[2,512,256]{2,1,0:T(8,128)(2,1)} %collective-permute-done.3), channel_id=1, source_target_pairs={{0,496},{16,0},{32,16},{48,32},{64,48},{80,64},{96,80},{112,96},{1... | collective-permute-start | bytes 1572872 | tf_op jit(solution)/shard_map/ppermute | solution.py:15
  131.5 6.0 %conditional.10 = ((f32[2,512,128]{2,1,0:T(8,128)S(1)}, f32[2,512,128]{2,1,0:T(8,128)S(1)}, f32[512,256]{1,0:T(8,128)S(1)})) conditional(s32[]{:T(128)} %convert_element_type.144, (f32[2,512,128]{2,1,0:T(8,128)S(1)}, f32[2,512,128]{2,1,0:T(8,128)S(1)}, f32[512,256]{1,0:T(8,128)S(1)}) %get-tuple-element.463, (s32[]{:T(128)}, s32[32]{0:T(128)S(1)}, ...), branch_computations={%region_14.15_spmd, %region_15.17_spmd} | conditional | flops 268485120 | bytes 3192984 | solution.py:117
  133.0 4.5 %branch_1_fun.11 = (f32[2,512,128]{2,1,0:T(8,128)S(1)}, f32[2,512,128]{2,1,0:T(8,128)S(1)}, f32[512,256]{1,0:T(8,128)S(1)}) custom-call(s32[512,128]{1,0:T(8,128)S(1)} %get-tuple-element.245.q_doc, s32[8,512]{1,0:T(8,128)} %broadcast_in_dim.36.k_doc, ...), custom_call_target="tpu_custom_call", output_to_operand_aliasing={{0}: (6, {}), {1}: (7, {}), {2}: (8, {})} | custom-call | flops 268435456 | bytes 3145728 | tf_op jit(solution)/shard_map/cond/branch_1_fun/pallas_call | solution.py:57
  137.5 5.8 %conditional.11 = ((f32[2,512,128]{2,1,0:T(8,128)S(1)}, f32[2,512,128]{2,1,0:T(8,128)S(1)}, f32[512,256]{1,0:T(8,128)S(1)})) conditional(s32[]{:T(128)} %convert_element_type.142, (f32[2,512,128]{2,1,0:T(8,128)S(1)}, f32[2,512,128]{2,1,0:T(8,128)S(1)}, f32[512,256]{1,0:T(8,128)S(1)}) %get-tuple-element.464, (s32[]{:T(128)}, s32[32]{0:T(128)S(1)}, ...), branch_computations={%region_17.18_spmd, %region_18.20_spmd} | conditional | flops 268485120 | bytes 3192984 | solution.py:117
  138.8 4.5 %branch_1_fun.12 = (f32[2,512,128]{2,1,0:T(8,128)S(1)}, f32[2,512,128]{2,1,0:T(8,128)S(1)}, f32[512,256]{1,0:T(8,128)S(1)}) custom-call(s32[512,128]{1,0:T(8,128)S(1)} %get-tuple-element.254.q_doc, s32[8,512]{1,0:T(8,128)} %broadcast_in_dim.40.k_doc, ...), custom_call_target="tpu_custom_call", output_to_operand_aliasing={{0}: (6, {}), {1}: (7, {}), {2}: (8, {})} | custom-call | flops 268435456 | bytes 3145728 | tf_op jit(solution)/shard_map/cond/branch_1_fun/pallas_call | solution.py:57
  143.2 2.1 collective-permute-done.4
  145.9 1.9 collective-permute-start.6
  147.8 6.2 %collective-permute-start.7 = (bf16[2,512,256]{2,1,0:T(8,128)(2,1)}, bf16[2,512,256]{2,1,0:T(8,128)(2,1)}, u32[]{:S(2)}, u32[]{:S(2)}) collective-permute-start(bf16[2,512,256]{2,1,0:T(8,128)(2,1)} %collective-permute-done.5), channel_id=1, source_target_pairs={{0,496},{16,0},{32,16},{48,32},{64,48},{80,64},{96,80},{112,96},{1... | collective-permute-start | bytes 1572872 | tf_op jit(solution)/shard_map/ppermute | solution.py:15
  159.1 5.8 %conditional.12 = ((f32[2,512,128]{2,1,0:T(8,128)S(1)}, f32[2,512,128]{2,1,0:T(8,128)S(1)}, f32[512,256]{1,0:T(8,128)S(1)})) conditional(s32[]{:T(128)} %convert_element_type.148, (f32[2,512,128]{2,1,0:T(8,128)S(1)}, f32[2,512,128]{2,1,0:T(8,128)S(1)}, f32[512,256]{1,0:T(8,128)S(1)}) %get-tuple-element.465, (s32[]{:T(128)}, s32[32]{0:T(128)S(1)}, ...), branch_computations={%region_22.23_spmd, %region_23.25_spmd} | conditional | flops 268485120 | bytes 3192984 | solution.py:117
  160.4 4.5 %branch_1_fun.13 = (f32[2,512,128]{2,1,0:T(8,128)S(1)}, f32[2,512,128]{2,1,0:T(8,128)S(1)}, f32[512,256]{1,0:T(8,128)S(1)}) custom-call(s32[512,128]{1,0:T(8,128)S(1)} %get-tuple-element.263.q_doc, s32[8,512]{1,0:T(8,128)} %broadcast_in_dim.42.k_doc, ...), custom_call_target="tpu_custom_call", output_to_operand_aliasing={{0}: (6, {}), {1}: (7, {}), {2}: (8, {})} | custom-call | flops 268435456 | bytes 3145728 | tf_op jit(solution)/shard_map/cond/branch_1_fun/pallas_call | solution.py:57
  164.9 5.8 %conditional.13 = ((f32[2,512,128]{2,1,0:T(8,128)S(1)}, f32[2,512,128]{2,1,0:T(8,128)S(1)}, f32[512,256]{1,0:T(8,128)S(1)})) conditional(s32[]{:T(128)} %convert_element_type.146, (f32[2,512,128]{2,1,0:T(8,128)S(1)}, f32[2,512,128]{2,1,0:T(8,128)S(1)}, f32[512,256]{1,0:T(8,128)S(1)}) %get-tuple-element.466, (s32[]{:T(128)}, s32[32]{0:T(128)S(1)}, ...), branch_computations={%region_25.26_spmd, %region_26.28_spmd} | conditional | flops 268485120 | bytes 3192984 | solution.py:117
  166.2 4.5 %branch_1_fun.14 = (f32[2,512,128]{2,1,0:T(8,128)S(1)}, f32[2,512,128]{2,1,0:T(8,128)S(1)}, f32[512,256]{1,0:T(8,128)S(1)}) custom-call(s32[512,128]{1,0:T(8,128)S(1)} %get-tuple-element.272.q_doc, s32[8,512]{1,0:T(8,128)} %broadcast_in_dim.56.k_doc, ...), custom_call_target="tpu_custom_call", output_to_operand_aliasing={{0}: (6, {}), {1}: (7, {}), {2}: (8, {})} | custom-call | flops 268435456 | bytes 3145728 | tf_op jit(solution)/shard_map/cond/branch_1_fun/pallas_call | solution.py:57
  170.7 6.0 %conditional.14 = ((f32[2,512,128]{2,1,0:T(8,128)S(1)}, f32[2,512,128]{2,1,0:T(8,128)S(1)}, f32[512,256]{1,0:T(8,128)S(1)})) conditional(s32[]{:T(128)} %convert_element_type.136, (f32[2,512,128]{2,1,0:T(8,128)S(1)}, f32[2,512,128]{2,1,0:T(8,128)S(1)}, f32[512,256]{1,0:T(8,128)S(1)}) %get-tuple-element.467, (s32[]{:T(128)}, s32[32]{0:T(128)S(1)}, ...), branch_computations={%region_28.29_spmd, %region_29.31_spmd} | conditional | flops 268485120 | bytes 3192984 | solution.py:117
  172.2 4.5 %branch_1_fun.15 = (f32[2,512,128]{2,1,0:T(8,128)S(1)}, f32[2,512,128]{2,1,0:T(8,128)S(1)}, f32[512,256]{1,0:T(8,128)S(1)}) custom-call(s32[512,128]{1,0:T(8,128)S(1)} %get-tuple-element.281.q_doc, s32[8,512]{1,0:T(8,128)} %broadcast_in_dim.58.k_doc, ...), custom_call_target="tpu_custom_call", output_to_operand_aliasing={{0}: (6, {}), {1}: (7, {}), {2}: (8, {})} | custom-call | flops 268435456 | bytes 3145728 | tf_op jit(solution)/shard_map/cond/branch_1_fun/pallas_call | solution.py:57
  176.7 5.8 %conditional.15 = ((f32[2,512,128]{2,1,0:T(8,128)S(1)}, f32[512,256]{1,0:T(8,128)S(1)})) conditional(s32[]{:T(128)} %convert_element_type.134, (f32[2,512,128]{2,1,0:T(8,128)S(1)}, f32[512,256]{1,0:T(8,128)S(1)}) %tuple.86, (s32[]{:T(128)}, s32[32]{0:T(128)S(1)}, s32[512,128]{1,0:T(8,128)S(1)}, s32[512,128]{1,0:T(8,128)S(1)}, ...), branch_computations={%region_31.32_spmd, %region_32.34_spmd} | conditional | flops 268485120 | bytes 3193000 | solution.py:117
  178.0 4.5 %branch_1_fun.16 = (f32[2,512,128]{2,1,0:T(8,128)S(1)}, f32[2,512,128]{2,1,0:T(8,128)S(1)}, f32[512,256]{1,0:T(8,128)S(1)}) custom-call(s32[512,128]{1,0:T(8,128)S(1)} %get-tuple-element.290.q_doc, s32[8,512]{1,0:T(8,128)} %broadcast_in_dim.60.k_doc, ...), custom_call_target="tpu_custom_call", output_to_operand_aliasing={{0}: (6, {}), {1}: (7, {}), {2}: (8, {})} | custom-call | flops 268435456 | bytes 3145728 | tf_op jit(solution)/shard_map/cond/branch_1_fun/pallas_call | solution.py:57
  187.1 1.8 fusion
  191.0 23.4 %all_to_all.10 = bf16[16,2,32,256]{3,2,1,0:T(8,128)(2,1)S(1)} all-to-all(bf16[16,2,32,256]{3,2,1,0:T(8,128)(2,1)S(1)} %copy.142), channel_id=1, replica_groups=mesh['ctx'=32,'head'=16] {'head'}, dimensions={0} | all-to-all | bytes 1048576 | tf_op jit(solution)/shard_map/all_to_all | solution.py:206
  (144 shorter events, 30.6 us)
Async XLA Ops:
  7.2 2.2 copy-start.1
  7.2 2.2 copy-start.2
  7.2 2.3 %copy-start.3 = (bf16[32,4096]{1,0:T(8,128)(2,1)S(1)}, bf16[32,4096]{1,0:T(8,128)(2,1)}, u32[]{:S(2)}) copy-start(bf16[32,4096]{1,0:T(8,128)(2,1)} %param.33) | copy-start | bytes 786436
  7.2 2.3 %copy-start.4 = (bf16[32,4096]{1,0:T(8,128)(2,1)S(1)}, bf16[32,4096]{1,0:T(8,128)(2,1)}, u32[]{:S(2)}) copy-start(bf16[32,4096]{1,0:T(8,128)(2,1)} %param.34) | copy-start | bytes 786436
  11.4 11.2 %copy-start.7 = (f32[2,512]{1,0:T(2,128)S(1)}, f32[2,512]{1,0:T(2,128)}, u32[]{:S(2)}) copy-start(f32[2,512]{1,0:T(2,128)} %param.35) | copy-start | bytes 12292
  11.4 49.6 %all-to-all-start = ((bf16[16,6,32,256]{3,2,1,0:T(8,128)(2,1)}), bf16[16,6,32,256]{3,2,1,0:T(8,128)(2,1)S(1)}, u32[]{:S(2)}, u32[]{:S(2)}) async-start(bf16[16,6,32,256]{3,2,1,0:T(8,128)(2,1)} %copy.128), calls=%async_computation | async-start | bytes 3145728 | tf_op jit(solution)/shard_map/all_to_all | solution.py:199
  22.6 161.4 %all-gather.3.cloned.1.call-start = ((), (), s32[]{:S(2)}) async-start(), calls=%async_computation.2 | async-start | bytes 2433024 | tf_op jit(solution)/shard_map/all_gather | solution.py:161
  61.1 1.9 copy-start.8
  61.3 2.0 copy-start.5
  63.3 7.9 %copy-start = (bf16[2,16,32,256]{3,2,1,0:T(8,128)(2,1)}, bf16[2,16,32,256]{3,2,1,0:T(8,128)(2,1)S(1)}, u32[]{:S(2)}) copy-start(bf16[2,16,32,256]{3,2,1,0:T(8,128)(2,1)S(1)} %copy.129) | copy-start | bytes 1572868
  63.3 18.4 %collective-permute-start = (bf16[2,512,256]{2,1,0:T(8,128)(2,1)S(1)}, bf16[2,512,256]{2,1,0:T(8,128)(2,1)}, u32[]{:S(2)}, u32[]{:S(2)}) collective-permute-start(bf16[2,512,256]{2,1,0:T(8,128)(2,1)S(1)} %bitcast.121), channel_id=1, source_target_pairs={{0,16},{16,32},{32,48},{48,64},{64,80},{80,96},{96,112},{112,128},... | collective-permute-start | bytes 1572872 | tf_op jit(solution)/shard_map/ppermute | solution.py:15
  66.6 38.5 %collective-permute-start.2 = (bf16[2,512,256]{2,1,0:T(8,128)(2,1)S(1)}, bf16[2,512,256]{2,1,0:T(8,128)(2,1)}, u32[]{:S(2)}, u32[]{:S(2)}) collective-permute-start(bf16[2,512,256]{2,1,0:T(8,128)(2,1)S(1)} %bitcast.122), channel_id=1, source_target_pairs={{0,128},{16,144},{32,160},{48,176},{64,192},{80,208},{96,224},{112... | collective-permute-start | bytes 1572872 | tf_op jit(solution)/shard_map/ppermute | solution.py:15
  81.8 39.6 %collective-permute-start.1 = (bf16[2,512,256]{2,1,0:T(8,128)(2,1)}, bf16[2,512,256]{2,1,0:T(8,128)(2,1)}, u32[]{:S(2)}, u32[]{:S(2)}) collective-permute-start(bf16[2,512,256]{2,1,0:T(8,128)(2,1)} %collective-permute-done), channel_id=1, source_target_pairs={{0,16},{16,32},{32,48},{48,64},{64,80},{80,96},{96,112},{112,128},... | collective-permute-start | bytes 1572872 | tf_op jit(solution)/shard_map/ppermute | solution.py:15
  105.0 16.7 %collective-permute-start.3 = (bf16[2,512,256]{2,1,0:T(8,128)(2,1)}, bf16[2,512,256]{2,1,0:T(8,128)(2,1)}, u32[]{:S(2)}, u32[]{:S(2)}) collective-permute-start(bf16[2,512,256]{2,1,0:T(8,128)(2,1)} %collective-permute-done.2), channel_id=1, source_target_pairs={{0,496},{16,0},{32,16},{48,32},{64,48},{80,64},{96,80},{112,96},{1... | collective-permute-start | bytes 1572872 | tf_op jit(solution)/shard_map/ppermute | solution.py:15
  121.8 23.5 %collective-permute-start.4 = (bf16[2,512,256]{2,1,0:T(8,128)(2,1)}, bf16[2,512,256]{2,1,0:T(8,128)(2,1)}, u32[]{:S(2)}, u32[]{:S(2)}) collective-permute-start(bf16[2,512,256]{2,1,0:T(8,128)(2,1)} %collective-permute-done.1), channel_id=1, source_target_pairs={{0,16},{16,32},{32,48},{48,64},{64,80},{80,96},{96,112},{112,128},... | collective-permute-start | bytes 1572872 | tf_op jit(solution)/shard_map/ppermute | solution.py:15
  123.7 22.2 %collective-permute-start.5 = (bf16[2,512,256]{2,1,0:T(8,128)(2,1)}, bf16[2,512,256]{2,1,0:T(8,128)(2,1)}, u32[]{:S(2)}, u32[]{:S(2)}) collective-permute-start(bf16[2,512,256]{2,1,0:T(8,128)(2,1)} %collective-permute-done.3), channel_id=1, source_target_pairs={{0,496},{16,0},{32,16},{48,32},{64,48},{80,64},{96,80},{112,96},{1... | collective-permute-start | bytes 1572872 | tf_op jit(solution)/shard_map/ppermute | solution.py:15
  145.9 24.8 %collective-permute-start.6 = (bf16[2,512,256]{2,1,0:T(8,128)(2,1)}, bf16[2,512,256]{2,1,0:T(8,128)(2,1)}, u32[]{:S(2)}, u32[]{:S(2)}) collective-permute-start(bf16[2,512,256]{2,1,0:T(8,128)(2,1)} %collective-permute-done.4), channel_id=1, source_target_pairs={{0,16},{16,32},{32,48},{48,64},{64,80},{80,96},{96,112},{112,128},... | collective-permute-start | bytes 1572872 | tf_op jit(solution)/shard_map/ppermute | solution.py:15
  147.8 22.9 %collective-permute-start.7 = (bf16[2,512,256]{2,1,0:T(8,128)(2,1)}, bf16[2,512,256]{2,1,0:T(8,128)(2,1)}, u32[]{:S(2)}, u32[]{:S(2)}) collective-permute-start(bf16[2,512,256]{2,1,0:T(8,128)(2,1)} %collective-permute-done.5), channel_id=1, source_target_pairs={{0,496},{16,0},{32,16},{48,32},{64,48},{80,64},{96,80},{112,96},{1... | collective-permute-start | bytes 1572872 | tf_op jit(solution)/shard_map/ppermute | solution.py:15
  187.1 2.2 copy-start.6
  189.3 1.1 copy-start.9
Sparse Core Ops, SparseCore 0:
  63.0 82.0 all-gather.2

commit v10 on v3

--- a/solution.py
+++ b/solution.py
@@ -128,11 +128,10 @@
         behind_next = shifted(behind, "ctx", -1) if i + 1 < len(bwd_offsets) else None
         if i < len(fwd_offsets):
             running = absorb_if_needed(running, ahead, fwd_offsets[i])
+            ahead_next, running = lax.optimization_barrier((ahead_next, running))
         if i < len(bwd_offsets):
             running = absorb_if_needed(running, behind, bwd_offsets[i])
-        ahead_next, behind_next, running = lax.optimization_barrier(
-            (ahead_next, behind_next, running)
-        )
+            behind_next, running = lax.optimization_barrier((behind_next, running))
         ahead, behind = ahead_next, behind_next
     run_max, run_total, run_acc = running
     totals = run_total[:, :, 0].T

time: 223 us -> 223 us (level)
  the two profiles are of different devices: /device:TPU:63 before, /device:TPU:27 now
where the time goes in v10:
time: 223 us; the launch traced here: 222 us
  waiting for transfers between devices  52.7 us (24%)
  starting transfers between devices  49.1 us (22%)
  Pallas kernels  40.1 us (18%)
  between operations  24.7 us (11%)
  local copies, waits for them, and re-layouts  23.3 us (10%)
  blocking collectives  23.3 us (10%)
  other arithmetic  4.51 us (2%)
  matrix products  3.55 us (2%)
    pallas_call x9, Pallas kernels, online_block(): pl.pallas_call(online_block_kernel, out_shape=(jax.ShapeDtypeStruct(run_m...  40.1 us
    ppermute x8, starting transfers between devices, shifted(): return lax.ppermute(block, axis, route)  38 us
    all_to_all x1, waiting for transfers between devices, to_heads(): got = lax.all_to_all(send, 'head', split_axis=0, concat_axis=0, tiled=True)  36.7 us
    all_to_all x1, blocking collectives, to_tokens(): got = lax.all_to_all(send, 'head', split_axis=0, concat_axis=0, tiled=True)  23.3 us
    ppermute x8, waiting for transfers between devices, shifted(): return lax.ppermute(block, axis, route)  16 us
    all_to_all x1, starting transfers between devices, to_heads(): got = lax.all_to_all(send, 'head', split_axis=0, concat_axis=0, tiled=True)  11.1 us
    broadcast_in_dim x9, local copies, waits for them, and re-layouts, absorb(): jnp.broadcast_to(key_doc[None, :], (8, row_count))  5.44 us
    broadcast_in_dim x9, local copies, waits for them, and re-layouts, absorb(): jnp.broadcast_to(key_pos[None, :], (8, row_count))  5.38 us
  transfers between devices with their start and end apart: 10, of which 3 were waited for; matrix products, arithmetic and copies ran while one was open for 8% of the time, Pallas kernels for 18%

profile of v10, /device:TPU:27, one launch (start us, length us, event | category | flops | bytes accessed | tf_op | source)
XLA Modules:
  0.0 222.0 jit_solution(16559670644228586214)
XLA Ops:
  11.4 11.1 %all-to-all-start = ((bf16[16,6,32,256]{3,2,1,0:T(8,128)(2,1)}), bf16[16,6,32,256]{3,2,1,0:T(8,128)(2,1)S(1)}, u32[]{:S(2)}, u32[]{:S(2)}) async-start(bf16[16,6,32,256]{3,2,1,0:T(8,128)(2,1)} %copy.128), calls=%async_computation | async-start | bytes 3145728 | tf_op jit(solution)/shard_map/all_to_all | solution.py:196
  24.3 36.7 %all-to-all-done = bf16[16,6,32,256]{3,2,1,0:T(8,128)(2,1)S(1)} async-done(((bf16[16,6,32,256]{3,2,1,0:T(8,128)(2,1)}), bf16[16,6,32,256]{3,2,1,0:T(8,128)(2,1)S(1)}, u32[]{:S(2)}, u32[]{:S(2)}) %all-to-all-start) | async-done | bytes 1572896 | tf_op jit(solution)/shard_map/all_to_all | solution.py:196
  63.0 4.4 %collective-permute-start.2 = (bf16[2,512,256]{2,1,0:T(8,128)(2,1)S(1)}, bf16[2,512,256]{2,1,0:T(8,128)(2,1)}, u32[]{:S(2)}, u32[]{:S(2)}) collective-permute-start(bf16[2,512,256]{2,1,0:T(8,128)(2,1)S(1)} %bitcast.121), channel_id=1, source_target_pairs={{0,16},{16,32},{32,48},{48,64},{64,80},{80,96},{96,112},{112,128},... | collective-permute-start | bytes 1572872 | tf_op jit(solution)/shard_map/ppermute | solution.py:15
  67.5 3.1 %collective-permute-start = (bf16[2,512,256]{2,1,0:T(8,128)(2,1)S(1)}, bf16[2,512,256]{2,1,0:T(8,128)(2,1)}, u32[]{:S(2)}, u32[]{:S(2)}) collective-permute-start(bf16[2,512,256]{2,1,0:T(8,128)(2,1)S(1)} %bitcast.122), channel_id=1, source_target_pairs={{0,128},{16,144},{32,160},{48,176},{64,192},{80,208},{96,224},{112... | collective-permute-start | bytes 1572872 | tf_op jit(solution)/shard_map/ppermute | solution.py:15
  70.9 8.7 %collective-permute-done.2 = bf16[2,512,256]{2,1,0:T(8,128)(2,1)} collective-permute-done((bf16[2,512,256]{2,1,0:T(8,128)(2,1)S(1)}, bf16[2,512,256]{2,1,0:T(8,128)(2,1)}, u32[]{:S(2)}, u32[]{:S(2)}) %collective-permute-start.2) | collective-permute-done | bytes 524320 | tf_op jit(solution)/shard_map/ppermute | solution.py:15
  79.6 5.4 %collective-permute-start.3 = (bf16[2,512,256]{2,1,0:T(8,128)(2,1)}, bf16[2,512,256]{2,1,0:T(8,128)(2,1)}, u32[]{:S(2)}, u32[]{:S(2)}) collective-permute-start(bf16[2,512,256]{2,1,0:T(8,128)(2,1)} %collective-permute-done.2), channel_id=1, source_target_pairs={{0,16},{16,32},{32,48},{48,64},{64,80},{80,96},{96,112},{112,128},... | collective-permute-start | bytes 1572872 | tf_op jit(solution)/shard_map/ppermute | solution.py:15
  85.0 1.9 collective-permute-start.1
  92.5 4.5 %shard_map.104 = (f32[2,512,128]{2,1,0:T(8,128)S(1)}, f32[2,512,128]{2,1,0:T(8,128)S(1)}, f32[512,256]{1,0:T(8,128)S(1)}) custom-call(s32[512,128]{1,0:T(8,128)S(1)} %broadcast_in_dim.84.q_doc, s32[8,512]{1,0:T(8,128)} %broadcast_in_dim.85.k_doc, s32[512,128]{1,0:T(8,128)S(1)} %broadcast_in_dim.86.q_pos, ...), custom_call_target="tpu_custom_call", output_to_operand_aliasing={{0}: (6, {}), {1}: (7, {}), {2}: (8, {})} | custom-call | flops 268435456 | bytes 3145728 | tf_op jit(solution)/shard_map/pallas_call | solution.py:57
  96.9 5.8 %conditional.8 = ((f32[2,512,128]{2,1,0:T(8,128)S(1)}, f32[2,512,128]{2,1,0:T(8,128)S(1)}, f32[512,256]{1,0:T(8,128)S(1)})) conditional(s32[]{:T(128)} %convert_element_type.140, (f32[2,512,128]{2,1,0:T(8,128)S(1)}, f32[2,512,128]{2,1,0:T(8,128)S(1)}, f32[512,256]{1,0:T(8,128)S(1)}) %shard_map.104, (s32[]{:T(128)}, s32[32]{0:T(128)S(1)}, ...), branch_computations={%region_6.7_spmd, %region_7.9_spmd} | conditional | flops 268485120 | bytes 3192984 | solution.py:117
  98.3 4.5 %branch_1_fun.9 = (f32[2,512,128]{2,1,0:T(8,128)S(1)}, f32[2,512,128]{2,1,0:T(8,128)S(1)}, f32[512,256]{1,0:T(8,128)S(1)}) custom-call(s32[512,128]{1,0:T(8,128)S(1)} %get-tuple-element.227.q_doc, s32[8,512]{1,0:T(8,128)} %broadcast_in_dim.24.k_doc, ...), custom_call_target="tpu_custom_call", output_to_operand_aliasing={{0}: (6, {}), {1}: (7, {}), {2}: (8, {})} | custom-call | flops 268435456 | bytes 3145728 | tf_op jit(solution)/shard_map/cond/branch_1_fun/pallas_call | solution.py:57
  102.7 4.6 %collective-permute-start.5 = (bf16[2,512,256]{2,1,0:T(8,128)(2,1)}, bf16[2,512,256]{2,1,0:T(8,128)(2,1)}, u32[]{:S(2)}, u32[]{:S(2)}) collective-permute-start(bf16[2,512,256]{2,1,0:T(8,128)(2,1)} %collective-permute-done.3), channel_id=1, source_target_pairs={{0,16},{16,32},{32,48},{48,64},{64,80},{80,96},{96,112},{112,128},... | collective-permute-start | bytes 1572872 | tf_op jit(solution)/shard_map/ppermute | solution.py:15
  107.3 5.8 %conditional.9 = ((f32[2,512,128]{2,1,0:T(8,128)S(1)}, f32[2,512,128]{2,1,0:T(8,128)S(1)}, f32[512,256]{1,0:T(8,128)S(1)})) conditional(s32[]{:T(128)} %convert_element_type.138, (f32[2,512,128]{2,1,0:T(8,128)S(1)}, f32[2,512,128]{2,1,0:T(8,128)S(1)}, f32[512,256]{1,0:T(8,128)S(1)}) %get-tuple-element.472, (s32[]{:T(128)}, s32[32]{0:T(128)S(1)}, ...), branch_computations={%region_9.10_spmd, %region_10.12_spmd} | conditional | flops 268485120 | bytes 3192984 | solution.py:117
  108.6 4.5 %branch_1_fun.10 = (f32[2,512,128]{2,1,0:T(8,128)S(1)}, f32[2,512,128]{2,1,0:T(8,128)S(1)}, f32[512,256]{1,0:T(8,128)S(1)}) custom-call(s32[512,128]{1,0:T(8,128)S(1)} %get-tuple-element.236.q_doc, s32[8,512]{1,0:T(8,128)} %broadcast_in_dim.28.k_doc, ...), custom_call_target="tpu_custom_call", output_to_operand_aliasing={{0}: (6, {}), {1}: (7, {}), {2}: (8, {})} | custom-call | flops 268435456 | bytes 3145728 | tf_op jit(solution)/shard_map/cond/branch_1_fun/pallas_call | solution.py:57
  113.1 1.9 collective-permute-start.4
  117.5 6.0 %conditional.10 = ((f32[2,512,128]{2,1,0:T(8,128)S(1)}, f32[2,512,128]{2,1,0:T(8,128)S(1)}, f32[512,256]{1,0:T(8,128)S(1)})) conditional(s32[]{:T(128)} %convert_element_type.144, (f32[2,512,128]{2,1,0:T(8,128)S(1)}, f32[2,512,128]{2,1,0:T(8,128)S(1)}, f32[512,256]{1,0:T(8,128)S(1)}) %get-tuple-element.473, (s32[]{:T(128)}, s32[32]{0:T(128)S(1)}, ...), branch_computations={%region_14.15_spmd, %region_15.17_spmd} | conditional | flops 268485120 | bytes 3192984 | solution.py:117
  119.0 4.5 %branch_1_fun.11 = (f32[2,512,128]{2,1,0:T(8,128)S(1)}, f32[2,512,128]{2,1,0:T(8,128)S(1)}, f32[512,256]{1,0:T(8,128)S(1)}) custom-call(s32[512,128]{1,0:T(8,128)S(1)} %get-tuple-element.245.q_doc, s32[8,512]{1,0:T(8,128)} %broadcast_in_dim.36.k_doc, ...), custom_call_target="tpu_custom_call", output_to_operand_aliasing={{0}: (6, {}), {1}: (7, {}), {2}: (8, {})} | custom-call | flops 268435456 | bytes 3145728 | tf_op jit(solution)/shard_map/cond/branch_1_fun/pallas_call | solution.py:57
  123.5 1.9 collective-permute-start.7
  125.4 5.8 %conditional.11 = ((f32[2,512,128]{2,1,0:T(8,128)S(1)}, f32[2,512,128]{2,1,0:T(8,128)S(1)}, f32[512,256]{1,0:T(8,128)S(1)})) conditional(s32[]{:T(128)} %convert_element_type.142, (f32[2,512,128]{2,1,0:T(8,128)S(1)}, f32[2,512,128]{2,1,0:T(8,128)S(1)}, f32[512,256]{1,0:T(8,128)S(1)}) %get-tuple-element.474, (s32[]{:T(128)}, s32[32]{0:T(128)S(1)}, ...), branch_computations={%region_17.18_spmd, %region_18.20_spmd} | conditional | flops 268485120 | bytes 3192984 | solution.py:117
  126.8 4.5 %branch_1_fun.12 = (f32[2,512,128]{2,1,0:T(8,128)S(1)}, f32[2,512,128]{2,1,0:T(8,128)S(1)}, f32[512,256]{1,0:T(8,128)S(1)}) custom-call(s32[512,128]{1,0:T(8,128)S(1)} %get-tuple-element.254.q_doc, s32[8,512]{1,0:T(8,128)} %broadcast_in_dim.40.k_doc, ...), custom_call_target="tpu_custom_call", output_to_operand_aliasing={{0}: (6, {}), {1}: (7, {}), {2}: (8, {})} | custom-call | flops 268435456 | bytes 3145728 | tf_op jit(solution)/shard_map/cond/branch_1_fun/pallas_call | solution.py:57
  131.2 7.3 %collective-permute-done.4 = bf16[2,512,256]{2,1,0:T(8,128)(2,1)} collective-permute-done((bf16[2,512,256]{2,1,0:T(8,128)(2,1)}, bf16[2,512,256]{2,1,0:T(8,128)(2,1)}, u32[]{:S(2)}, u32[]{:S(2)}) %collective-permute-start.4) | collective-permute-done | bytes 524320 | tf_op jit(solution)/shard_map/ppermute | solution.py:15
  138.5 14.7 %collective-permute-start.6 = (bf16[2,512,256]{2,1,0:T(8,128)(2,1)}, bf16[2,512,256]{2,1,0:T(8,128)(2,1)}, u32[]{:S(2)}, u32[]{:S(2)}) collective-permute-start(bf16[2,512,256]{2,1,0:T(8,128)(2,1)} %collective-permute-done.4), channel_id=1, source_target_pairs={{0,496},{16,0},{32,16},{48,32},{64,48},{80,64},{96,80},{112,96},{1... | collective-permute-start | bytes 1572872 | tf_op jit(solution)/shard_map/ppermute | solution.py:15
  158.5 5.8 %conditional.12 = ((f32[2,512,128]{2,1,0:T(8,128)S(1)}, f32[2,512,128]{2,1,0:T(8,128)S(1)}, f32[512,256]{1,0:T(8,128)S(1)})) conditional(s32[]{:T(128)} %convert_element_type.148, (f32[2,512,128]{2,1,0:T(8,128)S(1)}, f32[2,512,128]{2,1,0:T(8,128)S(1)}, f32[512,256]{1,0:T(8,128)S(1)}) %get-tuple-element.475, (s32[]{:T(128)}, s32[32]{0:T(128)S(1)}, ...), branch_computations={%region_22.23_spmd, %region_23.25_spmd} | conditional | flops 268485120 | bytes 3192984 | solution.py:117
  159.9 4.5 %branch_1_fun.13 = (f32[2,512,128]{2,1,0:T(8,128)S(1)}, f32[2,512,128]{2,1,0:T(8,128)S(1)}, f32[512,256]{1,0:T(8,128)S(1)}) custom-call(s32[512,128]{1,0:T(8,128)S(1)} %get-tuple-element.263.q_doc, s32[8,512]{1,0:T(8,128)} %broadcast_in_dim.42.k_doc, ...), custom_call_target="tpu_custom_call", output_to_operand_aliasing={{0}: (6, {}), {1}: (7, {}), {2}: (8, {})} | custom-call | flops 268435456 | bytes 3145728 | tf_op jit(solution)/shard_map/cond/branch_1_fun/pallas_call | solution.py:57
  164.3 5.8 %conditional.13 = ((f32[2,512,128]{2,1,0:T(8,128)S(1)}, f32[2,512,128]{2,1,0:T(8,128)S(1)}, f32[512,256]{1,0:T(8,128)S(1)})) conditional(s32[]{:T(128)} %convert_element_type.146, (f32[2,512,128]{2,1,0:T(8,128)S(1)}, f32[2,512,128]{2,1,0:T(8,128)S(1)}, f32[512,256]{1,0:T(8,128)S(1)}) %get-tuple-element.476, (s32[]{:T(128)}, s32[32]{0:T(128)S(1)}, ...), branch_computations={%region_25.26_spmd, %region_26.28_spmd} | conditional | flops 268485120 | bytes 3192984 | solution.py:117
  165.6 4.5 %branch_1_fun.14 = (f32[2,512,128]{2,1,0:T(8,128)S(1)}, f32[2,512,128]{2,1,0:T(8,128)S(1)}, f32[512,256]{1,0:T(8,128)S(1)}) custom-call(s32[512,128]{1,0:T(8,128)S(1)} %get-tuple-element.272.q_doc, s32[8,512]{1,0:T(8,128)} %broadcast_in_dim.56.k_doc, ...), custom_call_target="tpu_custom_call", output_to_operand_aliasing={{0}: (6, {}), {1}: (7, {}), {2}: (8, {})} | custom-call | flops 268435456 | bytes 3145728 | tf_op jit(solution)/shard_map/cond/branch_1_fun/pallas_call | solution.py:57
  170.1 6.0 %conditional.14 = ((f32[2,512,128]{2,1,0:T(8,128)S(1)}, f32[2,512,128]{2,1,0:T(8,128)S(1)}, f32[512,256]{1,0:T(8,128)S(1)})) conditional(s32[]{:T(128)} %convert_element_type.136, (f32[2,512,128]{2,1,0:T(8,128)S(1)}, f32[2,512,128]{2,1,0:T(8,128)S(1)}, f32[512,256]{1,0:T(8,128)S(1)}) %get-tuple-element.477, (s32[]{:T(128)}, s32[32]{0:T(128)S(1)}, ...), branch_computations={%region_28.29_spmd, %region_29.31_spmd} | conditional | flops 268485120 | bytes 3192984 | solution.py:117
  171.7 4.5 %branch_1_fun.15 = (f32[2,512,128]{2,1,0:T(8,128)S(1)}, f32[2,512,128]{2,1,0:T(8,128)S(1)}, f32[512,256]{1,0:T(8,128)S(1)}) custom-call(s32[512,128]{1,0:T(8,128)S(1)} %get-tuple-element.281.q_doc, s32[8,512]{1,0:T(8,128)} %broadcast_in_dim.58.k_doc, ...), custom_call_target="tpu_custom_call", output_to_operand_aliasing={{0}: (6, {}), {1}: (7, {}), {2}: (8, {})} | custom-call | flops 268435456 | bytes 3145728 | tf_op jit(solution)/shard_map/cond/branch_1_fun/pallas_call | solution.py:57
  176.1 5.8 %conditional.15 = ((f32[2,512,128]{2,1,0:T(8,128)S(1)}, f32[512,256]{1,0:T(8,128)S(1)})) conditional(s32[]{:T(128)} %convert_element_type.134, (f32[2,512,128]{2,1,0:T(8,128)S(1)}, f32[512,256]{1,0:T(8,128)S(1)}) %tuple.94, (s32[]{:T(128)}, s32[32]{0:T(128)S(1)}, s32[512,128]{1,0:T(8,128)S(1)}, s32[512,128]{1,0:T(8,128)S(1)}, ...), branch_computations={%region_31.32_spmd, %region_32.34_spmd} | conditional | flops 268485120 | bytes 3193000 | solution.py:117
  177.4 4.5 %branch_1_fun.16 = (f32[2,512,128]{2,1,0:T(8,128)S(1)}, f32[2,512,128]{2,1,0:T(8,128)S(1)}, f32[512,256]{1,0:T(8,128)S(1)}) custom-call(s32[512,128]{1,0:T(8,128)S(1)} %get-tuple-element.290.q_doc, s32[8,512]{1,0:T(8,128)} %broadcast_in_dim.60.k_doc, ...), custom_call_target="tpu_custom_call", output_to_operand_aliasing={{0}: (6, {}), {1}: (7, {}), {2}: (8, {})} | custom-call | flops 268435456 | bytes 3145728 | tf_op jit(solution)/shard_map/cond/branch_1_fun/pallas_call | solution.py:57
  184.5 1.7 slice.131
  186.5 1.8 fusion
  190.4 23.3 %all_to_all.10 = bf16[16,2,32,256]{3,2,1,0:T(8,128)(2,1)S(1)} all-to-all(bf16[16,2,32,256]{3,2,1,0:T(8,128)(2,1)S(1)} %copy.142), channel_id=1, replica_groups=mesh['ctx'=32,'head'=16] {'head'}, dimensions={0} | all-to-all | bytes 1048576 | tf_op jit(solution)/shard_map/all_to_all | solution.py:203
  (144 shorter events, 27.9 us)
Async XLA Ops:
  7.2 2.2 copy-start.1
  7.2 2.2 copy-start.2
  7.2 2.3 %copy-start.3 = (bf16[32,4096]{1,0:T(8,128)(2,1)S(1)}, bf16[32,4096]{1,0:T(8,128)(2,1)}, u32[]{:S(2)}) copy-start(bf16[32,4096]{1,0:T(8,128)(2,1)} %param.33) | copy-start | bytes 786436
  7.2 2.3 %copy-start.4 = (bf16[32,4096]{1,0:T(8,128)(2,1)S(1)}, bf16[32,4096]{1,0:T(8,128)(2,1)}, u32[]{:S(2)}) copy-start(bf16[32,4096]{1,0:T(8,128)(2,1)} %param.34) | copy-start | bytes 786436
  11.4 11.2 %copy-start.7 = (f32[2,512]{1,0:T(2,128)S(1)}, f32[2,512]{1,0:T(2,128)}, u32[]{:S(2)}) copy-start(f32[2,512]{1,0:T(2,128)} %param.35) | copy-start | bytes 12292
  11.4 49.6 %all-to-all-start = ((bf16[16,6,32,256]{3,2,1,0:T(8,128)(2,1)}), bf16[16,6,32,256]{3,2,1,0:T(8,128)(2,1)S(1)}, u32[]{:S(2)}, u32[]{:S(2)}) async-start(bf16[16,6,32,256]{3,2,1,0:T(8,128)(2,1)} %copy.128), calls=%async_computation | async-start | bytes 3145728 | tf_op jit(solution)/shard_map/all_to_all | solution.py:196
  22.6 160.8 %all-gather.3.cloned.1.call-start = ((), (), s32[]{:S(2)}) async-start(), calls=%async_computation.2 | async-start | bytes 2433024 | tf_op jit(solution)/shard_map/all_gather | solution.py:158
  61.2 1.7 copy-start.5
  62.0 8.7 %copy-start.8 = (s32[32]{0:T(128)S(1)}, s32[32]{0:T(128)}, u32[]{:S(2)}) copy-start(s32[32]{0:T(128)} %param.37) | copy-start | bytes 388
  63.0 29.4 %copy-start = (bf16[2,16,32,256]{3,2,1,0:T(8,128)(2,1)}, bf16[2,16,32,256]{3,2,1,0:T(8,128)(2,1)S(1)}, u32[]{:S(2)}) copy-start(bf16[2,16,32,256]{3,2,1,0:T(8,128)(2,1)S(1)} %copy.129) | copy-start | bytes 1572868
  63.0 16.5 %collective-permute-start.2 = (bf16[2,512,256]{2,1,0:T(8,128)(2,1)S(1)}, bf16[2,512,256]{2,1,0:T(8,128)(2,1)}, u32[]{:S(2)}, u32[]{:S(2)}) collective-permute-start(bf16[2,512,256]{2,1,0:T(8,128)(2,1)S(1)} %bitcast.121), channel_id=1, source_target_pairs={{0,16},{16,32},{32,48},{48,64},{64,80},{80,96},{96,112},{112,128},... | collective-permute-start | bytes 1572872 | tf_op jit(solution)/shard_map/ppermute | solution.py:15
  67.5 17.5 %collective-permute-start = (bf16[2,512,256]{2,1,0:T(8,128)(2,1)S(1)}, bf16[2,512,256]{2,1,0:T(8,128)(2,1)}, u32[]{:S(2)}, u32[]{:S(2)}) collective-permute-start(bf16[2,512,256]{2,1,0:T(8,128)(2,1)S(1)} %bitcast.122), channel_id=1, source_target_pairs={{0,128},{16,144},{32,160},{48,176},{64,192},{80,208},{96,224},{112... | collective-permute-start | bytes 1572872 | tf_op jit(solution)/shard_map/ppermute | solution.py:15
  79.6 23.1 %collective-permute-start.3 = (bf16[2,512,256]{2,1,0:T(8,128)(2,1)}, bf16[2,512,256]{2,1,0:T(8,128)(2,1)}, u32[]{:S(2)}, u32[]{:S(2)}) collective-permute-start(bf16[2,512,256]{2,1,0:T(8,128)(2,1)} %collective-permute-done.2), channel_id=1, source_target_pairs={{0,16},{16,32},{32,48},{48,64},{64,80},{80,96},{96,112},{112,128},... | collective-permute-start | bytes 1572872 | tf_op jit(solution)/shard_map/ppermute | solution.py:15
  85.0 28.1 %collective-permute-start.1 = (bf16[2,512,256]{2,1,0:T(8,128)(2,1)}, bf16[2,512,256]{2,1,0:T(8,128)(2,1)}, u32[]{:S(2)}, u32[]{:S(2)}) collective-permute-start(bf16[2,512,256]{2,1,0:T(8,128)(2,1)} %collective-permute-done), channel_id=1, source_target_pairs={{0,496},{16,0},{32,16},{48,32},{64,48},{80,64},{96,80},{112,96},{1... | collective-permute-start | bytes 1572872 | tf_op jit(solution)/shard_map/ppermute | solution.py:15
  102.7 20.8 %collective-permute-start.5 = (bf16[2,512,256]{2,1,0:T(8,128)(2,1)}, bf16[2,512,256]{2,1,0:T(8,128)(2,1)}, u32[]{:S(2)}, u32[]{:S(2)}) collective-permute-start(bf16[2,512,256]{2,1,0:T(8,128)(2,1)} %collective-permute-done.3), channel_id=1, source_target_pairs={{0,16},{16,32},{32,48},{48,64},{64,80},{80,96},{96,112},{112,128},... | collective-permute-start | bytes 1572872 | tf_op jit(solution)/shard_map/ppermute | solution.py:15
  113.1 25.5 %collective-permute-start.4 = (bf16[2,512,256]{2,1,0:T(8,128)(2,1)}, bf16[2,512,256]{2,1,0:T(8,128)(2,1)}, u32[]{:S(2)}, u32[]{:S(2)}) collective-permute-start(bf16[2,512,256]{2,1,0:T(8,128)(2,1)} %collective-permute-done.1), channel_id=1, source_target_pairs={{0,496},{16,0},{32,16},{48,32},{64,48},{80,64},{96,80},{112,96},{1... | collective-permute-start | bytes 1572872 | tf_op jit(solution)/shard_map/ppermute | solution.py:15
  123.5 40.8 %collective-permute-start.7 = (bf16[2,512,256]{2,1,0:T(8,128)(2,1)}, bf16[2,512,256]{2,1,0:T(8,128)(2,1)}, u32[]{:S(2)}, u32[]{:S(2)}) collective-permute-start(bf16[2,512,256]{2,1,0:T(8,128)(2,1)} %collective-permute-done.5), channel_id=1, source_target_pairs={{0,16},{16,32},{32,48},{48,64},{64,80},{80,96},{96,112},{112,128},... | collective-permute-start | bytes 1572872 | tf_op jit(solution)/shard_map/ppermute | solution.py:15
  138.5 31.6 %collective-permute-start.6 = (bf16[2,512,256]{2,1,0:T(8,128)(2,1)}, bf16[2,512,256]{2,1,0:T(8,128)(2,1)}, u32[]{:S(2)}, u32[]{:S(2)}) collective-permute-start(bf16[2,512,256]{2,1,0:T(8,128)(2,1)} %collective-permute-done.4), channel_id=1, source_target_pairs={{0,496},{16,0},{32,16},{48,32},{64,48},{80,64},{96,80},{112,96},{1... | collective-permute-start | bytes 1572872 | tf_op jit(solution)/shard_map/ppermute | solution.py:15
  186.5 2.2 %copy-start.6 = (bf16[512,2,128]{2,1,0:T(2,128)(2,1)S(1)}, bf16[512,2,128]{2,1,0:T(2,128)(2,1)}, u32[]{:S(2)}) copy-start(bf16[512,2,128]{2,1,0:T(2,128)(2,1)} %copy-done.5) | copy-start | bytes 786436
  188.8 1.1 copy-start.9
Sparse Core Ops, SparseCore 0:
  63.0 78.6 all-gather.2
